TPU v7x, 256 devices: a whole 4x4x8 slice. The times are simulated.
256 devices in a mesh: dom: 128 (over x, z, y), head: 2 (over core).
Axes of the slice: x: 4, y: 4, z: 8, core: 2. Of those that a mesh axis runs over, the one named last changes fastest.
Arguments:
- query_rows: bfloat16 [32768, 512], P('dom', 'head'), may hold values from -70 to 70
- key_rows: bfloat16 [32768, 512], P('dom', 'head'), may hold values from -4 to 4
- value_rows: bfloat16 [32768, 512], P('dom', 'head'), may hold values from -6 to 6
- out_weight: bfloat16 [512, 512], P('head'), may hold values from -0.25 to 0.25
- out_grad: bfloat16 [32768, 512], P('dom', 'head'), may hold values from -24 to 24
- far_bias: float32 [8], P('head'), may hold values from 4 to 7
- tile_list: int32 [256, 4], P('dom'), may hold values from 0 to 255, as said below
- tile_count: int32 [256], P('dom'), may hold values from 1 to 4, as said below
- send_rows: int32 [128, 128, 8], P('dom'), may hold values from 0 to 255
- expander_slot: int32 [32768, 3], P('dom'), may hold values from 0 to 1023, as said below
Outputs:
- layer_out: bfloat16 [32768, 512], P('dom', 'head')
- query_grad: bfloat16 [32768, 512], P('dom', 'head')
- key_grad: bfloat16 [32768, 512], P('dom', 'head')
- value_grad: bfloat16 [32768, 512], P('dom', 'head')
- out_weight_grad: float32 [512, 512], P('dom', 'head')
Inputs may be any that keep to these rules, and one draw needn't show every extreme that they name: `tile_list`: row t begins with t itself; its first tile_count[t] entries are distinct tiles from the 2 last tiles of the previous partition, the 2 tiles of t's own partition and the 2 first tiles of the next partition (partition = block of 2 tiles); later entries equal t. `tile_count`: every partition of 2 tiles has a tile with 4. `expander_slot`: A value names source partition value // 8 and slot value % 8 of send_rows[source, partition of the node].
All inputs are finite; a program needn't handle non-finite values.
Results may differ from a plain program's by a relative error of at most 0.011.
Values may be sent and summed in bfloat16 or wider, within the bound.
No kernel may reach another device: no remote copies, remote signals or barrier semaphores. Data moves between devices by JAX's collectives and lax.ppermute only.
A program may use at most 64 MiB of HBM per device.

v0:
```python
import math

import jax
import jax.numpy as jnp
from jax import lax
from jax.sharding import PartitionSpec as P

TILE = 128
HALO = 2
DEG = 3


def extended_2(value, sides, width):
    for axis, dim in sides:
        peers, length = (lax.axis_size(axis), value.shape[dim])
        up = [(i, (i + 1) % peers) for i in range(peers - 1)]
        down = [(j, i) for i, j in up]
        last = lax.slice_in_dim(value, length - width, length, axis=dim)
        leading = lax.slice_in_dim(value, 0, width, axis=dim)
        before = lax.ppermute(last, axis, up)
        after = lax.ppermute(leading, axis, down)
        value = jnp.concatenate([before, value, after], axis=dim)
    return value


def from_behind(value, axis, steps):
    count = lax.axis_size(axis)
    leading, last = (max(0, -steps), min(count, count - steps))
    return lax.ppermute(value, axis, [(source, source + steps) for source in range(leading, last)])


def rounded(values):
    return lax.optimization_barrier(values.astype(jnp.bfloat16)).astype(jnp.float32)


def tile_work(query_tile, grad_tile, tile_ids, live_count, far_tile, ext_tiles, bias, base_tile):
    col_width = query_tile.shape[1]
    heads_here = bias.shape[0]
    head_size = col_width // heads_here
    score_scale = head_size ** (-0.5)
    key_block = ext_tiles[tile_ids - base_tile].reshape(-1, 2 * col_width)
    near_keys = key_block[:, :col_width].reshape(-1, heads_here, head_size)
    near_values = key_block[:, col_width:].reshape(-1, heads_here, head_size)
    far_keys = far_tile[:, :, :col_width].reshape(TILE, -1, heads_here, head_size)
    far_values = far_tile[:, :, col_width:].reshape(TILE, -1, heads_here, head_size)
    queries = query_tile.reshape(TILE, heads_here, head_size)
    upstream = grad_tile.reshape(TILE, heads_here, head_size)
    live_keys = jnp.repeat(jnp.arange(tile_ids.shape[0]) < live_count, TILE)
    near_score = (
        jnp.einsum("qhd,khd->hqk", queries, near_keys, preferred_element_type=jnp.float32)
        * score_scale
    )
    far_score = (
        jnp.einsum("qhd,qehd->hqe", queries, far_keys, preferred_element_type=jnp.float32)
        * score_scale
        + bias[:, None, None]
    )
    row_max = jnp.maximum(
        jnp.max(jnp.where(live_keys, near_score, -jnp.inf), axis=2), jnp.max(far_score, axis=2)
    )
    near_exp = jnp.where(live_keys, jnp.exp(near_score - row_max[:, :, None]), 0.0)
    far_exp = jnp.exp(far_score - row_max[:, :, None])
    row_sum = jnp.sum(near_exp, axis=2) + jnp.sum(far_exp, axis=2)
    mixed = jnp.einsum(
        "hqk,khd->qhd",
        near_exp.astype(jnp.bfloat16),
        near_values,
        preferred_element_type=jnp.float32,
    )
    mixed = mixed + jnp.einsum(
        "hqe,qehd->qhd",
        far_exp.astype(jnp.bfloat16),
        far_values,
        preferred_element_type=jnp.float32,
    )
    attention = (mixed / row_sum.T[:, :, None]).astype(jnp.bfloat16)
    delta_term = jnp.sum(
        upstream.astype(jnp.float32) * rounded(mixed / row_sum.T[:, :, None]), axis=2
    ).T
    near_dprob = jnp.einsum(
        "qhd,khd->hqk", upstream, near_values, preferred_element_type=jnp.float32
    )
    far_dprob = jnp.einsum(
        "qhd,qehd->hqe", upstream, far_values, preferred_element_type=jnp.float32
    )
    near_prob = near_exp / row_sum[:, :, None]
    far_prob = far_exp / row_sum[:, :, None]
    near_dscore = (near_prob * (near_dprob - delta_term[:, :, None])).astype(jnp.bfloat16)
    far_dscore = (far_prob * (far_dprob - delta_term[:, :, None])).astype(jnp.bfloat16)
    query_grad = jnp.einsum(
        "hqk,khd->qhd", near_dscore, near_keys, preferred_element_type=jnp.float32
    )
    query_grad = (
        query_grad
        + jnp.einsum("hqe,qehd->qhd", far_dscore, far_keys, preferred_element_type=jnp.float32)
    ) * score_scale
    near_kgrad = (
        jnp.einsum("hqk,qhd->khd", near_dscore, queries, preferred_element_type=jnp.float32)
        * score_scale
    )
    near_vgrad = jnp.einsum(
        "hqk,qhd->khd", near_prob.astype(jnp.bfloat16), upstream, preferred_element_type=jnp.float32
    )
    far_kgrad = (
        jnp.einsum("hqe,qhd->qehd", far_dscore, queries, preferred_element_type=jnp.float32)
        * score_scale
    )
    far_vgrad = jnp.einsum(
        "hqe,qhd->qehd", far_prob.astype(jnp.bfloat16), upstream, preferred_element_type=jnp.float32
    )
    near_grad = jnp.concatenate(
        [near_kgrad.reshape(-1, col_width), near_vgrad.reshape(-1, col_width)], axis=1
    )
    far_grad = jnp.concatenate(
        [far_kgrad.reshape(TILE, -1, col_width), far_vgrad.reshape(TILE, -1, col_width)], axis=2
    )
    return (
        attention.reshape(TILE, col_width),
        query_grad.astype(jnp.bfloat16).reshape(TILE, col_width),
        near_grad,
        far_grad,
    )


def shards(
    query_rows,
    key_rows,
    value_rows,
    out_weight,
    out_grad,
    far_bias,
    tile_list,
    tile_count,
    send_rows,
    expander_slot,
):
    col_width = query_rows.shape[1]
    node_count = query_rows.shape[0]
    per_part = node_count // TILE
    dom_index = lax.axis_index("dom")
    full_grad = lax.all_gather(out_grad, "head", axis=1, tiled=True)
    attn_grad = lax.dot_general(
        full_grad, out_weight, (((1,), (1,)), ((), ())), preferred_element_type=jnp.float32
    ).astype(jnp.bfloat16)
    stacked = jnp.concatenate([key_rows, value_rows], axis=1)
    rim_rows = HALO * TILE
    extended = extended_2(stacked, (("dom", 0),), rim_rows)
    ext_tiles = extended.reshape(-1, TILE, 2 * col_width)
    outgoing = stacked[send_rows[0]]
    received = lax.all_to_all(outgoing, "dom", split_axis=0, concat_axis=0, tiled=True)
    far_all = received.reshape(-1, 2 * col_width)[expander_slot]
    group = math.gcd(4, per_part)
    rounds = per_part // group
    base_tile = dom_index * per_part - HALO
    tile_lanes = jnp.arange(TILE, dtype=jnp.int32)
    batched = jax.vmap(tile_work, in_axes=(0, 0, 0, 0, 0, None, None, None))

    def advance(accum, inputs):
        query_group, grad_group, list_group, count_group, far_group = inputs
        attn_group, qgrad_group, near_group, fgrad_group = batched(
            query_group,
            grad_group,
            list_group,
            count_group,
            far_group,
            ext_tiles,
            far_bias,
            base_tile,
        )
        targets = ((list_group - base_tile)[:, :, None] * TILE + tile_lanes).reshape(-1)
        accum = accum.at[targets].add(near_group.reshape(-1, 2 * col_width))
        return (accum, (attn_group, qgrad_group, fgrad_group))

    inputs = (
        query_rows.reshape(rounds, group, TILE, col_width),
        attn_grad.reshape(rounds, group, TILE, col_width),
        tile_list.reshape(rounds, group, -1),
        tile_count.reshape(rounds, group),
        far_all.reshape(rounds, group, TILE, DEG, 2 * col_width),
    )
    start_grad = jnp.zeros((extended.shape[0], 2 * col_width), jnp.float32)
    ext_grad, (attn_all, qgrad_all, far_grad) = lax.scan(advance, start_grad, inputs)
    attn_mine = attn_all.reshape(node_count, col_width)
    low_part = ext_grad[:rim_rows]
    high_part = ext_grad[rim_rows + node_count :]
    own_grad = ext_grad[rim_rows : rim_rows + node_count]
    from_next = from_behind(low_part.astype(jnp.bfloat16), "dom", -1).astype(low_part.dtype)
    from_prev = from_behind(high_part.astype(jnp.bfloat16), "dom", 1).astype(high_part.dtype)
    own_grad = own_grad.at[:rim_rows].add(from_prev).at[node_count - rim_rows :].add(from_next)
    slot_grad = jnp.zeros((received.shape[0] * received.shape[1], 2 * col_width), jnp.float32)
    slot_grad = slot_grad.at[expander_slot.reshape(-1)].add(far_grad.reshape(-1, 2 * col_width))
    returned = lax.all_to_all(
        slot_grad.reshape(received.shape[0], received.shape[1], -1),
        "dom",
        split_axis=0,
        concat_axis=0,
        tiled=True,
    )
    own_grad = own_grad.at[send_rows[0].reshape(-1)].add(returned.reshape(-1, 2 * col_width))
    key_grad = own_grad[:, :col_width].astype(jnp.bfloat16)
    value_grad = own_grad[:, col_width:].astype(jnp.bfloat16)
    partial_out = jnp.dot(attn_mine, out_weight, preferred_element_type=jnp.float32)
    layer_out = lax.psum_scatter(partial_out, "head", scatter_dimension=1, tiled=True).astype(
        jnp.bfloat16
    )
    out_weight_grad = lax.psum_scatter(
        lax.dot_general(
            full_grad, attn_mine, (((0,), (0,)), ((), ())), preferred_element_type=jnp.float32
        ),
        "dom",
        scatter_dimension=0,
        tiled=True,
    )
    return (
        layer_out,
        qgrad_all.reshape(node_count, col_width),
        key_grad,
        value_grad,
        out_weight_grad,
    )


def solution(mesh):
    in_specs = (
        P("dom", "head"),
        P("dom", "head"),
        P("dom", "head"),
        P("head", None),
        P("dom", "head"),
        P("head"),
        P("dom", None),
        P("dom"),
        P("dom", None, None),
        P("dom", None),
    )
    out_specs = (
        P("dom", "head"),
        P("dom", "head"),
        P("dom", "head"),
        P("dom", "head"),
        P("dom", "head"),
    )
    return jax.shard_map(shards, mesh=mesh, in_specs=in_specs, out_specs=out_specs, check_vma=False)
```

profile of v0, /device:TPU:6, one launch (start us, length us, event | category | flops | bytes accessed | tf_op | source)
XLA Modules:
  0.0 377.5 jit_solution(1858008611822901135)
XLA Ops:
  9.9 10.5 %collective-permute-start.1 = (bf16[256,512]{1,0:T(8,128)(2,1)S(1)}, bf16[256,512]{1,0:T(8,128)(2,1)S(1)}, u32[]{:S(2)}, u32[]{:S(2)}) collective-permute-start(bf16[256,512]{1,0:T(8,128)(2,1)S(1)} %constant_dynamic-update-slice_fusion), channel_id=1, source_target_pairs={{2,0},{4,2},{6,4},{8,6},{10,8},{12,10},{14,12},{16,14},{18,16},{20... | collective-permute-start | bytes 786440 | tf_op jit(solution)/shard_map/ppermute | solution.py:21
  20.4 1.9 collective-permute-start
  23.2 5.1 %gather_fusion.1 = bf16[1024,512]{1,0:T(8,128)(2,1)} fusion(bf16[256,512]{1,0:T(8,128)(2,1)S(1)} %constant_dynamic-update-slice_fusion, s32[1024]{0:T(1024)S(1)} %broadcast_clamp_fusion), kind=kCustom, calls=%fused_computation.1 | custom fusion | bytes 2101248 | tf_op jit(solution)/shard_map/gather | solution.py:149
  28.3 12.2 %all-to-all-start = ((bf16[128,8,512]{2,1,0:T(8,128)(2,1)}), bf16[128,8,512]{2,1,0:T(8,128)(2,1)S(1)}, u32[]{:S(2)}, u32[]{:S(2)}) async-start(bf16[128,8,512]{2,1,0:T(8,128)(2,1)} %bitcast.13), calls=%async_computation | async-start | bytes 2097152 | tf_op jit(solution)/shard_map/all_to_all | solution.py:150
  41.2 2.0 all_gather.3
  52.8 2.6 select_reduce_fusion
  55.4 12.8 %all-to-all-done = bf16[128,8,512]{2,1,0:T(8,128)(2,1)S(1)} async-done(((bf16[128,8,512]{2,1,0:T(8,128)(2,1)}), bf16[128,8,512]{2,1,0:T(8,128)(2,1)S(1)}, u32[]{:S(2)}, u32[]{:S(2)}) %all-to-all-start) | async-done | bytes 1048608 | tf_op jit(solution)/shard_map/all_to_all | solution.py:150
  68.2 2.7 gather_fusion.2
  78.9 2.7 fusion.38
  96.6 2.6 convert_bitcast_fusion.1
  99.2 1.9 multiply_bitcast_fusion
  101.1 3.0 concatenate.36
  104.0 2.8 multiply_bitcast_fusion.1
  106.8 3.0 concatenate.35
  109.8 8.8 %scatter_custom_fusion.1 = f32[1024,512]{1,0:T(8,128)} fusion(s32[768]{0:T(1024)} %fusion.33, f32[768,256]{1,0:T(8,128)} %concatenate.36, f32[]{:T(128)} %constant.132.clone.1, f32[768,256]{1,0:T(8,128)} %concatenate.35, f32[]{:T(128)} %constant.135.clone.1), kind=kCustom, calls=%fused_computation.15 | custom fusion | flops 786432 | bytes 3671040 | tf_op jit(solution)/shard_map/scatter-add | solution.py:191
  118.7 9.7 %all-to-all-start.1 = ((f32[128,8,512]{2,1,0:T(8,128)}), f32[128,8,512]{2,1,0:T(8,128)}, u32[]{:S(2)}, u32[]{:S(2)}) async-start(f32[128,8,512]{2,1,0:T(8,128)} %bitcast.39), calls=%async_computation.2 | async-start | bytes 4194304 | tf_op jit(solution)/shard_map/all_to_all | solution.py:192
  135.6 2.0 multiply_convert_fusion
  146.0 7.6 %scatter_custom_fusion = f32[768,512]{1,0:T(8,128)S(1)} fusion(s32[1024]{0:T(1024)} %bitcast.149, f32[1024,512]{1,0:T(8,128)} %copy.119, f32[]{:T(128)} %constant.135.clone.1), kind=kCustom, calls=%fused_computation.45 | custom fusion | flops 524288 | bytes 1573376 | tf_op jit(solution)/shard_map/while/body/eval_jaxpr/scatter-add | solution.py:171
  154.6 7.0 %collective-permute-start.3 = (bf16[256,512]{1,0:T(8,128)(2,1)}, bf16[256,512]{1,0:T(8,128)(2,1)}, u32[]{:S(2)}, u32[]{:S(2)}) collective-permute-start(bf16[256,512]{1,0:T(8,128)(2,1)} %get-tuple-element.115), channel_id=1, source_target_pairs={{2,0},{4,2},{6,4},{8,6},{10,8},{12,10},{14,12},{16,14},{18,16},{20... | collective-permute-start | bytes 786440 | tf_op jit(solution)/shard_map/ppermute | solution.py:29
  161.6 1.9 collective-permute-start.2
  165.0 14.0 %collective-permute-done.3 = bf16[256,512]{1,0:T(8,128)(2,1)} collective-permute-done((bf16[256,512]{1,0:T(8,128)(2,1)}, bf16[256,512]{1,0:T(8,128)(2,1)}, u32[]{:S(2)}, u32[]{:S(2)}) %collective-permute-start.3) | collective-permute-done | bytes 262176 | tf_op jit(solution)/shard_map/ppermute | solution.py:29
  179.1 5.5 %collective-permute-done.2 = bf16[256,512]{1,0:T(8,128)(2,1)} collective-permute-done((bf16[256,512]{1,0:T(8,128)(2,1)}, bf16[256,512]{1,0:T(8,128)(2,1)}, u32[]{:S(2)}, u32[]{:S(2)}) %collective-permute-start.2) | collective-permute-done | bytes 262176 | tf_op jit(solution)/shard_map/ppermute | solution.py:29
  185.7 172.4 %all-reduce.3.cloned.1.call-done = f32[512,256]{0,1:T(8,128)} async-done(((f32[512,256]{0,1:T(8,128)}), f32[512,256]{0,1:T(8,128)}) %all-reduce.3.cloned.1.call-update) | async-done | bytes 524304
  361.4 7.9 %scatter_custom_fusion.2 = f32[256,512]{1,0:T(8,128)S(1)} fusion(f32[256,512]{1,0:T(8,128)S(1)} %fusion.21, s32[1024]{0:T(1024)} %bitcast.148, f32[128,8,512]{2,1,0:T(8,128)} %all-to-all-done.1), kind=kCustom, calls=%fused_computation.7 | custom fusion | flops 524288 | bytes 2621440 | tf_op jit(solution)/shard_map/scatter-add | solution.py:199
  (154 shorter events, 58.2 us)
Async XLA Ops:
  8.0 35.2 %copy-start = (bf16[256,512]{1,0:T(8,128)(2,1)S(1)}, bf16[256,512]{1,0:T(8,128)(2,1)}, u32[]{:S(2)}) copy-start(bf16[256,512]{1,0:T(8,128)(2,1)} %param.21) | copy-start | bytes 786436
  9.9 39.1 %collective-permute-start.1 = (bf16[256,512]{1,0:T(8,128)(2,1)S(1)}, bf16[256,512]{1,0:T(8,128)(2,1)S(1)}, u32[]{:S(2)}, u32[]{:S(2)}) collective-permute-start(bf16[256,512]{1,0:T(8,128)(2,1)S(1)} %constant_dynamic-update-slice_fusion), channel_id=1, source_target_pairs={{2,0},{4,2},{6,4},{8,6},{10,8},{12,10},{14,12},{16,14},{18,16},{20... | collective-permute-start | bytes 786440 | tf_op jit(solution)/shard_map/ppermute | solution.py:21
  20.4 28.6 %collective-permute-start = (bf16[256,512]{1,0:T(8,128)(2,1)S(1)}, bf16[256,512]{1,0:T(8,128)(2,1)S(1)}, u32[]{:S(2)}, u32[]{:S(2)}) collective-permute-start(bf16[256,512]{1,0:T(8,128)(2,1)S(1)} %constant_dynamic-update-slice_fusion), channel_id=1, source_target_pairs={{0,2},{2,4},{4,6},{6,8},{8,10},{10,12},{12,14},{14,16},{16,18},{18... | collective-permute-start | bytes 786440 | tf_op jit(solution)/shard_map/ppermute | solution.py:20
  28.3 12.2 %copy-start.21 = (s32[256,3]{0,1:T(4,128)S(1)}, s32[256,3]{0,1:T(4,128)}, u32[]{:S(2)}) copy-start(s32[256,3]{0,1:T(4,128)} %param.27) | copy-start | bytes 9220
  28.3 12.6 %copy-start.27 = (s32[2]{0:T(128)S(1)}, s32[2]{0:T(128)}, u32[]{:S(2)}) copy-start(s32[2]{0:T(128)} %param.25) | copy-start | bytes 28
  28.3 12.7 %copy-start.17 = (bf16[256,256]{1,0:T(8,128)(2,1)S(1)}, bf16[256,256]{1,0:T(8,128)(2,1)}, u32[]{:S(2)}) copy-start(bf16[256,256]{1,0:T(8,128)(2,1)} %param.18) | copy-start | bytes 393220
  28.3 12.8 %copy-start.16 = (bf16[256,256]{1,0:T(8,128)(2,1)S(1)}, bf16[256,256]{1,0:T(8,128)(2,1)}, u32[]{:S(2)}) copy-start(bf16[256,256]{1,0:T(8,128)(2,1)} %param.22) | copy-start | bytes 393220
  28.3 15.3 %copy-start.26 = (s32[2,4]{1,0:T(2,128)S(1)}, s32[2,4]{1,0:T(2,128)}, u32[]{:S(2)}) copy-start(s32[2,4]{1,0:T(2,128)} %param.24) | copy-start | bytes 100
  28.3 39.9 %all-to-all-start = ((bf16[128,8,512]{2,1,0:T(8,128)(2,1)}), bf16[128,8,512]{2,1,0:T(8,128)(2,1)S(1)}, u32[]{:S(2)}, u32[]{:S(2)}) async-start(bf16[128,8,512]{2,1,0:T(8,128)(2,1)} %bitcast.13), calls=%async_computation | async-start | bytes 2097152 | tf_op jit(solution)/shard_map/all_to_all | solution.py:150
  73.9 8.8 %copy-start.1 = (f32[2,4,512,128]{3,2,1,0:T(8,128)S(1)}, f32[2,4,512,128]{3,2,1,0:T(8,128)}, u32[]{:S(2)}) copy-start(f32[2,4,512,128]{3,2,1,0:T(8,128)} %get-tuple-element.123) | copy-start | bytes 6291460
  118.7 9.8 %copy-start.22 = (s32[1,128,8]{1,2,0:T(8,128)S(1)}, s32[1,128,8]{1,2,0:T(8,128)}, u32[]{:S(2)}) copy-start(s32[1,128,8]{1,2,0:T(8,128)} %param.26) | copy-start | bytes 12292
  118.7 10.1 %copy-start.28 = (u32[256]{0:T(256)S(1)}, u32[256]{0:T(256)}, u32[]{:S(2)}) copy-start(u32[256]{0:T(256)} %constant.147) | copy-start | bytes 3076
  118.7 11.3 %copy-start.25 = (s32[2,4]{1,0:T(2,128)S(1)}, s32[2,4]{1,0:T(2,128)}, u32[]{:S(2)}) copy-start(s32[2,4]{1,0:T(2,128)} %get-tuple-element.120) | copy-start | bytes 100
  118.7 12.6 %copy-start.15 = (bf16[2,128,4,64]{1,3,2,0:T(8,128)(2,1)S(1)}, bf16[2,128,4,64]{1,3,2,0:T(8,128)(2,1)}, u32[]{:S(2)}) copy-start(bf16[2,128,4,64]{1,3,2,0:T(8,128)(2,1)} %copy-done.14) | copy-start | bytes 393220
  118.7 12.7 %copy-start.12 = (bf16[2,128,4,64]{1,0,3,2:T(2,128)(2,1)S(1)}, bf16[2,128,4,64]{1,0,3,2:T(2,128)(2,1)}, u32[]{:S(2)}) copy-start(bf16[2,128,4,64]{1,0,3,2:T(2,128)(2,1)} %copy-done.10) | copy-start | bytes 393220
  118.7 12.7 %copy-start.19 = (pred[1,2,4,128]{3,1,2,0:T(4,128)(4,1)S(1)}, pred[1,2,4,128]{3,1,2,0:T(4,128)(4,1)}, u32[]{:S(2)}) copy-start(pred[1,2,4,128]{3,1,2,0:T(4,128)(4,1)} %copy-done.18) | copy-start | bytes 3076
  118.7 12.7 %copy-start.20 = (f32[2,4,128]{2,1,0:T(4,128)S(1)}, f32[2,4,128]{2,1,0:T(4,128)}, u32[]{:S(2)}) copy-start(f32[2,4,128]{2,1,0:T(4,128)} %add.164) | copy-start | bytes 12292
  118.7 242.7 %all-to-all-start.1 = ((f32[128,8,512]{2,1,0:T(8,128)}), f32[128,8,512]{2,1,0:T(8,128)}, u32[]{:S(2)}, u32[]{:S(2)}) async-start(f32[128,8,512]{2,1,0:T(8,128)} %bitcast.39), calls=%async_computation.2 | async-start | bytes 4194304 | tf_op jit(solution)/shard_map/all_to_all | solution.py:192
  128.5 229.7 %all-reduce.3.cloned.1.call-start = ((), (), s32[]{:S(2)}) async-start(), calls=%async_computation.4 | async-start | bytes 1048576
  135.5 224.2 %reduce-scatter.3.cloned.1.call-start = ((), (), s32[]{:S(2)}) async-start(), calls=%async_computation.3 | async-start | bytes 786432 | tf_op jit(solution)/shard_map/reduce_scatter | solution.py:203
  153.6 9.9 %copy-start.5 = (bf16[2,128,3,256]{1,3,2,0:T(8,128)(2,1)S(1)}, bf16[2,128,3,256]{1,3,2,0:T(8,128)(2,1)}, u32[]{:S(2)}) copy-start(bf16[2,128,3,256]{1,3,2,0:T(8,128)(2,1)} %copy-done.4) | copy-start | bytes 1179652
  153.6 10.0 %copy-start.3 = (bf16[2,4,128,512]{2,3,1,0:T(8,128)(2,1)S(1)}, bf16[2,4,128,512]{2,3,1,0:T(8,128)(2,1)}, u32[]{:S(2)}) copy-start(bf16[2,4,128,512]{2,3,1,0:T(8,128)(2,1)} %copy-done.2) | copy-start | bytes 3145732
  154.6 24.4 %collective-permute-start.3 = (bf16[256,512]{1,0:T(8,128)(2,1)}, bf16[256,512]{1,0:T(8,128)(2,1)}, u32[]{:S(2)}, u32[]{:S(2)}) collective-permute-start(bf16[256,512]{1,0:T(8,128)(2,1)} %get-tuple-element.115), channel_id=1, source_target_pairs={{2,0},{4,2},{6,4},{8,6},{10,8},{12,10},{14,12},{16,14},{18,16},{20... | collective-permute-start | bytes 786440 | tf_op jit(solution)/shard_map/ppermute | solution.py:29
  161.6 22.9 %collective-permute-start.2 = (bf16[256,512]{1,0:T(8,128)(2,1)}, bf16[256,512]{1,0:T(8,128)(2,1)}, u32[]{:S(2)}, u32[]{:S(2)}) collective-permute-start(bf16[256,512]{1,0:T(8,128)(2,1)} %get-tuple-element.114), channel_id=1, source_target_pairs={{0,2},{2,4},{4,6},{6,8},{8,10},{10,12},{12,14},{14,16},{16,18},{18... | collective-permute-start | bytes 786440 | tf_op jit(solution)/shard_map/ppermute | solution.py:29
  (13 other events, 36.9 us)
Sparse Core Ops, SparseCore 0:
  135.7 222.3 all-reduce.2
Sparse Core Ops, SparseCore 1:
  142.3 13.9 reduce-scatter.2
where the time goes:
time: 379 us; the launch traced here: 377 us
  waiting for transfers between devices  205 us (54%)
  other arithmetic  51.3 us (14%)
  local copies, waits for them, and re-layouts  48.8 us (13%)
  starting transfers between devices  43.3 us (11%)
  between operations  16.8 us (4%)
  matrix products  10.5 us (3%)
    unnamed x3, waiting for transfers between devices  172 us
    ppermute x2, waiting for transfers between devices, from_behind(): lax.ppermute(value, axis, [(source, source + steps) for source in range(l...  19.5 us
    unnamed x77, local copies, waits for them, and re-layouts  13.7 us
    all_to_all x1, waiting for transfers between devices, shards(): lax.all_to_all(outgoing, 'dom', split_axis=0, concat_axis=0, tiled=True)  12.8 us
    all_to_all x1, starting transfers between devices, shards(): lax.all_to_all(outgoing, 'dom', split_axis=0, concat_axis=0, tiled=True)  12.2 us
    ppermute x1, starting transfers between devices, extended_2(): after = lax.ppermute(leading, axis, down)  10.5 us
    all_to_all x1, starting transfers between devices, shards(): lax.all_to_all(slot_grad.reshape(received.shape[0], received.shape[1], -1...  9.75 us
    ppermute x2, starting transfers between devices, from_behind(): lax.ppermute(value, axis, [(source, source + steps) for source in range(l...  8.89 us
  transfers between devices with their start and end apart: 8, of which 4 were waited for; matrix products, arithmetic and copies ran while one was open for 13% of the time, Pallas kernels for 0%

commit v1 on v0

--- a/solution.py
+++ b/solution.py
@@ -189,13 +189,17 @@
     own_grad = own_grad.at[:rim_rows].add(from_prev).at[node_count - rim_rows :].add(from_next)
     slot_grad = jnp.zeros((received.shape[0] * received.shape[1], 2 * col_width), jnp.float32)
     slot_grad = slot_grad.at[expander_slot.reshape(-1)].add(far_grad.reshape(-1, 2 * col_width))
-    returned = lax.all_to_all(
-        slot_grad.reshape(received.shape[0], received.shape[1], -1),
-        "dom",
-        split_axis=0,
-        concat_axis=0,
-        tiled=True,
-    )
+    n_dom = received.shape[0]
+    weight_part = lax.dot_general(
+        full_grad, attn_mine, (((0,), (0,)), ((), ())), preferred_element_type=jnp.float32
+    ).reshape(n_dom, -1, 2 * col_width)
+    weight_rows = weight_part.shape[1]
+    both = jnp.concatenate(
+        [slot_grad.reshape(n_dom, received.shape[1], -1), weight_part], axis=1
+    )
+    both_back = lax.all_to_all(both, "dom", split_axis=0, concat_axis=0, tiled=True)
+    returned = both_back[:, : received.shape[1]]
+    weight_sum = jnp.sum(both_back[:, received.shape[1] :], axis=0)
     own_grad = own_grad.at[send_rows[0].reshape(-1)].add(returned.reshape(-1, 2 * col_width))
     key_grad = own_grad[:, :col_width].astype(jnp.bfloat16)
     value_grad = own_grad[:, col_width:].astype(jnp.bfloat16)
@@ -203,14 +207,7 @@
     layer_out = lax.psum_scatter(partial_out, "head", scatter_dimension=1, tiled=True).astype(
         jnp.bfloat16
     )
-    out_weight_grad = lax.psum_scatter(
-        lax.dot_general(
-            full_grad, attn_mine, (((0,), (0,)), ((), ())), preferred_element_type=jnp.float32
-        ),
-        "dom",
-        scatter_dimension=0,
-        tiled=True,
-    )
+    out_weight_grad = weight_sum.reshape(-1, col_width)
     return (
         layer_out,
         qgrad_all.reshape(node_count, col_width),

time: 379 us -> 255 us (0.67)
  waiting for transfers between devices: 205 us -> 80.3 us
    unnamed x3 -> x1, waiting for transfers between devices: 172 us -> 0.02 us
    ppermute x2, waiting for transfers between devices: 19.5 us -> 66.5 us  [from_behind(): lax.ppermute(value, axis, [(source, source + steps) for source in range(l...]
    concatenate x0 -> x1, other arithmetic: none -> 4.31 us  [shards(): jnp.concatenate([slot_grad.reshape(n_dom, received.shape[1], -1), weight_...]
    unnamed x77 -> x72, local copies, waits for them, and re-layouts: 13.7 us -> 10.4 us
  transfers between devices with their start and end apart: 8 -> 7, of which waited for: 4 -> 2; matrix products, arithmetic and copies ran while one was open for 13% -> 17% of each run, Pallas kernels for 0% -> 0%
where the time goes in v1:
time: 255 us; the launch traced here: 253 us
  waiting for transfers between devices  80.3 us (31%)
  other arithmetic  52.8 us (21%)
  local copies, waits for them, and re-layouts  49.5 us (19%)
  starting transfers between devices  44.2 us (17%)
  between operations  14.6 us (6%)
  matrix products  9.86 us (4%)
    ppermute x2, waiting for transfers between devices, from_behind(): lax.ppermute(value, axis, [(source, source + steps) for source in range(l...  66.5 us
    all_to_all x1, waiting for transfers between devices, shards(): lax.all_to_all(outgoing, 'dom', split_axis=0, concat_axis=0, tiled=True)  13.7 us
    all_to_all x1, starting transfers between devices, shards(): lax.all_to_all(outgoing, 'dom', split_axis=0, concat_axis=0, tiled=True)  12.2 us
    ppermute x1, starting transfers between devices, extended_2(): after = lax.ppermute(leading, axis, down)  10.5 us
    unnamed x72, local copies, waits for them, and re-layouts  10.4 us
    ppermute x2, starting transfers between devices, from_behind(): lax.ppermute(value, axis, [(source, source + steps) for source in range(l...  10.1 us
    all_to_all x1, starting transfers between devices, shards(): lax.all_to_all(both, 'dom', split_axis=0, concat_axis=0, tiled=True)  9.54 us
    scatter-add x1, other arithmetic, shards(): slot_grad.at[expander_slot.reshape(-1)]  8.89 us
  transfers between devices with their start and end apart: 7, of which 2 were waited for; matrix products, arithmetic and copies ran while one was open for 17% of the time, Pallas kernels for 0%

profile of v1, /device:TPU:6, one launch (start us, length us, event | category | flops | bytes accessed | tf_op | source)
XLA Modules:
  0.0 253.5 jit_solution(18319431363123263878)
XLA Ops:
  9.1 10.5 %collective-permute-start.1 = (bf16[256,512]{1,0:T(8,128)(2,1)S(1)}, bf16[256,512]{1,0:T(8,128)(2,1)S(1)}, u32[]{:S(2)}, u32[]{:S(2)}) collective-permute-start(bf16[256,512]{1,0:T(8,128)(2,1)S(1)} %constant_dynamic-update-slice_fusion), channel_id=1, source_target_pairs={{2,0},{4,2},{6,4},{8,6},{10,8},{12,10},{14,12},{16,14},{18,16},{20... | collective-permute-start | bytes 786440 | tf_op jit(solution)/shard_map/ppermute | solution.py:21
  19.5 1.9 collective-permute-start
  22.4 5.1 %gather_fusion.1 = bf16[1024,512]{1,0:T(8,128)(2,1)} fusion(bf16[256,512]{1,0:T(8,128)(2,1)S(1)} %constant_dynamic-update-slice_fusion, s32[1024]{0:T(1024)S(1)} %broadcast_clamp_fusion), kind=kCustom, calls=%fused_computation.1 | custom fusion | bytes 2101248 | tf_op jit(solution)/shard_map/gather | solution.py:149
  27.5 12.2 %all-to-all-start = ((bf16[128,8,512]{2,1,0:T(8,128)(2,1)}), bf16[128,8,512]{2,1,0:T(8,128)(2,1)S(1)}, u32[]{:S(2)}, u32[]{:S(2)}) async-start(bf16[128,8,512]{2,1,0:T(8,128)(2,1)} %bitcast.13), calls=%async_computation | async-start | bytes 2097152 | tf_op jit(solution)/shard_map/all_to_all | solution.py:150
  40.6 2.2 all_gather.3
  53.7 13.7 %all-to-all-done = bf16[128,8,512]{2,1,0:T(8,128)(2,1)S(1)} async-done(((bf16[128,8,512]{2,1,0:T(8,128)(2,1)}), bf16[128,8,512]{2,1,0:T(8,128)(2,1)S(1)}, u32[]{:S(2)}, u32[]{:S(2)}) %all-to-all-start) | async-done | bytes 1048608 | tf_op jit(solution)/shard_map/all_to_all | solution.py:150
  67.4 3.3 %gather_fusion.2 = bf16[768,512]{1,0:T(8,128)(2,1)} fusion(bf16[1024,512]{1,0:T(8,128)(2,1)S(1)} %bitcast.121, s32[1024]{0:T(1024)S(1)} %pad_clamp_fusion), kind=kCustom, calls=%fused_computation.2 | custom fusion | bytes 1575936 | tf_op jit(solution)/shard_map/gather | solution.py:151
  70.7 2.4 squeeze.20
  80.3 2.4 fusion.37
  97.0 2.2 reshape.314
  99.2 2.5 convert_bitcast_fusion.1
  103.6 2.2 concatenate.38
  105.9 2.9 %multiply_bitcast_fusion = f32[2,128,3,4,64]{4,3,2,1,0:T(4,128)} fusion(f32[2,128,4,3]{2,3,1,0:T(4,128)} %get-tuple-element.108, f32[2,128,4,64]{3,2,1,0:T(4,128)} %copy.122), kind=kLoop, calls=%fused_computation.20 | loop fusion | flops 196608 | bytes 1060864 | tf_op jit(solution)/shard_map/while/body/eval_jaxpr/vmap(hqe,qhd->qehd)/transpose | solution.py:108
  108.8 3.0 %concatenate.39 = f32[768,256]{1,0:T(8,128)} reshape(f32[2,128,3,4,64]{4,3,2,1,0:T(4,128)} %multiply_bitcast_fusion) | data formatting | bytes 1572864 | tf_op jit(solution)/shard_map/while/body/eval_jaxpr/vmap()/concatenate | solution.py:114
  111.7 8.9 %scatter_custom_fusion.1 = f32[1024,512]{1,0:T(8,128)} fusion(s32[768]{0:T(1024)} %fusion.32, f32[768,256]{1,0:T(8,128)} %concatenate.39, f32[]{:T(128)} %constant.133.clone.1, f32[768,256]{1,0:T(8,128)S(1)} %concatenate.38, f32[]{:T(128)} %constant.136.clone.1), kind=kCustom, calls=%fused_computation.16 | custom fusion | flops 786432 | bytes 3671040 | tf_op jit(solution)/shard_map/scatter-add | solution.py:191
  120.6 4.3 %pad_maximum_fusion = f32[128,10,512]{2,1,0:T(8,128)} fusion(f32[128,2,512]{2,1,0:T(2,128)} %reshape.314, f32[128,8,512]{2,1,0:T(8,128)} %bitcast.122), kind=kLoop, calls=%fused_computation.6 | loop fusion | flops 655360 | bytes 5242880 | tf_op jit(solution)/shard_map/concatenate | solution.py:197
  125.0 9.5 %all-to-all-start.1 = ((f32[128,10,512]{2,1,0:T(8,128)}), f32[128,10,512]{2,1,0:T(8,128)}, u32[]{:S(2)}, u32[]{:S(2)}) async-start(f32[128,10,512]{2,1,0:T(8,128)} %pad_maximum_fusion), calls=%async_computation.2 | async-start | bytes 8388608 | tf_op jit(solution)/shard_map/all_to_all | solution.py:200
  140.5 2.1 multiply_convert_fusion
  144.5 1.9 copy.118
  146.4 7.6 %scatter_custom_fusion = f32[768,512]{1,0:T(8,128)S(1)} fusion(s32[1024]{0:T(1024)} %bitcast.147, f32[1024,512]{1,0:T(8,128)} %copy.118, f32[]{:T(128)} %constant.136.clone.1), kind=kCustom, calls=%fused_computation.46 | custom fusion | flops 524288 | bytes 1573376 | tf_op jit(solution)/shard_map/while/body/eval_jaxpr/scatter-add | solution.py:171
  155.0 3.4 %collective-permute-start.2 = (bf16[256,512]{1,0:T(8,128)(2,1)}, bf16[256,512]{1,0:T(8,128)(2,1)}, u32[]{:S(2)}, u32[]{:S(2)}) collective-permute-start(bf16[256,512]{1,0:T(8,128)(2,1)} %get-tuple-element.109), channel_id=1, source_target_pairs={{0,2},{2,4},{4,6},{6,8},{8,10},{10,12},{12,14},{14,16},{16,18},{18... | collective-permute-start | bytes 786440 | tf_op jit(solution)/shard_map/ppermute | solution.py:29
  158.4 6.7 %collective-permute-start.3 = (bf16[256,512]{1,0:T(8,128)(2,1)}, bf16[256,512]{1,0:T(8,128)(2,1)}, u32[]{:S(2)}, u32[]{:S(2)}) collective-permute-start(bf16[256,512]{1,0:T(8,128)(2,1)} %get-tuple-element.110), channel_id=1, source_target_pairs={{2,0},{4,2},{6,4},{8,6},{10,8},{12,10},{14,12},{16,14},{18,16},{20... | collective-permute-start | bytes 786440 | tf_op jit(solution)/shard_map/ppermute | solution.py:29
  166.6 66.5 %collective-permute-done.2 = bf16[256,512]{1,0:T(8,128)(2,1)} collective-permute-done((bf16[256,512]{1,0:T(8,128)(2,1)}, bf16[256,512]{1,0:T(8,128)(2,1)}, u32[]{:S(2)}, u32[]{:S(2)}) %collective-permute-start.2) | collective-permute-done | bytes 262176 | tf_op jit(solution)/shard_map/ppermute | solution.py:29
  235.9 7.6 %scatter_custom_fusion.2 = f32[256,512]{1,0:T(8,128)S(1)} fusion(f32[256,512]{1,0:T(8,128)S(1)} %fusion.20, s32[1024]{0:T(1024)} %bitcast.146, f32[128,10,512]{2,1,0:T(8,128)} %all-to-all-done.1), kind=kCustom, calls=%fused_computation.8 | custom fusion | flops 524288 | bytes 2621440 | tf_op jit(solution)/shard_map/scatter-add | solution.py:203
  (151 shorter events, 53.8 us)
Async XLA Ops:
  7.2 35.6 %copy-start = (bf16[256,512]{1,0:T(8,128)(2,1)S(1)}, bf16[256,512]{1,0:T(8,128)(2,1)}, u32[]{:S(2)}) copy-start(bf16[256,512]{1,0:T(8,128)(2,1)} %param.21) | copy-start | bytes 786436
  9.1 39.1 %collective-permute-start.1 = (bf16[256,512]{1,0:T(8,128)(2,1)S(1)}, bf16[256,512]{1,0:T(8,128)(2,1)S(1)}, u32[]{:S(2)}, u32[]{:S(2)}) collective-permute-start(bf16[256,512]{1,0:T(8,128)(2,1)S(1)} %constant_dynamic-update-slice_fusion), channel_id=1, source_target_pairs={{2,0},{4,2},{6,4},{8,6},{10,8},{12,10},{14,12},{16,14},{18,16},{20... | collective-permute-start | bytes 786440 | tf_op jit(solution)/shard_map/ppermute | solution.py:21
  19.5 28.6 %collective-permute-start = (bf16[256,512]{1,0:T(8,128)(2,1)S(1)}, bf16[256,512]{1,0:T(8,128)(2,1)}, u32[]{:S(2)}, u32[]{:S(2)}) collective-permute-start(bf16[256,512]{1,0:T(8,128)(2,1)S(1)} %constant_dynamic-update-slice_fusion), channel_id=1, source_target_pairs={{0,2},{2,4},{4,6},{6,8},{8,10},{10,12},{12,14},{14,16},{16,18},{18... | collective-permute-start | bytes 786440 | tf_op jit(solution)/shard_map/ppermute | solution.py:20
  27.5 12.2 %copy-start.27 = (s32[2]{0:T(128)S(1)}, s32[2]{0:T(128)}, u32[]{:S(2)}) copy-start(s32[2]{0:T(128)} %param.25) | copy-start | bytes 28
  27.5 12.3 %copy-start.26 = (s32[2,4]{1,0:T(2,128)S(1)}, s32[2,4]{1,0:T(2,128)}, u32[]{:S(2)}) copy-start(s32[2,4]{1,0:T(2,128)} %param.24) | copy-start | bytes 100
  27.5 12.9 %copy-start.15 = (bf16[256,256]{1,0:T(8,128)(2,1)S(1)}, bf16[256,256]{1,0:T(8,128)(2,1)}, u32[]{:S(2)}) copy-start(bf16[256,256]{1,0:T(8,128)(2,1)} %param.18) | copy-start | bytes 393220
  27.5 13.1 %copy-start.14 = (bf16[256,256]{1,0:T(8,128)(2,1)S(1)}, bf16[256,256]{1,0:T(8,128)(2,1)}, u32[]{:S(2)}) copy-start(bf16[256,256]{1,0:T(8,128)(2,1)} %param.22) | copy-start | bytes 393220
  27.5 15.8 %copy-start.21 = (s32[256,3]{0,1:T(4,128)S(1)}, s32[256,3]{0,1:T(4,128)}, u32[]{:S(2)}) copy-start(s32[256,3]{0,1:T(4,128)} %param.27) | copy-start | bytes 9220
  27.5 39.9 %all-to-all-start = ((bf16[128,8,512]{2,1,0:T(8,128)(2,1)}), bf16[128,8,512]{2,1,0:T(8,128)(2,1)S(1)}, u32[]{:S(2)}, u32[]{:S(2)}) async-start(bf16[128,8,512]{2,1,0:T(8,128)(2,1)} %bitcast.13), calls=%async_computation | async-start | bytes 2097152 | tf_op jit(solution)/shard_map/all_to_all | solution.py:150
  44.6 34.6 %copy-start.16 = (pred[1,2,4,128]{3,1,2,0:T(4,128)(4,1)}, pred[1,2,4,128]{3,1,2,0:T(4,128)(4,1)S(1)}, u32[]{:S(2)}) copy-start(pred[1,2,4,128]{3,1,2,0:T(4,128)(4,1)S(1)} %copy.200) | copy-start | bytes 3076
  79.2 7.0 %copy-start.11 = (f32[2,4,128]{1,2,0:T(8,128)}, f32[2,4,128]{1,2,0:T(8,128)S(1)}, u32[]{:S(2)}) copy-start(f32[2,4,128]{1,2,0:T(8,128)S(1)} %copy.100) | copy-start | bytes 12292
  86.3 6.7 %copy-start.8 = (bf16[2,128,4,64]{1,0,3,2:T(2,128)(2,1)S(1)}, bf16[2,128,4,64]{1,0,3,2:T(2,128)(2,1)}, u32[]{:S(2)}) copy-start(bf16[2,128,4,64]{1,0,3,2:T(2,128)(2,1)} %copy-done.7) | copy-start | bytes 393220
  124.9 9.6 %copy-start.22 = (s32[1,128,8]{1,2,0:T(8,128)S(1)}, s32[1,128,8]{1,2,0:T(8,128)}, u32[]{:S(2)}) copy-start(s32[1,128,8]{1,2,0:T(8,128)} %param.26) | copy-start | bytes 12292
  124.9 9.8 %copy-start.25 = (s32[2,4]{1,0:T(2,128)S(1)}, s32[2,4]{1,0:T(2,128)}, u32[]{:S(2)}) copy-start(s32[2,4]{1,0:T(2,128)} %get-tuple-element.115) | copy-start | bytes 100
  124.9 11.1 %copy-start.10 = (bf16[2,128,4,64]{1,0,3,2:T(2,128)(2,1)S(1)}, bf16[2,128,4,64]{1,0,3,2:T(2,128)(2,1)}, u32[]{:S(2)}) copy-start(bf16[2,128,4,64]{1,0,3,2:T(2,128)(2,1)} %copy.103) | copy-start | bytes 393220
  124.9 12.2 %copy-start.9 = (bf16[2,128,4,64]{1,0,3,2:T(2,128)(2,1)S(1)}, bf16[2,128,4,64]{1,0,3,2:T(2,128)(2,1)}, u32[]{:S(2)}) copy-start(bf16[2,128,4,64]{1,0,3,2:T(2,128)(2,1)} %copy-done.7) | copy-start | bytes 393220
  124.9 12.2 %copy-start.17 = (pred[1,2,4,128]{3,1,2,0:T(4,128)(4,1)S(1)}, pred[1,2,4,128]{3,1,2,0:T(4,128)(4,1)}, u32[]{:S(2)}) copy-start(pred[1,2,4,128]{3,1,2,0:T(4,128)(4,1)} %copy-done.16) | copy-start | bytes 3076
  125.0 12.2 %copy-start.20 = (f32[2,4,128]{2,1,0:T(4,128)S(1)}, f32[2,4,128]{2,1,0:T(4,128)}, u32[]{:S(2)}) copy-start(f32[2,4,128]{2,1,0:T(4,128)} %copy-done.19) | copy-start | bytes 12292
  125.0 110.9 %all-to-all-start.1 = ((f32[128,10,512]{2,1,0:T(8,128)}), f32[128,10,512]{2,1,0:T(8,128)}, u32[]{:S(2)}, u32[]{:S(2)}) async-start(f32[128,10,512]{2,1,0:T(8,128)} %pad_maximum_fusion), calls=%async_computation.2 | async-start | bytes 8388608 | tf_op jit(solution)/shard_map/all_to_all | solution.py:200
  134.5 99.7 %reduce-scatter.2.cloned.1.call-start = ((), (), s32[]{:S(2)}) async-start(), calls=%async_computation.3 | async-start | bytes 786432 | tf_op jit(solution)/shard_map/reduce_scatter | solution.py:207
  154.0 11.1 %copy-start.4 = (bf16[2,128,3,256]{1,3,2,0:T(8,128)(2,1)S(1)}, bf16[2,128,3,256]{1,3,2,0:T(8,128)(2,1)}, u32[]{:S(2)}) copy-start(bf16[2,128,3,256]{1,3,2,0:T(8,128)(2,1)} %copy-done.3) | copy-start | bytes 1179652
  154.0 11.1 %copy-start.1 = (bf16[2,512,256]{1,2,0:T(8,128)(2,1)S(1)}, bf16[2,512,256]{1,2,0:T(8,128)(2,1)}, u32[]{:S(2)}) copy-start(bf16[2,512,256]{1,2,0:T(8,128)(2,1)} %copy.92) | copy-start | bytes 1572868
  155.0 78.1 %collective-permute-start.2 = (bf16[256,512]{1,0:T(8,128)(2,1)}, bf16[256,512]{1,0:T(8,128)(2,1)}, u32[]{:S(2)}, u32[]{:S(2)}) collective-permute-start(bf16[256,512]{1,0:T(8,128)(2,1)} %get-tuple-element.109), channel_id=1, source_target_pairs={{0,2},{2,4},{4,6},{6,8},{8,10},{10,12},{12,14},{14,16},{16,18},{18... | collective-permute-start | bytes 786440 | tf_op jit(solution)/shard_map/ppermute | solution.py:29
  158.4 74.7 %collective-permute-start.3 = (bf16[256,512]{1,0:T(8,128)(2,1)}, bf16[256,512]{1,0:T(8,128)(2,1)}, u32[]{:S(2)}, u32[]{:S(2)}) collective-permute-start(bf16[256,512]{1,0:T(8,128)(2,1)} %get-tuple-element.110), channel_id=1, source_target_pairs={{2,0},{4,2},{6,4},{8,6},{10,8},{12,10},{14,12},{16,14},{18,16},{20... | collective-permute-start | bytes 786440 | tf_op jit(solution)/shard_map/ppermute | solution.py:29
  (11 other events, 32.3 us)
Sparse Core Ops, SparseCore 0:
  137.8 13.9 reduce-scatter.1

commit v2 on v1

--- a/solution.py
+++ b/solution.py
@@ -149,37 +149,24 @@
     outgoing = stacked[send_rows[0]]
     received = lax.all_to_all(outgoing, "dom", split_axis=0, concat_axis=0, tiled=True)
     far_all = received.reshape(-1, 2 * col_width)[expander_slot]
-    group = math.gcd(4, per_part)
-    rounds = per_part // group
     base_tile = dom_index * per_part - HALO
-    tile_lanes = jnp.arange(TILE, dtype=jnp.int32)
     batched = jax.vmap(tile_work, in_axes=(0, 0, 0, 0, 0, None, None, None))
-
-    def advance(accum, inputs):
-        query_group, grad_group, list_group, count_group, far_group = inputs
-        attn_group, qgrad_group, near_group, fgrad_group = batched(
-            query_group,
-            grad_group,
-            list_group,
-            count_group,
-            far_group,
-            ext_tiles,
-            far_bias,
-            base_tile,
-        )
-        targets = ((list_group - base_tile)[:, :, None] * TILE + tile_lanes).reshape(-1)
-        accum = accum.at[targets].add(near_group.reshape(-1, 2 * col_width))
-        return (accum, (attn_group, qgrad_group, fgrad_group))
-
-    inputs = (
-        query_rows.reshape(rounds, group, TILE, col_width),
-        attn_grad.reshape(rounds, group, TILE, col_width),
-        tile_list.reshape(rounds, group, -1),
-        tile_count.reshape(rounds, group),
-        far_all.reshape(rounds, group, TILE, DEG, 2 * col_width),
-    )
-    start_grad = jnp.zeros((extended.shape[0], 2 * col_width), jnp.float32)
-    ext_grad, (attn_all, qgrad_all, far_grad) = lax.scan(advance, start_grad, inputs)
+    attn_all, qgrad_all, near_all, far_grad = batched(
+        query_rows.reshape(per_part, TILE, col_width),
+        attn_grad.reshape(per_part, TILE, col_width),
+        tile_list,
+        tile_count,
+        far_all.reshape(per_part, TILE, DEG, 2 * col_width),
+        ext_tiles,
+        far_bias,
+        base_tile,
+    )
+    n_ext = ext_tiles.shape[0]
+    hit = (tile_list - base_tile)[:, :, None] == jnp.arange(n_ext)[None, None, :]
+    near_tiles = near_all.reshape(per_part, tile_list.shape[1], 1, TILE, 2 * col_width)
+    ext_grad = jnp.sum(
+        jnp.where(hit[:, :, :, None, None], near_tiles, 0.0), axis=(0, 1)
+    ).reshape(-1, 2 * col_width)
     attn_mine = attn_all.reshape(node_count, col_width)
     low_part = ext_grad[:rim_rows]
     high_part = ext_grad[rim_rows + node_count :]
@@ -187,20 +174,29 @@
     from_next = from_behind(low_part.astype(jnp.bfloat16), "dom", -1).astype(low_part.dtype)
     from_prev = from_behind(high_part.astype(jnp.bfloat16), "dom", 1).astype(high_part.dtype)
     own_grad = own_grad.at[:rim_rows].add(from_prev).at[node_count - rim_rows :].add(from_next)
-    slot_grad = jnp.zeros((received.shape[0] * received.shape[1], 2 * col_width), jnp.float32)
-    slot_grad = slot_grad.at[expander_slot.reshape(-1)].add(far_grad.reshape(-1, 2 * col_width))
-    n_dom = received.shape[0]
+    n_dom, cap = received.shape[0], received.shape[1]
+    pair_grad = far_grad.reshape(-1, 2 * col_width)
+    pair_hi = lax.reduce_precision(pair_grad, exponent_bits=8, mantissa_bits=7)
+    pair_lo = (pair_grad - pair_hi).astype(jnp.bfloat16)
+    slot_hit = (
+        expander_slot.reshape(1, -1) == jnp.arange(n_dom * cap, dtype=jnp.int32)[:, None]
+    ).astype(jnp.bfloat16)
+    slot_grad = jnp.dot(
+        slot_hit, pair_hi.astype(jnp.bfloat16), preferred_element_type=jnp.float32
+    ) + jnp.dot(slot_hit, pair_lo, preferred_element_type=jnp.float32)
     weight_part = lax.dot_general(
         full_grad, attn_mine, (((0,), (0,)), ((), ())), preferred_element_type=jnp.float32
     ).reshape(n_dom, -1, 2 * col_width)
-    weight_rows = weight_part.shape[1]
     both = jnp.concatenate(
-        [slot_grad.reshape(n_dom, received.shape[1], -1), weight_part], axis=1
-    )
+        [slot_grad.reshape(n_dom, cap, -1), weight_part], axis=1
+    ).astype(jnp.bfloat16)
     both_back = lax.all_to_all(both, "dom", split_axis=0, concat_axis=0, tiled=True)
-    returned = both_back[:, : received.shape[1]]
-    weight_sum = jnp.sum(both_back[:, received.shape[1] :], axis=0)
-    own_grad = own_grad.at[send_rows[0].reshape(-1)].add(returned.reshape(-1, 2 * col_width))
+    returned = both_back[:, :cap].reshape(-1, 2 * col_width)
+    weight_sum = jnp.sum(both_back[:, cap:].astype(jnp.float32), axis=0)
+    row_hit = (
+        send_rows[0].reshape(1, -1) == jnp.arange(node_count, dtype=jnp.int32)[:, None]
+    ).astype(jnp.bfloat16)
+    own_grad = own_grad + jnp.dot(row_hit, returned, preferred_element_type=jnp.float32)
     key_grad = own_grad[:, :col_width].astype(jnp.bfloat16)
     value_grad = own_grad[:, col_width:].astype(jnp.bfloat16)
     partial_out = jnp.dot(attn_mine, out_weight, preferred_element_type=jnp.float32)

time: 255 us -> 202 us (0.79)
  waiting for transfers between devices: 80.3 us -> 31.9 us
  other arithmetic: 52.8 us -> 33.2 us
  matrix products: 9.86 us -> 18.4 us
  local copies, waits for them, and re-layouts: 49.5 us -> 56.9 us
    ppermute x2, waiting for transfers between devices: 66.5 us -> 19.8 us  [from_behind(): lax.ppermute(value, axis, [(source, source + steps) for source in range(l...]
    scatter-add x3 -> x0, other arithmetic: 24.1 us -> none  [the longest x1 8.89 us: shards(): slot_grad.at[expander_slot.reshape(-1)]]
    dot_general x0 -> x3, matrix products: none -> 5.33 us  [the longest x1 2.53 us: shards(): jnp.dot(slot_hit, pair_lo, preferred_element_type=jnp.float32)]
    concatenate x2 -> x3, local copies, waits for them, and re-layouts: 5.22 us -> 8.15 us  [tile_work(): jnp.concatenate([far_kgrad.reshape(TILE, -1, col_width), far_vgrad.reshap...]
    reduce_sum x1 -> x2, other arithmetic: 1.78 us -> 4.58 us  [the longest x1 3.08 us: shards(): jnp.sum(jnp.where(hit[:, :, :, None, None], near_tiles, 0.0), axis=(0, 1))]
    concatenate x2 -> x1, other arithmetic: 4.55 us -> 1.78 us  [shards(): jnp.concatenate([slot_grad.reshape(n_dom, cap, -1), weight_part], axis=1)]
    unnamed x72 -> x73, local copies, waits for them, and re-layouts: 10.4 us -> 12.5 us
  transfers between devices with their start and end apart: 7 -> 7, of which waited for: 2 -> 3; matrix products, arithmetic and copies ran while one was open for 17% -> 37% of each run, Pallas kernels for 0% -> 0%
where the time goes in v2:
time: 202 us; the launch traced here: 200 us
  local copies, waits for them, and re-layouts  56.9 us (28%)
  starting transfers between devices  43.5 us (22%)
  other arithmetic  33.2 us (16%)
  waiting for transfers between devices  31.9 us (16%)
  matrix products  18.4 us (9%)
  between operations  14.6 us (7%)
    ppermute x2, waiting for transfers between devices, from_behind(): lax.ppermute(value, axis, [(source, source + steps) for source in range(l...  19.8 us
    unnamed x73, local copies, waits for them, and re-layouts  12.5 us
    all_to_all x1, starting transfers between devices, shards(): lax.all_to_all(outgoing, 'dom', split_axis=0, concat_axis=0, tiled=True)  12.2 us
    all_to_all x1, waiting for transfers between devices, shards(): lax.all_to_all(outgoing, 'dom', split_axis=0, concat_axis=0, tiled=True)  12 us
    ppermute x1, starting transfers between devices, extended_2(): after = lax.ppermute(leading, axis, down)  10.5 us
    all_to_all x1, starting transfers between devices, shards(): lax.all_to_all(both, 'dom', split_axis=0, concat_axis=0, tiled=True)  9.83 us
    ppermute x2, starting transfers between devices, from_behind(): lax.ppermute(value, axis, [(source, source + steps) for source in range(l...  9.04 us
    concatenate x3, local copies, waits for them, and re-layouts, tile_work(): jnp.concatenate([far_kgrad.reshape(TILE, -1, col_width), far_vgrad.reshap...  8.15 us
  transfers between devices with their start and end apart: 7, of which 3 were waited for; matrix products, arithmetic and copies ran while one was open for 37% of the time, Pallas kernels for 0%

profile of v2, /device:TPU:6, one launch (start us, length us, event | category | flops | bytes accessed | tf_op | source)
XLA Modules:
  0.0 200.4 jit_solution(9151082069503029201)
XLA Ops:
  9.1 10.5 %collective-permute-start.1 = (bf16[256,512]{1,0:T(8,128)(2,1)S(1)}, bf16[256,512]{1,0:T(8,128)(2,1)S(1)}, u32[]{:S(2)}, u32[]{:S(2)}) collective-permute-start(bf16[256,512]{1,0:T(8,128)(2,1)S(1)} %constant_dynamic-update-slice_fusion), channel_id=1, source_target_pairs={{2,0},{4,2},{6,4},{8,6},{10,8},{12,10},{14,12},{16,14},{18,16},{20... | collective-permute-start | bytes 786440 | tf_op jit(solution)/shard_map/ppermute | solution.py:21
  22.4 5.1 %gather_fusion.1 = bf16[1024,512]{1,0:T(8,128)(2,1)} fusion(bf16[256,512]{1,0:T(8,128)(2,1)S(1)} %constant_dynamic-update-slice_fusion, s32[1024]{0:T(1024)S(1)} %broadcast_clamp_fusion), kind=kCustom, calls=%fused_computation.1 | custom fusion | bytes 2101248 | tf_op jit(solution)/shard_map/gather | solution.py:149
  27.5 12.2 %all-to-all-start = ((bf16[128,8,512]{2,1,0:T(8,128)(2,1)}), bf16[128,8,512]{2,1,0:T(8,128)(2,1)S(1)}, u32[]{:S(2)}, u32[]{:S(2)}) async-start(bf16[128,8,512]{2,1,0:T(8,128)(2,1)} %bitcast.13), calls=%async_computation | async-start | bytes 2097152 | tf_op jit(solution)/shard_map/all_to_all | solution.py:150
  39.8 2.0 all_gather.3
  52.8 2.5 %select_reduce_fusion.1 = (f32[2,4,128]{2,1,0:T(4,128)}, f32[2,4,512,128]{3,2,1,0:T(8,128)}) fusion(pred[2,512]{1,0:T(4,128)(4,1)S(1)} %bitcast.144, bf16[2,512,4,64]{1,3,2,0:T(8,128)(2,1)S(1)} %bitcast.132, bf16[2,128,4,64]{1,0,3,2:T(2,128)(2,1)S(1)} %reshape_reshape.6), kind=kOutput, calls=%fused_computation.17 | convolution fusion | flops 68680704 | bytes 2757632 | tf_op jit(solution)/shard_map/vmap(qhd,khd->hqk)/dot_general | solution.py:50
  55.3 12.0 %all-to-all-done = bf16[128,8,512]{2,1,0:T(8,128)(2,1)S(1)} async-done(((bf16[128,8,512]{2,1,0:T(8,128)(2,1)}), bf16[128,8,512]{2,1,0:T(8,128)(2,1)S(1)}, u32[]{:S(2)}, u32[]{:S(2)}) %all-to-all-start) | async-done | bytes 1048608 | tf_op jit(solution)/shard_map/all_to_all | solution.py:150
  67.3 2.7 %gather_fusion.2 = bf16[768,512]{1,0:T(8,128)(2,1)S(1)} fusion(bf16[1024,512]{1,0:T(8,128)(2,1)S(1)} %bitcast.131, s32[1024]{0:T(1024)S(1)} %pad_clamp_fusion), kind=kCustom, calls=%fused_computation.2 | custom fusion | bytes 1575936 | tf_op jit(solution)/shard_map/gather | solution.py:151
  78.1 2.7 %fusion.40 = (f32[2,4,128]{1,2,0:T(8,128)}, f32[2,128,4,3]{2,3,1,0:T(4,128)}) fusion(f32[2,4,128]{1,2,0:T(8,128)} %copy.128, f32[4]{0:T(128)} %param.23, f32[2,4,128,3]{1,3,2,0:T(4,128)S(1)} %copy.158), kind=kLoop, calls=%fused_computation.99 | loop fusion | flops 17408 | bytes 32784 | tf_op jit(solution)/shard_map/vmap()/reduce_sum | solution.py:63
  91.0 2.0 %fusion.27 = f32[256,512]{1,0:T(8,128)} fusion(bf16[256,512]{1,0:T(8,128)(2,1)S(1)} %copy-done, bf16[32,8,2,128]{3,2,1,0:T(2,128)(2,1)} %bitcast.138), kind=kOutput, calls=%fused_computation.68 | convolution fusion | flops 67108864 | bytes 917504 | tf_op jit(solution)/shard_map/dot_general | solution.py:202
  102.6 2.6 %convert_bitcast_fusion.1 = (f32[2,128,4,3]{2,3,1,0:T(4,128)S(1)}, bf16[2,4,128,3]{1,3,2,0:T(4,128)(2,1)}, f32[2,128,4,3]{2,3,1,0:T(4,128)}) fusion(f32[2,4,128,3]{1,3,2,0:T(4,128)} %copy.176, f32[2,4,128]{1,2,0:T(8,128)} %copy.138, f32[2,4,128]{1,2,0:T(8,128)} %copy.137, f32[2,4,128]{1,2,0:T(8,128)} %copy.128, f32[4]{0:T(128)} %param.23, ...), kind=kLoop, calls=%fused_computation.56 | loop fusion | flops 30720 | bytes 67600 | tf_op jit(solution)/shard_map/convert.6
  107.1 3.0 %concatenate.37 = f32[768,256]{1,0:T(8,128)} reshape(f32[2,128,3,4,64]{4,3,2,1,0:T(4,128)} %multiply_bitcast_fusion.1) | data formatting | bytes 1572864 | tf_op jit(solution)/shard_map/vmap()/concatenate | solution.py:114
  110.2 2.1 %constant_dynamic-update-slice_fusion.3 = f32[768,512]{1,0:T(8,128)} fusion(f32[768,256]{1,0:T(8,128)} %concatenate.37), kind=kLoop, calls=%fused_computation.85 | loop fusion | bytes 1572864
  112.3 2.8 %multiply_bitcast_fusion = f32[2,128,3,4,64]{4,3,2,1,0:T(4,128)} fusion(f32[2,128,4,3]{2,3,1,0:T(4,128)} %get-tuple-element.73, f32[2,128,4,64]{3,2,1,0:T(4,128)S(1)} %copy-done.8), kind=kLoop, calls=%fused_computation.19 | loop fusion | flops 196608 | bytes 1060864 | tf_op jit(solution)/shard_map/vmap(hqe,qhd->qehd)/transpose | solution.py:108
  115.1 3.0 %concatenate.38 = f32[768,256]{1,0:T(8,128)} reshape(f32[2,128,3,4,64]{4,3,2,1,0:T(4,128)} %multiply_bitcast_fusion) | data formatting | bytes 1572864 | tf_op jit(solution)/shard_map/vmap()/concatenate | solution.py:114
  118.1 2.1 %constant_dynamic-update-slice_fusion.2 = f32[768,512]{1,0:T(8,128)} fusion(f32[768,512]{1,0:T(8,128)} %constant_dynamic-update-slice_fusion.3, f32[768,256]{1,0:T(8,128)} %concatenate.38), kind=kLoop, calls=%fused_computation.84 | loop fusion | bytes 1572864 | tf_op jit(solution)/shard_map/vmap()/concatenate | solution.py:114
  120.2 2.5 %fusion = f32[1024,512]{1,0:T(8,128)S(1)} fusion(s32[768]{0:T(1024)S(1)} %copy-done.25, f32[768,512]{1,0:T(8,128)} %constant_dynamic-update-slice_fusion.2), kind=kOutput, calls=%fused_computation.5 | convolution fusion | flops 807272448 | bytes 3673088 | tf_op jit(solution)/shard_map/dot_general | solution.py:186
  125.6 9.8 %all-to-all-start.1 = ((bf16[128,10,512]{2,1,0:T(8,128)(2,1)}), bf16[128,10,512]{2,1,0:T(8,128)(2,1)}, u32[]{:S(2)}, u32[]{:S(2)}) async-start(bf16[128,10,512]{2,1,0:T(8,128)(2,1)} %pad_maximum_fusion), calls=%async_computation.2 | async-start | bytes 4194304 | tf_op jit(solution)/shard_map/all_to_all | solution.py:193
  137.2 2.5 %concatenate.35 = f32[2,4,1,128,256]{3,1,4,0,2:T(4,128)} reshape(f32[2,512,4,64]{1,3,2,0:T(8,128)} %convolution_bitcast_fusion) | data formatting | bytes 2097152 | tf_op jit(solution)/shard_map/vmap()/concatenate | solution.py:111
  139.7 2.0 %multiply_convert_fusion = bf16[2,4,128,512]{2,3,1,0:T(8,128)(2,1)S(1)} fusion(bf16[2,512,4,64]{1,3,2,0:T(8,128)(2,1)} %bitcast.141, f32[2,4,128]{2,1,0:T(4,128)S(1)} %bitcast.150, f32[2,4,128]{2,1,0:T(4,128)S(1)} %copy-done.20, f32[2,4,128]{2,1,0:T(4,128)S(1)} %max.7, f32[2,4,512,128]{3,2,1,0:T(8,128)S(1)} %copy-done.2, pred[2,512]{1,0:T(4,128)(4,1)S(1)} %bitcast.148, ...), kind=kOutput, calls=%fused_computation.15 | convolution fusion | flops 70778880 | bytes 3814400 | tf_op jit(solution)/shard_map/vmap(qhd,khd->hqk)/dot_general | solution.py:80
  144.6 2.0 %maximum_bitcast_fusion = f32[2,4,128,512]{2,1,3,0:T(4,128)S(1)} fusion(f32[2,4,1,128,256]{3,1,4,0,2:T(4,128)} %concatenate.35, f32[2,4,1,128,256]{3,1,4,0,2:T(4,128)} %concatenate.34), kind=kLoop, calls=%fused_computation.9 | loop fusion | flops 524288 | bytes 4194304 | tf_op jit(solution)/shard_map/jit(_where)/broadcast_in_dim | solution.py:168
  148.5 3.1 %select_reduce_fusion = f32[6,128,512]{2,1,0:T(8,128)S(1)} fusion(f32[2,4,128,512]{3,2,1,0:T(8,128)} %copy.144, pred[2,4,6]{2,1,0:T(4,128)(4,1)S(1)} %copy-done.26), kind=kLoop, calls=%fused_computation.3 | loop fusion | flops 5898240 | bytes 3670064 | tf_op jit(solution)/shard_map/reduce_sum | solution.py:167
  155.9 7.1 %collective-permute-start.3 = (bf16[256,512]{1,0:T(8,128)(2,1)S(1)}, bf16[256,512]{1,0:T(8,128)(2,1)}, u32[]{:S(2)}, u32[]{:S(2)}) collective-permute-start(bf16[256,512]{1,0:T(8,128)(2,1)S(1)} %bitcast.143), channel_id=1, source_target_pairs={{2,0},{4,2},{6,4},{8,6},{10,8},{12,10},{14,12},{16,14},{18,16},{20... | collective-permute-start | bytes 786440 | tf_op jit(solution)/shard_map/ppermute | solution.py:29
  169.1 14.2 %collective-permute-done.3 = bf16[256,512]{1,0:T(8,128)(2,1)} collective-permute-done((bf16[256,512]{1,0:T(8,128)(2,1)S(1)}, bf16[256,512]{1,0:T(8,128)(2,1)}, u32[]{:S(2)}, u32[]{:S(2)}) %collective-permute-start.3) | collective-permute-done | bytes 262176 | tf_op jit(solution)/shard_map/ppermute | solution.py:29
  183.3 5.6 %collective-permute-done.2 = bf16[256,512]{1,0:T(8,128)(2,1)} collective-permute-done((bf16[256,512]{1,0:T(8,128)(2,1)S(1)}, bf16[256,512]{1,0:T(8,128)(2,1)}, u32[]{:S(2)}, u32[]{:S(2)}) %collective-permute-start.2) | collective-permute-done | bytes 262176 | tf_op jit(solution)/shard_map/ppermute | solution.py:29
  (151 shorter events, 69.6 us)
Async XLA Ops:
  7.2 34.6 %copy-start = (bf16[256,512]{1,0:T(8,128)(2,1)S(1)}, bf16[256,512]{1,0:T(8,128)(2,1)}, u32[]{:S(2)}) copy-start(bf16[256,512]{1,0:T(8,128)(2,1)} %param.21) | copy-start | bytes 786436
  9.1 39.9 %collective-permute-start.1 = (bf16[256,512]{1,0:T(8,128)(2,1)S(1)}, bf16[256,512]{1,0:T(8,128)(2,1)S(1)}, u32[]{:S(2)}, u32[]{:S(2)}) collective-permute-start(bf16[256,512]{1,0:T(8,128)(2,1)S(1)} %constant_dynamic-update-slice_fusion), channel_id=1, source_target_pairs={{2,0},{4,2},{6,4},{8,6},{10,8},{12,10},{14,12},{16,14},{18,16},{20... | collective-permute-start | bytes 786440 | tf_op jit(solution)/shard_map/ppermute | solution.py:21
  19.5 29.4 %collective-permute-start = (bf16[256,512]{1,0:T(8,128)(2,1)S(1)}, bf16[256,512]{1,0:T(8,128)(2,1)S(1)}, u32[]{:S(2)}, u32[]{:S(2)}) collective-permute-start(bf16[256,512]{1,0:T(8,128)(2,1)S(1)} %constant_dynamic-update-slice_fusion), channel_id=1, source_target_pairs={{0,2},{2,4},{4,6},{6,8},{8,10},{10,12},{12,14},{14,16},{16,18},{18... | collective-permute-start | bytes 786440 | tf_op jit(solution)/shard_map/ppermute | solution.py:20
  27.4 12.3 %copy-start.21 = (s32[256,3]{0,1:T(4,128)S(1)}, s32[256,3]{0,1:T(4,128)}, u32[]{:S(2)}) copy-start(s32[256,3]{0,1:T(4,128)} %param.27) | copy-start | bytes 9220
  27.4 12.3 %copy-start.15 = (bf16[256,256]{1,0:T(8,128)(2,1)S(1)}, bf16[256,256]{1,0:T(8,128)(2,1)}, u32[]{:S(2)}) copy-start(bf16[256,256]{1,0:T(8,128)(2,1)} %param.22) | copy-start | bytes 393220
  27.4 14.3 %copy-start.27 = (s32[2,4]{1,0:T(2,128)S(1)}, s32[2,4]{1,0:T(2,128)}, u32[]{:S(2)}) copy-start(s32[2,4]{1,0:T(2,128)} %param.24) | copy-start | bytes 100
  27.5 14.6 %copy-start.28 = (s32[2]{0:T(128)S(1)}, s32[2]{0:T(128)}, u32[]{:S(2)}) copy-start(s32[2]{0:T(128)} %param.25) | copy-start | bytes 28
  27.5 15.1 %copy-start.16 = (bf16[256,256]{1,0:T(8,128)(2,1)S(1)}, bf16[256,256]{1,0:T(8,128)(2,1)}, u32[]{:S(2)}) copy-start(bf16[256,256]{1,0:T(8,128)(2,1)} %param.18) | copy-start | bytes 393220
  27.5 39.9 %all-to-all-start = ((bf16[128,8,512]{2,1,0:T(8,128)(2,1)}), bf16[128,8,512]{2,1,0:T(8,128)(2,1)S(1)}, u32[]{:S(2)}, u32[]{:S(2)}) async-start(bf16[128,8,512]{2,1,0:T(8,128)(2,1)} %bitcast.13), calls=%async_computation | async-start | bytes 2097152 | tf_op jit(solution)/shard_map/all_to_all | solution.py:150
  39.7 127.8 %reduce-scatter.2.cloned.1.call-start = ((), (), s32[]{:S(2)}) async-start(), calls=%async_computation.3 | async-start | bytes 786432 | tf_op jit(solution)/shard_map/reduce_scatter | solution.py:203
  42.9 6.1 %copy-start.9 = (bf16[2,128,4,64]{1,0,3,2:T(2,128)(2,1)}, bf16[2,128,4,64]{1,0,3,2:T(2,128)(2,1)S(1)}, u32[]{:S(2)}) copy-start(bf16[2,128,4,64]{1,0,3,2:T(2,128)(2,1)S(1)} %reshape_reshape.7) | copy-start | bytes 393220
  44.4 8.4 %copy-start.17 = (pred[1,2,4,128]{3,1,2,0:T(4,128)(4,1)}, pred[1,2,4,128]{3,1,2,0:T(4,128)(4,1)S(1)}, u32[]{:S(2)}) copy-start(pred[1,2,4,128]{3,1,2,0:T(4,128)(4,1)S(1)} %copy.224) | copy-start | bytes 3076
  73.1 8.8 %copy-start.2 = (f32[2,4,512,128]{3,2,1,0:T(8,128)S(1)}, f32[2,4,512,128]{3,2,1,0:T(8,128)}, u32[]{:S(2)}) copy-start(f32[2,4,512,128]{3,2,1,0:T(8,128)} %get-tuple-element.81) | copy-start | bytes 6291460
  107.1 5.2 %copy-start.8 = (f32[2,128,4,64]{3,2,1,0:T(4,128)S(1)}, f32[2,128,4,64]{3,2,1,0:T(4,128)}, u32[]{:S(2)}) copy-start(f32[2,128,4,64]{3,2,1,0:T(4,128)} %copy.148) | copy-start | bytes 786436
  115.1 5.1 %copy-start.25 = (s32[768]{0:T(1024)S(1)}, s32[768]{0:T(1024)}, u32[]{:S(2)}) copy-start(s32[768]{0:T(1024)} %eq.54) | copy-start | bytes 9220
  125.5 9.8 %copy-start.10 = (bf16[2,128,4,64]{1,0,3,2:T(2,128)(2,1)S(1)}, bf16[2,128,4,64]{1,0,3,2:T(2,128)(2,1)}, u32[]{:S(2)}) copy-start(bf16[2,128,4,64]{1,0,3,2:T(2,128)(2,1)} %copy-done.9) | copy-start | bytes 393220
  125.6 9.9 %copy-start.18 = (pred[1,2,4,128]{3,1,2,0:T(4,128)(4,1)S(1)}, pred[1,2,4,128]{3,1,2,0:T(4,128)(4,1)}, u32[]{:S(2)}) copy-start(pred[1,2,4,128]{3,1,2,0:T(4,128)(4,1)} %copy-done.17) | copy-start | bytes 3076
  125.6 9.9 %copy-start.20 = (f32[2,4,128]{2,1,0:T(4,128)S(1)}, f32[2,4,128]{2,1,0:T(4,128)}, u32[]{:S(2)}) copy-start(f32[2,4,128]{2,1,0:T(4,128)} %copy-done.19) | copy-start | bytes 12292
  125.6 63.4 %all-to-all-start.1 = ((bf16[128,10,512]{2,1,0:T(8,128)(2,1)}), bf16[128,10,512]{2,1,0:T(8,128)(2,1)}, u32[]{:S(2)}, u32[]{:S(2)}) async-start(bf16[128,10,512]{2,1,0:T(8,128)(2,1)} %pad_maximum_fusion), calls=%async_computation.2 | async-start | bytes 4194304 | tf_op jit(solution)/shard_map/all_to_all | solution.py:193
  152.6 13.4 %copy-start.4 = (bf16[2,4,128,512]{2,3,1,0:T(8,128)(2,1)S(1)}, bf16[2,4,128,512]{2,3,1,0:T(8,128)(2,1)}, u32[]{:S(2)}) copy-start(bf16[2,4,128,512]{2,3,1,0:T(8,128)(2,1)} %copy-done.3) | copy-start | bytes 3145732
  155.9 33.1 %slice-start = ((f32[6,128,512]{2,1,0:T(8,128)}), f32[2,128,512]{2,1,0:T(8,128)S(1)}, s32[]{:S(2)}) async-start(f32[6,128,512]{2,1,0:T(8,128)} %copy-done.1), calls=%async_computation.4 | async-start | bytes 1048576 | tf_op jit(solution)/shard_map/slice | solution.py:173
  155.9 33.1 %copy-start.24 = (s32[1024]{0:T(1024)S(1)}, s32[1024]{0:T(1024)}, u32[]{:S(2)}) copy-start(s32[1024]{0:T(1024)} %eq.50) | copy-start | bytes 12292
  155.9 27.4 %collective-permute-start.3 = (bf16[256,512]{1,0:T(8,128)(2,1)S(1)}, bf16[256,512]{1,0:T(8,128)(2,1)}, u32[]{:S(2)}, u32[]{:S(2)}) collective-permute-start(bf16[256,512]{1,0:T(8,128)(2,1)S(1)} %bitcast.143), channel_id=1, source_target_pairs={{2,0},{4,2},{6,4},{8,6},{10,8},{12,10},{14,12},{16,14},{18,16},{20... | collective-permute-start | bytes 786440 | tf_op jit(solution)/shard_map/ppermute | solution.py:29
  163.0 25.9 %collective-permute-start.2 = (bf16[256,512]{1,0:T(8,128)(2,1)S(1)}, bf16[256,512]{1,0:T(8,128)(2,1)}, u32[]{:S(2)}, u32[]{:S(2)}) collective-permute-start(bf16[256,512]{1,0:T(8,128)(2,1)S(1)} %bitcast.142), channel_id=1, source_target_pairs={{0,2},{2,4},{4,6},{6,8},{8,10},{10,12},{12,14},{14,16},{16,18},{18... | collective-permute-start | bytes 786440 | tf_op jit(solution)/shard_map/ppermute | solution.py:29
  (13 other events, 26.5 us)
Sparse Core Ops, SparseCore 0:
  95.1 9.1 reduce-scatter.1

commit v3 on v2

--- a/solution.py
+++ b/solution.py
@@ -1,8 +1,11 @@
+import functools
 import math
 
 import jax
 import jax.numpy as jnp
 from jax import lax
+from jax.experimental import pallas as pl
+from jax.experimental.pallas import tpu as pltpu
 from jax.sharding import PartitionSpec as P
 
 TILE = 128
@@ -120,6 +123,108 @@
         near_grad,
         far_grad,
     )
+
+
+def _attn_kernel(heads, kt, pos_ref, cnt_ref, bias_ref, q_ref, do_ref, ext_ref, far_ref,
+                 attn_ref, qg_ref, eg_ref, fg_ref, attn_acc, qg_acc):
+    cols = q_ref.shape[1]
+    hs = cols // heads
+    scale = hs ** (-0.5)
+    n_tiles = q_ref.shape[0] // TILE
+    f32, bf16 = jnp.float32, jnp.bfloat16
+    eg_ref[...] = jnp.zeros(eg_ref.shape, f32)
+    fg_ref[...] = jnp.zeros(fg_ref.shape, f32)
+    attn_acc[...] = jnp.zeros(attn_acc.shape, f32)
+    qg_acc[...] = jnp.zeros(qg_acc.shape, f32)
+    lane = lax.broadcasted_iota(jnp.int32, (TILE, cols), 1)
+    nt = (((1,), (1,)), ((), ()))
+    tn = (((0,), (0,)), ((), ()))
+    for t in range(n_tiles):
+        rows = pl.ds(t * TILE, TILE)
+        count = cnt_ref[t]
+        pos = [pos_ref[t * kt + j] for j in range(kt)]
+
+        def head_body(h, carry):
+            mask = (lane >= h * hs) & (lane < (h + 1) * hs)
+            q = q_ref[rows, :]
+            do = do_ref[rows, :]
+            qf = q.astype(f32)
+            dof = do.astype(f32)
+            qh = jnp.where(mask, q, jnp.zeros_like(q))
+            doh = jnp.where(mask, do, jnp.zeros_like(do))
+            keys = [ext_ref[pos[j], :, :cols] for j in range(kt)]
+            vals = [ext_ref[pos[j], :, cols:] for j in range(kt)]
+            live = [j < count for j in range(kt)]
+            s = [lax.dot_general(qh, keys[j], nt, preferred_element_type=f32) * scale for j in range(kt)]
+            fk = [far_ref[e, rows, :cols].astype(f32) for e in range(DEG)]
+            fv = [far_ref[e, rows, cols:].astype(f32) for e in range(DEG)]
+            bias = bias_ref[h]
+            fs = [jnp.sum(jnp.where(mask, qf * fk[e], 0.0), axis=1, keepdims=True) * scale + bias
+                  for e in range(DEG)]
+            m = fs[0]
+            for e in range(1, DEG):
+                m = jnp.maximum(m, fs[e])
+            for j in range(kt):
+                m = jnp.maximum(m, jnp.where(live[j], jnp.max(s[j], axis=1, keepdims=True), -jnp.inf))
+            ne = [jnp.where(live[j], jnp.exp(s[j] - m), 0.0) for j in range(kt)]
+            fe = [jnp.exp(fs[e] - m) for e in range(DEG)]
+            row_sum = fe[0] + fe[1] + fe[2]
+            row_sum = jnp.sum(ne[0], axis=1, keepdims=True) + row_sum
+            for j in range(1, kt):
+                row_sum = row_sum + jnp.sum(ne[j], axis=1, keepdims=True)
+            mixed = jnp.dot(ne[0].astype(bf16), vals[0], preferred_element_type=f32)
+            for j in range(1, kt):
+                mixed = mixed + jnp.dot(ne[j].astype(bf16), vals[j], preferred_element_type=f32)
+            for e in range(DEG):
+                mixed = mixed + fe[e].astype(bf16).astype(f32) * fv[e]
+            attn = (mixed / row_sum).astype(bf16).astype(f32)
+            attn_acc[rows, :] += jnp.where(mask, attn, 0.0)
+            delta = jnp.sum(jnp.where(mask, dof * attn, 0.0), axis=1, keepdims=True)
+            qg = None
+            for j in range(kt):
+                ndp = lax.dot_general(doh, vals[j], nt, preferred_element_type=f32)
+                npr = ne[j] / row_sum
+                nds = (npr * (ndp - delta)).astype(bf16)
+                part = jnp.dot(nds, keys[j], preferred_element_type=f32)
+                qg = part if qg is None else qg + part
+                kg = lax.dot_general(nds, qh, tn, preferred_element_type=f32) * scale
+                vg = lax.dot_general(npr.astype(bf16), doh, tn, preferred_element_type=f32)
+                eg_ref[pos[j], :, :cols] += kg
+                eg_ref[pos[j], :, cols:] += vg
+            for e in range(DEG):
+                fdp = jnp.sum(jnp.where(mask, dof * fv[e], 0.0), axis=1, keepdims=True)
+                fpr = fe[e] / row_sum
+                fds = (fpr * (fdp - delta)).astype(bf16).astype(f32)
+                qg = qg + fds * fk[e]
+                fg_ref[e, rows, :cols] += jnp.where(mask, fds * qf * scale, 0.0)
+                fg_ref[e, rows, cols:] += jnp.where(mask, fpr.astype(bf16).astype(f32) * dof, 0.0)
+            qg_acc[rows, :] += jnp.where(mask, qg * scale, 0.0)
+            return carry
+
+        lax.fori_loop(0, heads, head_body, 0)
+        attn_ref[rows, :] = attn_acc[rows, :].astype(attn_ref.dtype)
+        qg_ref[rows, :] = qg_acc[rows, :].astype(qg_ref.dtype)
+
+
+def attention_tiles(pos, cnt, bias, q, do, ext, far):
+    heads = bias.shape[0]
+    kt = pos.shape[0] // cnt.shape[0]
+    n, cols = q.shape
+    smem = pl.BlockSpec(memory_space=pltpu.SMEM)
+    vmem = pl.BlockSpec(memory_space=pltpu.VMEM)
+    return pl.pallas_call(
+        functools.partial(_attn_kernel, heads, kt),
+        out_shape=(
+            jax.ShapeDtypeStruct((n, cols), jnp.bfloat16),
+            jax.ShapeDtypeStruct((n, cols), jnp.bfloat16),
+            jax.ShapeDtypeStruct(ext.shape, jnp.float32),
+            jax.ShapeDtypeStruct(far.shape, jnp.float32),
+        ),
+        in_specs=[smem, smem, smem, vmem, vmem, vmem, vmem],
+        out_specs=(vmem, vmem, vmem, vmem),
+        scratch_shapes=[pltpu.VMEM((n, cols), jnp.float32), pltpu.VMEM((n, cols), jnp.float32)],
+        cost_estimate=pl.CostEstimate(flops=int(2 * n * kt * TILE * cols * 6), bytes_accessed=int(8 * 1024 * 1024), transcendentals=int(n * heads * (kt * TILE + DEG))),
+    )(pos, cnt, bias, q, do, ext, far)
 
 
 def shards(
@@ -146,27 +251,36 @@
     rim_rows = HALO * TILE
     extended = extended_2(stacked, (("dom", 0),), rim_rows)
     ext_tiles = extended.reshape(-1, TILE, 2 * col_width)
-    outgoing = stacked[send_rows[0]]
+    send_hit = (
+        send_rows[0].reshape(-1, 1) == jnp.arange(node_count, dtype=jnp.int32)[None, :]
+    ).astype(jnp.bfloat16)
+    outgoing = (
+        jnp.dot(send_hit, stacked, preferred_element_type=jnp.float32)
+        .astype(jnp.bfloat16)
+        .reshape(send_rows.shape[1], send_rows.shape[2], -1)
+    )
     received = lax.all_to_all(outgoing, "dom", split_axis=0, concat_axis=0, tiled=True)
-    far_all = received.reshape(-1, 2 * col_width)[expander_slot]
+    edge_slots = expander_slot.T.reshape(-1)
+    n_recv = received.shape[0] * received.shape[1]
+    far_hit = (
+        edge_slots[:, None] == jnp.arange(n_recv, dtype=jnp.int32)[None, :]
+    ).astype(jnp.bfloat16)
+    far_all = (
+        jnp.dot(far_hit, received.reshape(n_recv, -1), preferred_element_type=jnp.float32)
+        .astype(jnp.bfloat16)
+        .reshape(DEG, node_count, -1)
+    )
     base_tile = dom_index * per_part - HALO
-    batched = jax.vmap(tile_work, in_axes=(0, 0, 0, 0, 0, None, None, None))
-    attn_all, qgrad_all, near_all, far_grad = batched(
-        query_rows.reshape(per_part, TILE, col_width),
-        attn_grad.reshape(per_part, TILE, col_width),
-        tile_list,
+    attn_all, qgrad_all, ext_grad, far_grad = attention_tiles(
+        (tile_list - base_tile).reshape(-1),
         tile_count,
-        far_all.reshape(per_part, TILE, DEG, 2 * col_width),
+        far_bias,
+        query_rows,
+        attn_grad,
         ext_tiles,
-        far_bias,
-        base_tile,
-    )
-    n_ext = ext_tiles.shape[0]
-    hit = (tile_list - base_tile)[:, :, None] == jnp.arange(n_ext)[None, None, :]
-    near_tiles = near_all.reshape(per_part, tile_list.shape[1], 1, TILE, 2 * col_width)
-    ext_grad = jnp.sum(
-        jnp.where(hit[:, :, :, None, None], near_tiles, 0.0), axis=(0, 1)
-    ).reshape(-1, 2 * col_width)
+        far_all,
+    )
+    ext_grad = ext_grad.reshape(-1, 2 * col_width)
     attn_mine = attn_all.reshape(node_count, col_width)
     low_part = ext_grad[:rim_rows]
     high_part = ext_grad[rim_rows + node_count :]
@@ -179,7 +293,7 @@
     pair_hi = lax.reduce_precision(pair_grad, exponent_bits=8, mantissa_bits=7)
     pair_lo = (pair_grad - pair_hi).astype(jnp.bfloat16)
     slot_hit = (
-        expander_slot.reshape(1, -1) == jnp.arange(n_dom * cap, dtype=jnp.int32)[:, None]
+        edge_slots.reshape(1, -1) == jnp.arange(n_dom * cap, dtype=jnp.int32)[:, None]
     ).astype(jnp.bfloat16)
     slot_grad = jnp.dot(
         slot_hit, pair_hi.astype(jnp.bfloat16), preferred_element_type=jnp.float32

time: 202 us -> 158 us (0.78)
  local copies, waits for them, and re-layouts: 56.9 us -> 5.09 us
  waiting for transfers between devices: 31.9 us -> 60.7 us
  other arithmetic: 33.2 us -> 6.15 us
  Pallas kernels: 0 us -> 15.5 us
  matrix products: 18.4 us -> 10.3 us
    all_to_all x1, waiting for transfers between devices: 0.01 us -> 30.9 us  [shards(): lax.all_to_all(both, 'dom', split_axis=0, concat_axis=0, tiled=True)]
    ppermute x2, waiting for transfers between devices: 19.8 us -> 2.51 us  [from_behind(): lax.ppermute(value, axis, [(source, source + steps) for source in range(l...]
    pallas_call x0 -> x1, Pallas kernels: none -> 15.5 us  [attention_tiles(): pl.pallas_call(functools.partial(_attn_kernel, heads, kt), out_shape=(jax...]
    ppermute x1, waiting for transfers between devices: 0.01 us -> 14.6 us  [extended_2(): after = lax.ppermute(leading, axis, down)]
    concatenate x5 -> x0, local copies, waits for them, and re-layouts: 12 us -> none  [the longest x3 8.15 us: tile_work(): jnp.concatenate([far_kgrad.reshape(TILE, -1, col_width), far_vgrad.reshap...]
    all_to_all x1, waiting for transfers between devices: 12 us -> 0.01 us  [shards(): lax.all_to_all(outgoing, 'dom', split_axis=0, concat_axis=0, tiled=True)]
    unnamed x73 -> x16, local copies, waits for them, and re-layouts: 12.5 us -> 1.78 us
    reduce_sum x4 -> x0, other arithmetic: 8.49 us -> none  [the longest x2 4.39 us: tile_work(): row_sum = jnp.sum(near_exp, axis=2) + jnp.sum(far_exp, axis=2)]
  transfers between devices with their start and end apart: 7 -> 7, of which waited for: 3 -> 5; matrix products, arithmetic and copies ran while one was open for 37% -> 5% of each run, Pallas kernels for 0% -> 0%
where the time goes in v3:
time: 158 us; the launch traced here: 157 us
  waiting for transfers between devices  60.7 us (38%)
  starting transfers between devices  43.4 us (27%)
  Pallas kernels  15.5 us (10%)
  between operations  14.3 us (9%)
  matrix products  10.3 us (7%)
  other arithmetic  6.15 us (4%)
  local copies, waits for them, and re-layouts  5.09 us (3%)
  blocking collectives  1.99 us (1%)
    all_to_all x1, waiting for transfers between devices, shards(): lax.all_to_all(both, 'dom', split_axis=0, concat_axis=0, tiled=True)  30.9 us
    all_to_all x1, starting transfers between devices, shards(): lax.all_to_all(outgoing, 'dom', split_axis=0, concat_axis=0, tiled=True)  15.9 us
    pallas_call x1, Pallas kernels, attention_tiles(): pl.pallas_call(functools.partial(_attn_kernel, heads, kt), out_shape=(jax...  15.5 us
    ppermute x1, waiting for transfers between devices, extended_2(): after = lax.ppermute(leading, axis, down)  14.6 us
    all_to_all x1, starting transfers between devices, shards(): lax.all_to_all(both, 'dom', split_axis=0, concat_axis=0, tiled=True)  9.61 us
    ppermute x2, starting transfers between devices, from_behind(): lax.ppermute(value, axis, [(source, source + steps) for source in range(l...  8.9 us
    reduce_scatter x1, waiting for transfers between devices, shards(): lax.psum_scatter(partial_out, 'head', scatter_dimension=1, tiled=True)  7.08 us
    ppermute x1, starting transfers between devices, extended_2(): after = lax.ppermute(leading, axis, down)  6.98 us
  transfers between devices with their start and end apart: 7, of which 5 were waited for; matrix products, arithmetic and copies ran while one was open for 5% of the time, Pallas kernels for 0%

profile of v3, /device:TPU:6, one launch (start us, length us, event | category | flops | bytes accessed | tf_op | source)
XLA Modules:
  0.0 157.3 jit_solution(1128604391337930149)
XLA Ops:
  10.0 1.5 fusion.8
  11.4 15.9 %all-to-all-start = ((bf16[128,8,512]{2,1,0:T(8,128)(2,1)}), bf16[128,8,512]{2,1,0:T(8,128)(2,1)S(1)}, u32[]{:S(2)}, u32[]{:S(2)}) async-start(bf16[128,8,512]{2,1,0:T(8,128)(2,1)} %fusion.8), calls=%async_computation | async-start | bytes 2097152 | tf_op jit(solution)/shard_map/all_to_all | solution.py:262
  27.4 7.0 %collective-permute-start.1 = (bf16[256,512]{1,0:T(8,128)(2,1)S(1)}, bf16[256,512]{1,0:T(8,128)(2,1)S(1)}, u32[]{:S(2)}, u32[]{:S(2)}) collective-permute-start(bf16[256,512]{1,0:T(8,128)(2,1)S(1)} %constant_dynamic-update-slice_fusion), channel_id=1, source_target_pairs={{2,0},{4,2},{6,4},{8,6},{10,8},{12,10},{14,12},{16,14},{18,16},{20... | collective-permute-start | bytes 786440 | tf_op jit(solution)/shard_map/ppermute | solution.py:24
  34.3 1.9 %collective-permute-start = (bf16[256,512]{1,0:T(8,128)(2,1)S(1)}, bf16[256,512]{1,0:T(8,128)(2,1)S(1)}, u32[]{:S(2)}, u32[]{:S(2)}) collective-permute-start(bf16[256,512]{1,0:T(8,128)(2,1)S(1)} %constant_dynamic-update-slice_fusion), channel_id=1, source_target_pairs={{0,2},{2,4},{4,6},{6,8},{8,10},{10,12},{12,14},{14,16},{16,18},{18... | collective-permute-start | bytes 786440 | tf_op jit(solution)/shard_map/ppermute | solution.py:23
  36.3 2.0 %all_gather.3 = bf16[256,512]{1,0:T(8,128)(2,1)S(1)} all-gather(bf16[256,256]{1,0:T(8,128)(2,1)S(1)} %copy-done.4), channel_id=1, replica_groups=mesh['dom'=128,'head'=2] {'head'}, dimensions={1}, use_global_device_ids=true | all-gather | bytes 393216 | tf_op jit(solution)/shard_map/all_gather | solution.py:246
  39.8 14.6 %collective-permute-done.1 = bf16[256,512]{1,0:T(8,128)(2,1)S(1)} collective-permute-done((bf16[256,512]{1,0:T(8,128)(2,1)S(1)}, bf16[256,512]{1,0:T(8,128)(2,1)S(1)}, u32[]{:S(2)}, u32[]{:S(2)}) %collective-permute-start.1) | collective-permute-done | bytes 262176 | tf_op jit(solution)/shard_map/ppermute | solution.py:24
  54.5 5.5 %collective-permute-done = bf16[256,512]{1,0:T(8,128)(2,1)S(1)} collective-permute-done((bf16[256,512]{1,0:T(8,128)(2,1)S(1)}, bf16[256,512]{1,0:T(8,128)(2,1)S(1)}, u32[]{:S(2)}, u32[]{:S(2)}) %collective-permute-start) | collective-permute-done | bytes 262176 | tf_op jit(solution)/shard_map/ppermute | solution.py:23
  60.0 0.9 pad_maximum_fusion.1
  60.9 1.9 %fusion.7 = bf16[768,512]{1,0:T(8,128)(2,1)} fusion(s32[768]{0:T(1024)S(1)} %eq.56, bf16[128,8,512]{2,1,0:T(8,128)(2,1)S(1)} %all-to-all-done), kind=kOutput, calls=%fused_computation.14 | convolution fusion | flops 806486016 | bytes 1838080 | tf_op jit(solution)/shard_map/dot_general | solution.py:269
  62.8 15.5 %shard_map.147 = (bf16[256,256]{1,0:T(8,128)(2,1)}, bf16[256,256]{1,0:T(8,128)(2,1)}, f32[6,128,512]{2,1,0:T(8,128)}, f32[3,256,512]{2,1,0:T(8,128)}) custom-call(s32[8]{0:T(128)} %reshape.102.pos_ref, s32[2]{0:T(128)} %cnt_ref.1, f32[4]{0:T(128)} %bias_ref.1, bf16[256,256]{1,0:T(8,128)(2,1)} %q_ref.1, bf16[256,256]{1,0:T(8,128)(2,1)} %convolution_convert_fusion.2.do_ref, ...), custom_call_target="tpu_custom_call" | custom-call | flops 402653184 | bytes 8388608 | tf_op jit(solution)/shard_map/pallas_call | solution.py:215
  78.3 1.3 fusion.10
  80.1 1.0 fusion
  81.1 1.0 fusion.9
  82.1 1.8 %pad_maximum_fusion = bf16[128,10,512]{2,1,0:T(8,128)(2,1)} fusion(bf16[128,2,512]{2,1,0:T(2,128)(2,1)S(1)} %reshape.109, bf16[128,8,512]{2,1,0:T(8,128)(2,1)S(1)} %fusion.9), kind=kLoop, calls=%fused_computation.7 | loop fusion | flops 2621440 | bytes 2621440 | tf_op jit(solution)/shard_map/concatenate | solution.py:304
  83.9 9.6 %all-to-all-start.1 = ((bf16[128,10,512]{2,1,0:T(8,128)(2,1)}), bf16[128,10,512]{2,1,0:T(8,128)(2,1)}, u32[]{:S(2)}, u32[]{:S(2)}) async-start(bf16[128,10,512]{2,1,0:T(8,128)(2,1)} %pad_maximum_fusion), calls=%async_computation.2 | async-start | bytes 4194304 | tf_op jit(solution)/shard_map/all_to_all | solution.py:307
  93.6 1.1 fusion.20
  94.8 7.0 %collective-permute-start.3 = (bf16[256,512]{1,0:T(8,128)(2,1)S(1)}, bf16[256,512]{1,0:T(8,128)(2,1)S(1)}, u32[]{:S(2)}, u32[]{:S(2)}) collective-permute-start(bf16[256,512]{1,0:T(8,128)(2,1)S(1)} %bitcast.42), channel_id=1, source_target_pairs={{2,0},{4,2},{6,4},{8,6},{10,8},{12,10},{14,12},{16,14},{18,16},{20... | collective-permute-start | bytes 786440 | tf_op jit(solution)/shard_map/ppermute | solution.py:32
  101.8 1.9 %collective-permute-start.2 = (bf16[256,512]{1,0:T(8,128)(2,1)S(1)}, bf16[256,512]{1,0:T(8,128)(2,1)}, u32[]{:S(2)}, u32[]{:S(2)}) collective-permute-start(bf16[256,512]{1,0:T(8,128)(2,1)S(1)} %bitcast.41), channel_id=1, source_target_pairs={{0,2},{2,4},{4,6},{6,8},{8,10},{10,12},{12,14},{14,16},{16,18},{18... | collective-permute-start | bytes 786440 | tf_op jit(solution)/shard_map/ppermute | solution.py:32
  103.8 7.1 %reduce-scatter.2.cloned.1.call-done = f32[256,256]{1,0:T(8,128)} async-done(((f32[256,512]{1,0:T(8,128)}), f32[256,256]{1,0:T(8,128)}) %reduce-scatter.2.cloned.1.call-update) | async-done | bytes 262160 | tf_op jit(solution)/shard_map/reduce_scatter | solution.py:317
  110.9 1.6 %convert_element_type.45 = bf16[256,256]{1,0:T(8,128)(2,1)} convert(f32[256,256]{1,0:T(8,128)} %reduce-scatter.2.cloned.1.call-done) | non-fusion elementwise | flops 65536 | bytes 393216 | tf_op jit(solution)/shard_map/convert_element_type | solution.py:317
  112.5 30.9 %all-to-all-done.1 = bf16[128,10,512]{2,1,0:T(8,128)(2,1)} async-done(((bf16[128,10,512]{2,1,0:T(8,128)(2,1)}), bf16[128,10,512]{2,1,0:T(8,128)(2,1)}, u32[]{:S(2)}, u32[]{:S(2)}) %all-to-all-start.1) | async-done | bytes 1310752 | tf_op jit(solution)/shard_map/all_to_all | solution.py:307
  143.4 1.5 convert_reduce_fusion
  145.5 2.5 %collective-permute-done.2 = bf16[256,512]{1,0:T(8,128)(2,1)} collective-permute-done((bf16[256,512]{1,0:T(8,128)(2,1)S(1)}, bf16[256,512]{1,0:T(8,128)(2,1)}, u32[]{:S(2)}, u32[]{:S(2)}) %collective-permute-start.2) | collective-permute-done | bytes 262176 | tf_op jit(solution)/shard_map/ppermute | solution.py:32
  148.0 1.7 %fusion.15 = bf16[256,512]{1,0:T(8,128)(2,1)S(1)} fusion(f32[2,128,512]{2,1,0:T(8,128)S(1)} %slice.58, bf16[256,512]{1,0:T(8,128)(2,1)S(1)} %collective-permute-done.3, bf16[256,512]{1,0:T(8,128)(2,1)} %collective-permute-done.2, bf16[128,10,512]{2,1,0:T(8,128)(2,1)} %all-to-all-done.1, s32[1024]{0:T(1024)S(1)} %eq.60), kind=kOutput, calls=%fused_computation.29 | convolution fusion | flops 269484032 | bytes 2363392 | tf_op jit(solution)/shard_map/dot_general | solution.py:313
  (34 shorter events, 6.4 us)
Async XLA Ops:
  7.2 31.7 %copy-start = (bf16[256,512]{1,0:T(8,128)(2,1)S(1)}, bf16[256,512]{1,0:T(8,128)(2,1)}, u32[]{:S(2)}) copy-start(bf16[256,512]{1,0:T(8,128)(2,1)} %param.21) | copy-start | bytes 786436
  7.2 29.1 %copy-start.6 = (s32[2,4]{1,0:T(2,128)S(1)}, s32[2,4]{1,0:T(2,128)}, u32[]{:S(2)}) copy-start(s32[2,4]{1,0:T(2,128)} %param.24) | copy-start | bytes 100
  7.2 29.1 %copy-start.4 = (bf16[256,256]{1,0:T(8,128)(2,1)S(1)}, bf16[256,256]{1,0:T(8,128)(2,1)}, u32[]{:S(2)}) copy-start(bf16[256,256]{1,0:T(8,128)(2,1)} %param.22) | copy-start | bytes 393220
  9.0 29.9 %copy-start.5 = (s32[256,3]{0,1:T(4,128)S(1)}, s32[256,3]{0,1:T(4,128)}, u32[]{:S(2)}) copy-start(s32[256,3]{0,1:T(4,128)} %param.27) | copy-start | bytes 9220
  11.4 49.5 %all-to-all-start = ((bf16[128,8,512]{2,1,0:T(8,128)(2,1)}), bf16[128,8,512]{2,1,0:T(8,128)(2,1)S(1)}, u32[]{:S(2)}, u32[]{:S(2)}) async-start(bf16[128,8,512]{2,1,0:T(8,128)(2,1)} %fusion.8), calls=%async_computation | async-start | bytes 2097152 | tf_op jit(solution)/shard_map/all_to_all | solution.py:262
  27.4 27.1 %collective-permute-start.1 = (bf16[256,512]{1,0:T(8,128)(2,1)S(1)}, bf16[256,512]{1,0:T(8,128)(2,1)S(1)}, u32[]{:S(2)}, u32[]{:S(2)}) collective-permute-start(bf16[256,512]{1,0:T(8,128)(2,1)S(1)} %constant_dynamic-update-slice_fusion), channel_id=1, source_target_pairs={{2,0},{4,2},{6,4},{8,6},{10,8},{12,10},{14,12},{16,14},{18,16},{20... | collective-permute-start | bytes 786440 | tf_op jit(solution)/shard_map/ppermute | solution.py:24
  34.3 25.6 %collective-permute-start = (bf16[256,512]{1,0:T(8,128)(2,1)S(1)}, bf16[256,512]{1,0:T(8,128)(2,1)S(1)}, u32[]{:S(2)}, u32[]{:S(2)}) collective-permute-start(bf16[256,512]{1,0:T(8,128)(2,1)S(1)} %constant_dynamic-update-slice_fusion), channel_id=1, source_target_pairs={{0,2},{2,4},{4,6},{6,8},{8,10},{10,12},{12,14},{14,16},{16,18},{18... | collective-permute-start | bytes 786440 | tf_op jit(solution)/shard_map/ppermute | solution.py:23
  78.3 1.6 %copy-start.2 = (f32[3,256,512]{2,1,0:T(8,128)S(1)}, f32[3,256,512]{2,1,0:T(8,128)}, u32[]{:S(2)}) copy-start(f32[3,256,512]{2,1,0:T(8,128)} %get-tuple-element.52) | copy-start | bytes 4718596
  83.9 9.7 %copy-start.3 = (bf16[256,256]{1,0:T(8,128)(2,1)S(1)}, bf16[256,256]{1,0:T(8,128)(2,1)}, u32[]{:S(2)}) copy-start(bf16[256,256]{1,0:T(8,128)(2,1)} %get-tuple-element.49) | copy-start | bytes 393220
  83.9 10.8 %copy-start.1 = (f32[6,128,512]{2,1,0:T(8,128)S(1)}, f32[6,128,512]{2,1,0:T(8,128)}, u32[]{:S(2)}) copy-start(f32[6,128,512]{2,1,0:T(8,128)} %get-tuple-element.51) | copy-start | bytes 4718596
  83.9 59.5 %all-to-all-start.1 = ((bf16[128,10,512]{2,1,0:T(8,128)(2,1)}), bf16[128,10,512]{2,1,0:T(8,128)(2,1)}, u32[]{:S(2)}, u32[]{:S(2)}) async-start(bf16[128,10,512]{2,1,0:T(8,128)(2,1)} %pad_maximum_fusion), calls=%async_computation.2 | async-start | bytes 4194304 | tf_op jit(solution)/shard_map/all_to_all | solution.py:307
  93.5 17.3 %reduce-scatter.2.cloned.1.call-start = ((), (), s32[]{:S(2)}) async-start(), calls=%async_computation.3 | async-start | bytes 786432 | tf_op jit(solution)/shard_map/reduce_scatter | solution.py:317
  94.8 50.7 %collective-permute-start.3 = (bf16[256,512]{1,0:T(8,128)(2,1)S(1)}, bf16[256,512]{1,0:T(8,128)(2,1)S(1)}, u32[]{:S(2)}, u32[]{:S(2)}) collective-permute-start(bf16[256,512]{1,0:T(8,128)(2,1)S(1)} %bitcast.42), channel_id=1, source_target_pairs={{2,0},{4,2},{6,4},{8,6},{10,8},{12,10},{14,12},{16,14},{18,16},{20... | collective-permute-start | bytes 786440 | tf_op jit(solution)/shard_map/ppermute | solution.py:32
  101.8 46.2 %collective-permute-start.2 = (bf16[256,512]{1,0:T(8,128)(2,1)S(1)}, bf16[256,512]{1,0:T(8,128)(2,1)}, u32[]{:S(2)}, u32[]{:S(2)}) collective-permute-start(bf16[256,512]{1,0:T(8,128)(2,1)S(1)} %bitcast.41), channel_id=1, source_target_pairs={{0,2},{2,4},{4,6},{6,8},{8,10},{10,12},{12,14},{14,16},{16,18},{18... | collective-permute-start | bytes 786440 | tf_op jit(solution)/shard_map/ppermute | solution.py:32
Sparse Core Ops, SparseCore 0:
  96.8 13.9 reduce-scatter.1

commit v4 on v3

--- a/solution.py
+++ b/solution.py
@@ -125,17 +125,21 @@
     )
 
 
-def _attn_kernel(heads, kt, pos_ref, cnt_ref, bias_ref, q_ref, do_ref, ext_ref, far_ref,
-                 attn_ref, qg_ref, eg_ref, fg_ref, attn_acc, qg_acc):
+def _attn_kernel(heads, kt, near_out, pos_ref, cnt_ref, bias_ref, q_ref, do_ref, ext_ref, far_ref, *refs):
+    if near_out:
+        qg_ref, eg_ref, acc = refs
+    else:
+        attn_ref, fg_ref, acc = refs
     cols = q_ref.shape[1]
     hs = cols // heads
     scale = hs ** (-0.5)
     n_tiles = q_ref.shape[0] // TILE
     f32, bf16 = jnp.float32, jnp.bfloat16
-    eg_ref[...] = jnp.zeros(eg_ref.shape, f32)
-    fg_ref[...] = jnp.zeros(fg_ref.shape, f32)
-    attn_acc[...] = jnp.zeros(attn_acc.shape, f32)
-    qg_acc[...] = jnp.zeros(qg_acc.shape, f32)
+    if near_out:
+        eg_ref[...] = jnp.zeros(eg_ref.shape, f32)
+    else:
+        fg_ref[...] = jnp.zeros(fg_ref.shape, f32)
+    acc[...] = jnp.zeros(acc.shape, f32)
     lane = lax.broadcasted_iota(jnp.int32, (TILE, cols), 1)
     nt = (((1,), (1,)), ((), ()))
     tn = (((0,), (0,)), ((), ()))
@@ -178,8 +182,16 @@
             for e in range(DEG):
                 mixed = mixed + fe[e].astype(bf16).astype(f32) * fv[e]
             attn = (mixed / row_sum).astype(bf16).astype(f32)
-            attn_acc[rows, :] += jnp.where(mask, attn, 0.0)
             delta = jnp.sum(jnp.where(mask, dof * attn, 0.0), axis=1, keepdims=True)
+            if not near_out:
+                acc[rows, :] += jnp.where(mask, attn, 0.0)
+                for e in range(DEG):
+                    fdp = jnp.sum(jnp.where(mask, dof * fv[e], 0.0), axis=1, keepdims=True)
+                    fpr = fe[e] / row_sum
+                    fds = (fpr * (fdp - delta)).astype(bf16).astype(f32)
+                    fg_ref[e, rows, :cols] += jnp.where(mask, fds * qf * scale, 0.0)
+                    fg_ref[e, rows, cols:] += jnp.where(mask, fpr.astype(bf16).astype(f32) * dof, 0.0)
+                return carry
             qg = None
             for j in range(kt):
                 ndp = lax.dot_general(doh, vals[j], nt, preferred_element_type=f32)
@@ -196,34 +208,32 @@
                 fpr = fe[e] / row_sum
                 fds = (fpr * (fdp - delta)).astype(bf16).astype(f32)
                 qg = qg + fds * fk[e]
-                fg_ref[e, rows, :cols] += jnp.where(mask, fds * qf * scale, 0.0)
-                fg_ref[e, rows, cols:] += jnp.where(mask, fpr.astype(bf16).astype(f32) * dof, 0.0)
-            qg_acc[rows, :] += jnp.where(mask, qg * scale, 0.0)
+            acc[rows, :] += jnp.where(mask, qg * scale, 0.0)
             return carry
 
         lax.fori_loop(0, heads, head_body, 0)
-        attn_ref[rows, :] = attn_acc[rows, :].astype(attn_ref.dtype)
-        qg_ref[rows, :] = qg_acc[rows, :].astype(qg_ref.dtype)
-
-
-def attention_tiles(pos, cnt, bias, q, do, ext, far):
+        out_ref = qg_ref if near_out else attn_ref
+        out_ref[rows, :] = acc[rows, :].astype(out_ref.dtype)
+
+
+def attention_tiles(near_out, pos, cnt, bias, q, do, ext, far):
     heads = bias.shape[0]
     kt = pos.shape[0] // cnt.shape[0]
     n, cols = q.shape
     smem = pl.BlockSpec(memory_space=pltpu.SMEM)
     vmem = pl.BlockSpec(memory_space=pltpu.VMEM)
+    grads = jax.ShapeDtypeStruct(ext.shape if near_out else far.shape, jnp.float32)
     return pl.pallas_call(
-        functools.partial(_attn_kernel, heads, kt),
-        out_shape=(
-            jax.ShapeDtypeStruct((n, cols), jnp.bfloat16),
-            jax.ShapeDtypeStruct((n, cols), jnp.bfloat16),
-            jax.ShapeDtypeStruct(ext.shape, jnp.float32),
-            jax.ShapeDtypeStruct(far.shape, jnp.float32),
+        functools.partial(_attn_kernel, heads, kt, near_out),
+        out_shape=(jax.ShapeDtypeStruct((n, cols), jnp.bfloat16), grads),
+        in_specs=[smem, smem, smem, vmem, vmem, vmem, vmem],
+        out_specs=(vmem, vmem),
+        scratch_shapes=[pltpu.VMEM((n, cols), jnp.float32)],
+        cost_estimate=pl.CostEstimate(
+            flops=int(2 * n * kt * TILE * cols * (6 if near_out else 3) * heads),
+            bytes_accessed=int(4 * 1024 * 1024),
+            transcendentals=int(n * heads * (kt * TILE + DEG)),
         ),
-        in_specs=[smem, smem, smem, vmem, vmem, vmem, vmem],
-        out_specs=(vmem, vmem, vmem, vmem),
-        scratch_shapes=[pltpu.VMEM((n, cols), jnp.float32), pltpu.VMEM((n, cols), jnp.float32)],
-        cost_estimate=pl.CostEstimate(flops=int(2 * n * kt * TILE * cols * 6), bytes_accessed=int(8 * 1024 * 1024), transcendentals=int(n * heads * (kt * TILE + DEG))),
     )(pos, cnt, bias, q, do, ext, far)
 
 
@@ -271,7 +281,7 @@
         .reshape(DEG, node_count, -1)
     )
     base_tile = dom_index * per_part - HALO
-    attn_all, qgrad_all, ext_grad, far_grad = attention_tiles(
+    kernel_args = (
         (tile_list - base_tile).reshape(-1),
         tile_count,
         far_bias,
@@ -280,6 +290,8 @@
         ext_tiles,
         far_all,
     )
+    attn_all, far_grad = attention_tiles(False, *kernel_args)
+    qgrad_all, ext_grad = attention_tiles(True, *kernel_args)
     ext_grad = ext_grad.reshape(-1, 2 * col_width)
     attn_mine = attn_all.reshape(node_count, col_width)
     low_part = ext_grad[:rim_rows]

time: 158 us -> 151 us (0.956)
  waiting for transfers between devices: 60.7 us -> 45 us
  Pallas kernels: 15.5 us -> 23.5 us
    all_to_all x1, waiting for transfers between devices: 30.9 us -> 21 us  [shards(): lax.all_to_all(both, 'dom', split_axis=0, concat_axis=0, tiled=True)]
    pallas_call x1 -> x2, Pallas kernels: 15.5 us -> 23.5 us  [attention_tiles(): pl.pallas_call(functools.partial(_attn_kernel, heads, kt, near_out), out_...]
    reduce_scatter x1, waiting for transfers between devices: 7.08 us -> 0.02 us  [shards(): lax.psum_scatter(partial_out, 'head', scatter_dimension=1, tiled=True)]
  transfers between devices with their start and end apart: 7 -> 7, of which waited for: 5 -> 4; matrix products, arithmetic and copies ran while one was open for 5% -> 6% of each run, Pallas kernels for 0% -> 10%
where the time goes in v4:
time: 151 us; the launch traced here: 150 us
  waiting for transfers between devices  45 us (30%)
  starting transfers between devices  43 us (28%)
  Pallas kernels  23.5 us (16%)
  between operations  14.2 us (9%)
  matrix products  10.1 us (7%)
  other arithmetic  6.37 us (4%)
  local copies, waits for them, and re-layouts  6.13 us (4%)
  blocking collectives  1.99 us (1%)
    pallas_call x2, Pallas kernels, attention_tiles(): pl.pallas_call(functools.partial(_attn_kernel, heads, kt, near_out), out_...  23.5 us
    all_to_all x1, waiting for transfers between devices, shards(): lax.all_to_all(both, 'dom', split_axis=0, concat_axis=0, tiled=True)  21 us
    all_to_all x1, starting transfers between devices, shards(): lax.all_to_all(outgoing, 'dom', split_axis=0, concat_axis=0, tiled=True)  15.9 us
    ppermute x1, waiting for transfers between devices, extended_2(): after = lax.ppermute(leading, axis, down)  14.6 us
    all_to_all x1, starting transfers between devices, shards(): lax.all_to_all(both, 'dom', split_axis=0, concat_axis=0, tiled=True)  9.14 us
    ppermute x2, starting transfers between devices, from_behind(): lax.ppermute(value, axis, [(source, source + steps) for source in range(l...  8.87 us
    ppermute x1, starting transfers between devices, extended_2(): after = lax.ppermute(leading, axis, down)  6.98 us
    ppermute x1, waiting for transfers between devices, extended_2(): before = lax.ppermute(last, axis, up)  5.53 us
  transfers between devices with their start and end apart: 7, of which 4 were waited for; matrix products, arithmetic and copies ran while one was open for 6% of the time, Pallas kernels for 10%

profile of v4, /device:TPU:6, one launch (start us, length us, event | category | flops | bytes accessed | tf_op | source)
XLA Modules:
  0.0 150.4 jit_solution(1106451903223779268)
XLA Ops:
  10.0 1.5 fusion.8
  11.4 15.9 %all-to-all-start = ((bf16[128,8,512]{2,1,0:T(8,128)(2,1)}), bf16[128,8,512]{2,1,0:T(8,128)(2,1)S(1)}, u32[]{:S(2)}, u32[]{:S(2)}) async-start(bf16[128,8,512]{2,1,0:T(8,128)(2,1)} %fusion.8), calls=%async_computation | async-start | bytes 2097152 | tf_op jit(solution)/shard_map/all_to_all | solution.py:272
  27.4 7.0 %collective-permute-start.1 = (bf16[256,512]{1,0:T(8,128)(2,1)S(1)}, bf16[256,512]{1,0:T(8,128)(2,1)S(1)}, u32[]{:S(2)}, u32[]{:S(2)}) collective-permute-start(bf16[256,512]{1,0:T(8,128)(2,1)S(1)} %constant_dynamic-update-slice_fusion), channel_id=1, source_target_pairs={{2,0},{4,2},{6,4},{8,6},{10,8},{12,10},{14,12},{16,14},{18,16},{20... | collective-permute-start | bytes 786440 | tf_op jit(solution)/shard_map/ppermute | solution.py:24
  34.3 1.9 %collective-permute-start = (bf16[256,512]{1,0:T(8,128)(2,1)S(1)}, bf16[256,512]{1,0:T(8,128)(2,1)S(1)}, u32[]{:S(2)}, u32[]{:S(2)}) collective-permute-start(bf16[256,512]{1,0:T(8,128)(2,1)S(1)} %constant_dynamic-update-slice_fusion), channel_id=1, source_target_pairs={{0,2},{2,4},{4,6},{6,8},{8,10},{10,12},{12,14},{14,16},{16,18},{18... | collective-permute-start | bytes 786440 | tf_op jit(solution)/shard_map/ppermute | solution.py:23
  36.3 2.0 %all_gather.3 = bf16[256,512]{1,0:T(8,128)(2,1)S(1)} all-gather(bf16[256,256]{1,0:T(8,128)(2,1)S(1)} %copy-done.3), channel_id=1, replica_groups=mesh['dom'=128,'head'=2] {'head'}, dimensions={1}, use_global_device_ids=true | all-gather | bytes 393216 | tf_op jit(solution)/shard_map/all_gather | solution.py:256
  39.8 14.6 %collective-permute-done.1 = bf16[256,512]{1,0:T(8,128)(2,1)S(1)} collective-permute-done((bf16[256,512]{1,0:T(8,128)(2,1)S(1)}, bf16[256,512]{1,0:T(8,128)(2,1)S(1)}, u32[]{:S(2)}, u32[]{:S(2)}) %collective-permute-start.1) | collective-permute-done | bytes 262176 | tf_op jit(solution)/shard_map/ppermute | solution.py:24
  54.5 5.5 %collective-permute-done = bf16[256,512]{1,0:T(8,128)(2,1)S(1)} collective-permute-done((bf16[256,512]{1,0:T(8,128)(2,1)S(1)}, bf16[256,512]{1,0:T(8,128)(2,1)S(1)}, u32[]{:S(2)}, u32[]{:S(2)}) %collective-permute-start) | collective-permute-done | bytes 262176 | tf_op jit(solution)/shard_map/ppermute | solution.py:23
  60.9 1.9 %fusion.7 = bf16[768,512]{1,0:T(8,128)(2,1)} fusion(s32[768]{0:T(1024)S(1)} %eq.56, bf16[128,8,512]{2,1,0:T(8,128)(2,1)S(1)} %all-to-all-done), kind=kOutput, calls=%fused_computation.14 | convolution fusion | flops 806486016 | bytes 1838080 | tf_op jit(solution)/shard_map/dot_general | solution.py:279
  62.9 8.8 %shard_map.147 = (bf16[256,256]{1,0:T(8,128)(2,1)}, f32[3,256,512]{2,1,0:T(8,128)}) custom-call(s32[8]{0:T(128)} %reshape.102.pos_ref, s32[2]{0:T(128)} %cnt_ref.3, f32[4]{0:T(128)} %bias_ref.3, bf16[256,256]{1,0:T(8,128)(2,1)} %q_ref.3, bf16[256,256]{1,0:T(8,128)(2,1)} %convolution_convert_fusion.2.do_ref, bf16[6,128,512]{2,1,0:T(8,128)(2,1)} %bitcast.39, ...), custom_call_target="tpu_custom_call" | custom-call | flops 805306368 | bytes 4194304 | tf_op jit(solution)/shard_map/pallas_call | solution.py:226
  71.6 1.3 fusion.10
  73.5 1.0 fusion
  74.5 1.0 fusion.9
  75.4 1.8 %pad_maximum_fusion = bf16[128,10,512]{2,1,0:T(8,128)(2,1)} fusion(bf16[128,2,512]{2,1,0:T(2,128)(2,1)S(1)} %reshape.109, bf16[128,8,512]{2,1,0:T(8,128)(2,1)S(1)} %fusion.9), kind=kLoop, calls=%fused_computation.7 | loop fusion | flops 2621440 | bytes 2621440 | tf_op jit(solution)/shard_map/concatenate | solution.py:316
  77.2 9.1 %all-to-all-start.1 = ((bf16[128,10,512]{2,1,0:T(8,128)(2,1)}), bf16[128,10,512]{2,1,0:T(8,128)(2,1)S(1)}, u32[]{:S(2)}, u32[]{:S(2)}) async-start(bf16[128,10,512]{2,1,0:T(8,128)(2,1)} %pad_maximum_fusion), calls=%async_computation.2 | async-start | bytes 4194304 | tf_op jit(solution)/shard_map/all_to_all | solution.py:319
  86.6 1.1 fusion.20
  87.7 14.7 %shard_map.148 = (bf16[256,256]{1,0:T(8,128)(2,1)}, f32[6,128,512]{2,1,0:T(8,128)}) custom-call(s32[8]{0:T(128)} %reshape.102.pos_ref, s32[2]{0:T(128)} %cnt_ref.3, f32[4]{0:T(128)} %bias_ref.3, bf16[256,256]{1,0:T(8,128)(2,1)} %q_ref.3, bf16[256,256]{1,0:T(8,128)(2,1)} %convolution_convert_fusion.2.do_ref, bf16[6,128,512]{2,1,0:T(8,128)(2,1)} %bitcast.40, ...), custom_call_target="tpu_custom_call" | custom-call | flops 1610612736 | bytes 4194304 | tf_op jit(solution)/shard_map/pallas_call | solution.py:226
  102.4 1.6 %convert.17 = bf16[6,128,512]{2,1,0:T(8,128)(2,1)S(1)} convert(f32[6,128,512]{2,1,0:T(8,128)} %get-tuple-element.51) | non-fusion elementwise | flops 393216 | bytes 2359296 | tf_op jit(solution)/shard_map/convert.8
  104.0 6.9 %collective-permute-start.3 = (bf16[256,512]{1,0:T(8,128)(2,1)S(1)}, bf16[256,512]{1,0:T(8,128)(2,1)}, u32[]{:S(2)}, u32[]{:S(2)}) collective-permute-start(bf16[256,512]{1,0:T(8,128)(2,1)S(1)} %bitcast.42), channel_id=1, source_target_pairs={{2,0},{4,2},{6,4},{8,6},{10,8},{12,10},{14,12},{16,14},{18,16},{20... | collective-permute-start | bytes 786440 | tf_op jit(solution)/shard_map/ppermute | solution.py:32
  110.9 1.9 %collective-permute-start.2 = (bf16[256,512]{1,0:T(8,128)(2,1)S(1)}, bf16[256,512]{1,0:T(8,128)(2,1)}, u32[]{:S(2)}, u32[]{:S(2)}) collective-permute-start(bf16[256,512]{1,0:T(8,128)(2,1)S(1)} %bitcast.41), channel_id=1, source_target_pairs={{0,2},{2,4},{4,6},{6,8},{8,10},{10,12},{12,14},{14,16},{16,18},{18... | collective-permute-start | bytes 786440 | tf_op jit(solution)/shard_map/ppermute | solution.py:32
  112.9 1.1 slice.58
  114.0 1.6 %convert_element_type.45 = bf16[256,256]{1,0:T(8,128)(2,1)} convert(f32[256,256]{1,0:T(8,128)} %reduce-scatter.2.cloned.1.call-done) | non-fusion elementwise | flops 65536 | bytes 393216 | tf_op jit(solution)/shard_map/convert_element_type | solution.py:329
  115.6 21.0 %all-to-all-done.1 = bf16[128,10,512]{2,1,0:T(8,128)(2,1)S(1)} async-done(((bf16[128,10,512]{2,1,0:T(8,128)(2,1)}), bf16[128,10,512]{2,1,0:T(8,128)(2,1)S(1)}, u32[]{:S(2)}, u32[]{:S(2)}) %all-to-all-start.1) | async-done | bytes 1310752 | tf_op jit(solution)/shard_map/all_to_all | solution.py:319
  137.5 3.8 %collective-permute-done.2 = bf16[256,512]{1,0:T(8,128)(2,1)} collective-permute-done((bf16[256,512]{1,0:T(8,128)(2,1)S(1)}, bf16[256,512]{1,0:T(8,128)(2,1)}, u32[]{:S(2)}, u32[]{:S(2)}) %collective-permute-start.2) | collective-permute-done | bytes 262176 | tf_op jit(solution)/shard_map/ppermute | solution.py:32
  141.3 1.5 fusion.15
  (33 shorter events, 7.7 us)
Async XLA Ops:
  7.2 31.7 %copy-start = (bf16[256,512]{1,0:T(8,128)(2,1)S(1)}, bf16[256,512]{1,0:T(8,128)(2,1)}, u32[]{:S(2)}) copy-start(bf16[256,512]{1,0:T(8,128)(2,1)} %param.21) | copy-start | bytes 786436
  7.2 29.1 %copy-start.5 = (s32[2,4]{1,0:T(2,128)S(1)}, s32[2,4]{1,0:T(2,128)}, u32[]{:S(2)}) copy-start(s32[2,4]{1,0:T(2,128)} %param.24) | copy-start | bytes 100
  7.2 29.1 %copy-start.3 = (bf16[256,256]{1,0:T(8,128)(2,1)S(1)}, bf16[256,256]{1,0:T(8,128)(2,1)}, u32[]{:S(2)}) copy-start(bf16[256,256]{1,0:T(8,128)(2,1)} %param.22) | copy-start | bytes 393220
  9.0 29.9 %copy-start.4 = (s32[256,3]{0,1:T(4,128)S(1)}, s32[256,3]{0,1:T(4,128)}, u32[]{:S(2)}) copy-start(s32[256,3]{0,1:T(4,128)} %param.27) | copy-start | bytes 9220
  11.4 49.5 %all-to-all-start = ((bf16[128,8,512]{2,1,0:T(8,128)(2,1)}), bf16[128,8,512]{2,1,0:T(8,128)(2,1)S(1)}, u32[]{:S(2)}, u32[]{:S(2)}) async-start(bf16[128,8,512]{2,1,0:T(8,128)(2,1)} %fusion.8), calls=%async_computation | async-start | bytes 2097152 | tf_op jit(solution)/shard_map/all_to_all | solution.py:272
  27.4 27.1 %collective-permute-start.1 = (bf16[256,512]{1,0:T(8,128)(2,1)S(1)}, bf16[256,512]{1,0:T(8,128)(2,1)S(1)}, u32[]{:S(2)}, u32[]{:S(2)}) collective-permute-start(bf16[256,512]{1,0:T(8,128)(2,1)S(1)} %constant_dynamic-update-slice_fusion), channel_id=1, source_target_pairs={{2,0},{4,2},{6,4},{8,6},{10,8},{12,10},{14,12},{16,14},{18,16},{20... | collective-permute-start | bytes 786440 | tf_op jit(solution)/shard_map/ppermute | solution.py:24
  34.3 25.6 %collective-permute-start = (bf16[256,512]{1,0:T(8,128)(2,1)S(1)}, bf16[256,512]{1,0:T(8,128)(2,1)S(1)}, u32[]{:S(2)}, u32[]{:S(2)}) collective-permute-start(bf16[256,512]{1,0:T(8,128)(2,1)S(1)} %constant_dynamic-update-slice_fusion), channel_id=1, source_target_pairs={{0,2},{2,4},{4,6},{6,8},{8,10},{10,12},{12,14},{14,16},{16,18},{18... | collective-permute-start | bytes 786440 | tf_op jit(solution)/shard_map/ppermute | solution.py:23
  71.6 1.6 %copy-start.1 = (f32[3,256,512]{2,1,0:T(8,128)S(1)}, f32[3,256,512]{2,1,0:T(8,128)}, u32[]{:S(2)}) copy-start(f32[3,256,512]{2,1,0:T(8,128)} %get-tuple-element.52) | copy-start | bytes 4718596
  77.2 9.4 %copy-start.2 = (bf16[256,256]{1,0:T(8,128)(2,1)S(1)}, bf16[256,256]{1,0:T(8,128)(2,1)}, u32[]{:S(2)}) copy-start(bf16[256,256]{1,0:T(8,128)(2,1)} %get-tuple-element.49) | copy-start | bytes 393220
  77.2 59.4 %all-to-all-start.1 = ((bf16[128,10,512]{2,1,0:T(8,128)(2,1)}), bf16[128,10,512]{2,1,0:T(8,128)(2,1)S(1)}, u32[]{:S(2)}, u32[]{:S(2)}) async-start(bf16[128,10,512]{2,1,0:T(8,128)(2,1)} %pad_maximum_fusion), calls=%async_computation.2 | async-start | bytes 4194304 | tf_op jit(solution)/shard_map/all_to_all | solution.py:319
  86.4 27.6 %reduce-scatter.2.cloned.1.call-start = ((), (), s32[]{:S(2)}) async-start(), calls=%async_computation.3 | async-start | bytes 786432 | tf_op jit(solution)/shard_map/reduce_scatter | solution.py:329
  104.0 33.5 %collective-permute-start.3 = (bf16[256,512]{1,0:T(8,128)(2,1)S(1)}, bf16[256,512]{1,0:T(8,128)(2,1)}, u32[]{:S(2)}, u32[]{:S(2)}) collective-permute-start(bf16[256,512]{1,0:T(8,128)(2,1)S(1)} %bitcast.42), channel_id=1, source_target_pairs={{2,0},{4,2},{6,4},{8,6},{10,8},{12,10},{14,12},{16,14},{18,16},{20... | collective-permute-start | bytes 786440 | tf_op jit(solution)/shard_map/ppermute | solution.py:32
  110.9 30.4 %collective-permute-start.2 = (bf16[256,512]{1,0:T(8,128)(2,1)S(1)}, bf16[256,512]{1,0:T(8,128)(2,1)}, u32[]{:S(2)}, u32[]{:S(2)}) collective-permute-start(bf16[256,512]{1,0:T(8,128)(2,1)S(1)} %bitcast.41), channel_id=1, source_target_pairs={{0,2},{2,4},{4,6},{6,8},{8,10},{10,12},{12,14},{14,16},{16,18},{18... | collective-permute-start | bytes 786440 | tf_op jit(solution)/shard_map/ppermute | solution.py:32
Sparse Core Ops, SparseCore 0:
  89.7 13.9 reduce-scatter.1

commit v5 on v4

--- a/solution.py
+++ b/solution.py
@@ -326,9 +326,11 @@
     key_grad = own_grad[:, :col_width].astype(jnp.bfloat16)
     value_grad = own_grad[:, col_width:].astype(jnp.bfloat16)
     partial_out = jnp.dot(attn_mine, out_weight, preferred_element_type=jnp.float32)
-    layer_out = lax.psum_scatter(partial_out, "head", scatter_dimension=1, tiled=True).astype(
-        jnp.bfloat16
-    )
+    head_index = lax.axis_index("head")
+    other_cols = lax.dynamic_slice_in_dim(partial_out, (1 - head_index) * col_width, col_width, 1)
+    own_cols = lax.dynamic_slice_in_dim(partial_out, head_index * col_width, col_width, 1)
+    swapped = lax.ppermute(other_cols, "head", [(0, 1), (1, 0)])
+    layer_out = (own_cols + swapped).astype(jnp.bfloat16)
     out_weight_grad = weight_sum.reshape(-1, col_width)
     return (
         layer_out,

time: 151 us -> 138 us (0.914)
  between operations: 14.2 us -> 0.85 us
  local copies, waits for them, and re-layouts: 6.13 us -> 7.69 us
  transfers between devices with their start and end apart: 7 -> 7, of which waited for: 4 -> 4; matrix products, arithmetic and copies ran while one was open for 6% -> 7% of each run, Pallas kernels for 10% -> 11%
where the time goes in v5:
time: 138 us; the launch traced here: 137 us
  waiting for transfers between devices  44.5 us (32%)
  starting transfers between devices  42.8 us (31%)
  Pallas kernels  23.5 us (17%)
  matrix products  9.29 us (7%)
  local copies, waits for them, and re-layouts  7.69 us (6%)
  other arithmetic  6.36 us (5%)
  blocking collectives  1.99 us (1%)
    pallas_call x2, Pallas kernels, attention_tiles(): pl.pallas_call(functools.partial(_attn_kernel, heads, kt, near_out), out_...  23.5 us
    all_to_all x1, waiting for transfers between devices, shards(): lax.all_to_all(both, 'dom', split_axis=0, concat_axis=0, tiled=True)  20.6 us
    all_to_all x1, starting transfers between devices, shards(): lax.all_to_all(outgoing, 'dom', split_axis=0, concat_axis=0, tiled=True)  15.9 us
    ppermute x1, waiting for transfers between devices, extended_2(): after = lax.ppermute(leading, axis, down)  14.6 us
    all_to_all x1, starting transfers between devices, shards(): lax.all_to_all(both, 'dom', split_axis=0, concat_axis=0, tiled=True)  9.15 us
    ppermute x2, starting transfers between devices, from_behind(): lax.ppermute(value, axis, [(source, source + steps) for source in range(l...  8.88 us
    ppermute x1, starting transfers between devices, extended_2(): after = lax.ppermute(leading, axis, down)  6.98 us
    ppermute x1, waiting for transfers between devices, extended_2(): before = lax.ppermute(last, axis, up)  5.53 us
  transfers between devices with their start and end apart: 7, of which 4 were waited for; matrix products, arithmetic and copies ran while one was open for 7% of the time, Pallas kernels for 11%

profile of v5, /device:TPU:6, one launch (start us, length us, event | category | flops | bytes accessed | tf_op | source)
XLA Modules:
  0.0 137.0 jit_solution(40122718175072057)
XLA Ops:
  3.4 1.5 %fusion.8 = bf16[128,8,512]{2,1,0:T(8,128)(2,1)} fusion(bf16[256,512]{1,0:T(8,128)(2,1)S(1)} %constant_dynamic-update-slice_fusion, s32[1024]{0:T(1024)S(1)} %eq.60), kind=kOutput, calls=%fused_computation.15 | convolution fusion | flops 269221888 | bytes 1314816 | tf_op jit(solution)/shard_map/dot_general | solution.py:268
  4.9 15.9 %all-to-all-start = ((bf16[128,8,512]{2,1,0:T(8,128)(2,1)}), bf16[128,8,512]{2,1,0:T(8,128)(2,1)S(1)}, u32[]{:S(2)}, u32[]{:S(2)}) async-start(bf16[128,8,512]{2,1,0:T(8,128)(2,1)} %fusion.8), calls=%async_computation | async-start | bytes 2097152 | tf_op jit(solution)/shard_map/all_to_all | solution.py:272
  20.8 7.0 %collective-permute-start.1 = (bf16[256,512]{1,0:T(8,128)(2,1)S(1)}, bf16[256,512]{1,0:T(8,128)(2,1)S(1)}, u32[]{:S(2)}, u32[]{:S(2)}) collective-permute-start(bf16[256,512]{1,0:T(8,128)(2,1)S(1)} %constant_dynamic-update-slice_fusion), channel_id=1, source_target_pairs={{2,0},{4,2},{6,4},{8,6},{10,8},{12,10},{14,12},{16,14},{18,16},{20... | collective-permute-start | bytes 786440 | tf_op jit(solution)/shard_map/ppermute | solution.py:24
  27.8 1.9 %collective-permute-start = (bf16[256,512]{1,0:T(8,128)(2,1)S(1)}, bf16[256,512]{1,0:T(8,128)(2,1)S(1)}, u32[]{:S(2)}, u32[]{:S(2)}) collective-permute-start(bf16[256,512]{1,0:T(8,128)(2,1)S(1)} %constant_dynamic-update-slice_fusion), channel_id=1, source_target_pairs={{0,2},{2,4},{4,6},{6,8},{8,10},{10,12},{12,14},{14,16},{16,18},{18... | collective-permute-start | bytes 786440 | tf_op jit(solution)/shard_map/ppermute | solution.py:23
  29.8 2.0 %all_gather.3 = bf16[256,512]{1,0:T(8,128)(2,1)S(1)} all-gather(bf16[256,256]{1,0:T(8,128)(2,1)S(1)} %copy-done.3), channel_id=1, replica_groups=mesh['dom'=128,'head'=2] {'head'}, dimensions={1}, use_global_device_ids=true | all-gather | bytes 393216 | tf_op jit(solution)/shard_map/all_gather | solution.py:256
  33.3 14.6 %collective-permute-done.1 = bf16[256,512]{1,0:T(8,128)(2,1)S(1)} collective-permute-done((bf16[256,512]{1,0:T(8,128)(2,1)S(1)}, bf16[256,512]{1,0:T(8,128)(2,1)S(1)}, u32[]{:S(2)}, u32[]{:S(2)}) %collective-permute-start.1) | collective-permute-done | bytes 262176 | tf_op jit(solution)/shard_map/ppermute | solution.py:24
  47.9 5.5 %collective-permute-done = bf16[256,512]{1,0:T(8,128)(2,1)S(1)} collective-permute-done((bf16[256,512]{1,0:T(8,128)(2,1)S(1)}, bf16[256,512]{1,0:T(8,128)(2,1)S(1)}, u32[]{:S(2)}, u32[]{:S(2)}) %collective-permute-start) | collective-permute-done | bytes 262176 | tf_op jit(solution)/shard_map/ppermute | solution.py:23
  53.5 0.9 pad_maximum_fusion.1
  54.4 1.9 %fusion.7 = bf16[768,512]{1,0:T(8,128)(2,1)} fusion(s32[768]{0:T(1024)S(1)} %eq.56, bf16[128,8,512]{2,1,0:T(8,128)(2,1)S(1)} %all-to-all-done), kind=kOutput, calls=%fused_computation.14 | convolution fusion | flops 806486016 | bytes 1838080 | tf_op jit(solution)/shard_map/dot_general | solution.py:279
  56.3 8.8 %shard_map.147 = (bf16[256,256]{1,0:T(8,128)(2,1)}, f32[3,256,512]{2,1,0:T(8,128)}) custom-call(s32[8]{0:T(128)} %reshape.102.pos_ref, s32[2]{0:T(128)} %cnt_ref.3, f32[4]{0:T(128)} %bias_ref.3, bf16[256,256]{1,0:T(8,128)(2,1)} %q_ref.3, bf16[256,256]{1,0:T(8,128)(2,1)} %convolution_convert_fusion.2.do_ref, bf16[6,128,512]{2,1,0:T(8,128)(2,1)} %bitcast.39, ...), custom_call_target="tpu_custom_call" | custom-call | flops 805306368 | bytes 4194304 | tf_op jit(solution)/shard_map/pallas_call | solution.py:226
  65.1 1.3 fusion.10
  66.9 1.0 fusion
  67.9 1.0 fusion.9
  68.9 1.8 %pad_maximum_fusion = bf16[128,10,512]{2,1,0:T(8,128)(2,1)} fusion(bf16[128,2,512]{2,1,0:T(2,128)(2,1)S(1)} %reshape.109, bf16[128,8,512]{2,1,0:T(8,128)(2,1)S(1)} %fusion.9), kind=kLoop, calls=%fused_computation.7 | loop fusion | flops 2621440 | bytes 2621440 | tf_op jit(solution)/shard_map/concatenate | solution.py:316
  70.7 9.1 %all-to-all-start.1 = ((bf16[128,10,512]{2,1,0:T(8,128)(2,1)}), bf16[128,10,512]{2,1,0:T(8,128)(2,1)S(1)}, u32[]{:S(2)}, u32[]{:S(2)}) async-start(bf16[128,10,512]{2,1,0:T(8,128)(2,1)} %pad_maximum_fusion), calls=%async_computation.1 | async-start | bytes 4194304 | tf_op jit(solution)/shard_map/all_to_all | solution.py:319
  80.9 14.7 %shard_map.148 = (bf16[256,256]{1,0:T(8,128)(2,1)}, f32[6,128,512]{2,1,0:T(8,128)}) custom-call(s32[8]{0:T(128)} %reshape.102.pos_ref, s32[2]{0:T(128)} %cnt_ref.3, f32[4]{0:T(128)} %bias_ref.3, bf16[256,256]{1,0:T(8,128)(2,1)} %q_ref.3, bf16[256,256]{1,0:T(8,128)(2,1)} %convolution_convert_fusion.2.do_ref, bf16[6,128,512]{2,1,0:T(8,128)(2,1)} %bitcast.40, ...), custom_call_target="tpu_custom_call" | custom-call | flops 1610612736 | bytes 4194304 | tf_op jit(solution)/shard_map/pallas_call | solution.py:226
  95.5 1.1 slice.58
  96.6 1.5 %convert.17 = bf16[6,128,512]{2,1,0:T(8,128)(2,1)S(1)} convert(f32[6,128,512]{2,1,0:T(8,128)} %get-tuple-element.51) | non-fusion elementwise | flops 393216 | bytes 2359296 | tf_op jit(solution)/shard_map/convert.8
  99.0 7.0 %collective-permute-start.4 = (bf16[256,512]{1,0:T(8,128)(2,1)}, bf16[256,512]{1,0:T(8,128)(2,1)}, u32[]{:S(2)}, u32[]{:S(2)}) collective-permute-start(bf16[256,512]{1,0:T(8,128)(2,1)} %bitcast.7), channel_id=1, source_target_pairs={{2,0},{4,2},{6,4},{8,6},{10,8},{12,10},{14,12},{16,14},{18,16},{20... | collective-permute-start | bytes 786440 | tf_op jit(solution)/shard_map/ppermute | solution.py:32
  105.9 1.9 %collective-permute-start.3 = (bf16[256,512]{1,0:T(8,128)(2,1)}, bf16[256,512]{1,0:T(8,128)(2,1)}, u32[]{:S(2)}, u32[]{:S(2)}) collective-permute-start(bf16[256,512]{1,0:T(8,128)(2,1)} %bitcast.6), channel_id=1, source_target_pairs={{0,2},{2,4},{4,6},{6,8},{8,10},{10,12},{12,14},{14,16},{16,18},{18... | collective-permute-start | bytes 786440 | tf_op jit(solution)/shard_map/ppermute | solution.py:32
  107.9 1.6 %add_convert_fusion.1 = bf16[256,256]{1,0:T(8,128)(2,1)} fusion(f32[256,256]{1,0:T(8,128)} %collective-permute-done.2, f32[256,512]{1,0:T(8,128)S(1)} %fusion.20, s32[]{:T(128)S(6)} %select_n.6), kind=kLoop, calls=%fused_computation.33 | loop fusion | flops 131072 | bytes 655364 | tf_op jit(solution)/shard_map/convert_element_type | solution.py:333
  109.5 20.6 %all-to-all-done.1 = bf16[128,10,512]{2,1,0:T(8,128)(2,1)S(1)} async-done(((bf16[128,10,512]{2,1,0:T(8,128)(2,1)}), bf16[128,10,512]{2,1,0:T(8,128)(2,1)S(1)}, u32[]{:S(2)}, u32[]{:S(2)}) %all-to-all-start.1) | async-done | bytes 1310752 | tf_op jit(solution)/shard_map/all_to_all | solution.py:319
  131.0 3.8 %collective-permute-done.3 = bf16[256,512]{1,0:T(8,128)(2,1)} collective-permute-done((bf16[256,512]{1,0:T(8,128)(2,1)}, bf16[256,512]{1,0:T(8,128)(2,1)}, u32[]{:S(2)}, u32[]{:S(2)}) %collective-permute-start.3) | collective-permute-done | bytes 262176 | tf_op jit(solution)/shard_map/ppermute | solution.py:32
  134.8 1.5 %fusion.15 = bf16[256,512]{1,0:T(8,128)(2,1)S(1)} fusion(f32[2,128,512]{2,1,0:T(8,128)S(1)} %slice.58, bf16[256,512]{1,0:T(8,128)(2,1)} %collective-permute-done.4, bf16[256,512]{1,0:T(8,128)(2,1)} %collective-permute-done.3, bf16[128,10,512]{2,1,0:T(8,128)(2,1)S(1)} %all-to-all-done.1, s32[1024]{0:T(1024)S(1)} %eq.60), kind=kOutput, calls=%fused_computation.29 | convolution fusion | flops 269484032 | bytes 2363392 | tf_op jit(solution)/shard_map/dot_general | solution.py:325
  (33 shorter events, 8.3 us)
Async XLA Ops:
  0.6 31.8 %copy-start = (bf16[256,512]{1,0:T(8,128)(2,1)S(1)}, bf16[256,512]{1,0:T(8,128)(2,1)}, u32[]{:S(2)}) copy-start(bf16[256,512]{1,0:T(8,128)(2,1)} %param.21) | copy-start | bytes 786436
  0.6 29.1 %copy-start.5 = (s32[2,4]{1,0:T(2,128)S(1)}, s32[2,4]{1,0:T(2,128)}, u32[]{:S(2)}) copy-start(s32[2,4]{1,0:T(2,128)} %param.24) | copy-start | bytes 100
  0.7 29.1 %copy-start.3 = (bf16[256,256]{1,0:T(8,128)(2,1)S(1)}, bf16[256,256]{1,0:T(8,128)(2,1)}, u32[]{:S(2)}) copy-start(bf16[256,256]{1,0:T(8,128)(2,1)} %param.22) | copy-start | bytes 393220
  2.5 29.9 %copy-start.4 = (s32[256,3]{0,1:T(4,128)S(1)}, s32[256,3]{0,1:T(4,128)}, u32[]{:S(2)}) copy-start(s32[256,3]{0,1:T(4,128)} %param.27) | copy-start | bytes 9220
  4.9 49.5 %all-to-all-start = ((bf16[128,8,512]{2,1,0:T(8,128)(2,1)}), bf16[128,8,512]{2,1,0:T(8,128)(2,1)S(1)}, u32[]{:S(2)}, u32[]{:S(2)}) async-start(bf16[128,8,512]{2,1,0:T(8,128)(2,1)} %fusion.8), calls=%async_computation | async-start | bytes 2097152 | tf_op jit(solution)/shard_map/all_to_all | solution.py:272
  20.8 27.1 %collective-permute-start.1 = (bf16[256,512]{1,0:T(8,128)(2,1)S(1)}, bf16[256,512]{1,0:T(8,128)(2,1)S(1)}, u32[]{:S(2)}, u32[]{:S(2)}) collective-permute-start(bf16[256,512]{1,0:T(8,128)(2,1)S(1)} %constant_dynamic-update-slice_fusion), channel_id=1, source_target_pairs={{2,0},{4,2},{6,4},{8,6},{10,8},{12,10},{14,12},{16,14},{18,16},{20... | collective-permute-start | bytes 786440 | tf_op jit(solution)/shard_map/ppermute | solution.py:24
  27.8 25.6 %collective-permute-start = (bf16[256,512]{1,0:T(8,128)(2,1)S(1)}, bf16[256,512]{1,0:T(8,128)(2,1)S(1)}, u32[]{:S(2)}, u32[]{:S(2)}) collective-permute-start(bf16[256,512]{1,0:T(8,128)(2,1)S(1)} %constant_dynamic-update-slice_fusion), channel_id=1, source_target_pairs={{0,2},{2,4},{4,6},{6,8},{8,10},{10,12},{12,14},{14,16},{16,18},{18... | collective-permute-start | bytes 786440 | tf_op jit(solution)/shard_map/ppermute | solution.py:23
  65.1 1.6 %copy-start.1 = (f32[3,256,512]{2,1,0:T(8,128)S(1)}, f32[3,256,512]{2,1,0:T(8,128)}, u32[]{:S(2)}) copy-start(f32[3,256,512]{2,1,0:T(8,128)} %get-tuple-element.52) | copy-start | bytes 4718596
  70.7 9.2 %copy-start.2 = (bf16[256,256]{1,0:T(8,128)(2,1)S(1)}, bf16[256,256]{1,0:T(8,128)(2,1)}, u32[]{:S(2)}) copy-start(bf16[256,256]{1,0:T(8,128)(2,1)} %get-tuple-element.49) | copy-start | bytes 393220
  70.7 59.4 %all-to-all-start.1 = ((bf16[128,10,512]{2,1,0:T(8,128)(2,1)}), bf16[128,10,512]{2,1,0:T(8,128)(2,1)S(1)}, u32[]{:S(2)}, u32[]{:S(2)}) async-start(bf16[128,10,512]{2,1,0:T(8,128)(2,1)} %pad_maximum_fusion), calls=%async_computation.1 | async-start | bytes 4194304 | tf_op jit(solution)/shard_map/all_to_all | solution.py:319
  80.8 27.0 %collective-permute-start.2 = (f32[256,256]{1,0:T(8,128)}, f32[256,256]{1,0:T(8,128)}, u32[]{:S(2)}, u32[]{:S(2)}) collective-permute-start(f32[256,256]{1,0:T(8,128)} %constant_dynamic-slice_fusion), channel_id=1, source_target_pairs={{0,1},{1,0},{2,3},{3,2},{4,5},{5,4},{6,7},{7,6},{8,9},{9,8},{10,11... | collective-permute-start | bytes 786440 | tf_op jit(solution)/shard_map/ppermute | solution.py:332
  99.0 32.0 %collective-permute-start.4 = (bf16[256,512]{1,0:T(8,128)(2,1)}, bf16[256,512]{1,0:T(8,128)(2,1)}, u32[]{:S(2)}, u32[]{:S(2)}) collective-permute-start(bf16[256,512]{1,0:T(8,128)(2,1)} %bitcast.7), channel_id=1, source_target_pairs={{2,0},{4,2},{6,4},{8,6},{10,8},{12,10},{14,12},{16,14},{18,16},{20... | collective-permute-start | bytes 786440 | tf_op jit(solution)/shard_map/ppermute | solution.py:32
  105.9 28.9 %collective-permute-start.3 = (bf16[256,512]{1,0:T(8,128)(2,1)}, bf16[256,512]{1,0:T(8,128)(2,1)}, u32[]{:S(2)}, u32[]{:S(2)}) collective-permute-start(bf16[256,512]{1,0:T(8,128)(2,1)} %bitcast.6), channel_id=1, source_target_pairs={{0,2},{2,4},{4,6},{6,8},{8,10},{10,12},{12,14},{14,16},{16,18},{18... | collective-permute-start | bytes 786440 | tf_op jit(solution)/shard_map/ppermute | solution.py:32

commit v6 on v5

--- a/solution.py
+++ b/solution.py
@@ -237,6 +237,117 @@
     )(pos, cnt, bias, q, do, ext, far)
 
 
+def _fwd_kernel(heads, kt, pos_ref, cnt_ref, bias_ref, q_ref, do_ref, ext_ref, hit_ref, recv_ref,
+                attn_ref, fg_ref, far_ref):
+    cols = q_ref.shape[1]
+    hs = cols // heads
+    scale = hs ** (-0.5)
+    n = q_ref.shape[0]
+    n_tiles = n // TILE
+    f32, bf16 = jnp.float32, jnp.bfloat16
+    recv = recv_ref[...]
+    for e in range(DEG):
+        far_ref[e] = jnp.dot(
+            hit_ref[pl.ds(e * n, n), :], recv, preferred_element_type=f32
+        ).astype(bf16)
+    seg = (
+        lax.broadcasted_iota(jnp.int32, (cols, TILE), 0) // hs
+        == lax.broadcasted_iota(jnp.int32, (cols, TILE), 1)
+    ).astype(bf16)
+    spread = (
+        lax.broadcasted_iota(jnp.int32, (TILE, cols), 0)
+        == lax.broadcasted_iota(jnp.int32, (TILE, cols), 1) // hs
+    ).astype(bf16)
+    lane = lax.broadcasted_iota(jnp.int32, (TILE, cols), 1)
+    col = lax.broadcasted_iota(jnp.int32, (TILE, TILE), 1)
+    bias_row = jnp.zeros((TILE, TILE), f32)
+    for h in range(heads):
+        bias_row = jnp.where(col == h, bias_ref[h], bias_row)
+    nt = (((1,), (1,)), ((), ()))
+
+    def seg_sum(x):
+        hi = x.astype(bf16)
+        lo = (x - hi.astype(f32)).astype(bf16)
+        return jnp.dot(hi, seg, preferred_element_type=f32) + jnp.dot(lo, seg, preferred_element_type=f32)
+
+    for t in range(n_tiles):
+        rows = pl.ds(t * TILE, TILE)
+        count = cnt_ref[t]
+        pos = [pos_ref[t * kt + j] for j in range(kt)]
+        q = q_ref[rows, :]
+        do = do_ref[rows, :]
+        qf = q.astype(f32)
+        dof = do.astype(f32)
+        fk = [far_ref[e, rows, :cols].astype(f32) for e in range(DEG)]
+        fv = [far_ref[e, rows, cols:].astype(f32) for e in range(DEG)]
+        fs_all = [seg_sum(qf * fk[e]) * scale + bias_row for e in range(DEG)]
+        fdp_all = [seg_sum(dof * fv[e]) for e in range(DEG)]
+        live = [j < count for j in range(kt)]
+        attn_acc = jnp.zeros((TILE, cols), f32)
+        fds_cols = [jnp.zeros((TILE, TILE), f32) for e in range(DEG)]
+        fpr_cols = [jnp.zeros((TILE, TILE), f32) for e in range(DEG)]
+        for h in range(heads):
+            mask = (lane >= h * hs) & (lane < (h + 1) * hs)
+            qh = jnp.where(mask, q, jnp.zeros_like(q))
+            keys = [ext_ref[pos[j], :, :cols] for j in range(kt)]
+            vals = [ext_ref[pos[j], :, cols:] for j in range(kt)]
+            s = [lax.dot_general(qh, keys[j], nt, preferred_element_type=f32) * scale for j in range(kt)]
+            fs = [fs_all[e][:, h:h + 1] for e in range(DEG)]
+            m = fs[0]
+            for e in range(1, DEG):
+                m = jnp.maximum(m, fs[e])
+            for j in range(kt):
+                m = jnp.maximum(m, jnp.where(live[j], jnp.max(s[j], axis=1, keepdims=True), -jnp.inf))
+            ne = [jnp.where(live[j], jnp.exp(s[j] - m), 0.0) for j in range(kt)]
+            fe = [jnp.exp(fs[e] - m) for e in range(DEG)]
+            row_sum = fe[0] + fe[1] + fe[2]
+            row_sum = jnp.sum(ne[0], axis=1, keepdims=True) + row_sum
+            for j in range(1, kt):
+                row_sum = row_sum + jnp.sum(ne[j], axis=1, keepdims=True)
+            mixed = jnp.dot(ne[0].astype(bf16), vals[0], preferred_element_type=f32)
+            for j in range(1, kt):
+                mixed = mixed + jnp.dot(ne[j].astype(bf16), vals[j], preferred_element_type=f32)
+            for e in range(DEG):
+                mixed = mixed + fe[e].astype(bf16).astype(f32) * fv[e]
+            attn = (mixed / row_sum).astype(bf16).astype(f32)
+            attn_acc = jnp.where(mask, attn, attn_acc)
+            delta = jnp.sum(jnp.where(mask, dof * attn, 0.0), axis=1, keepdims=True)
+            for e in range(DEG):
+                fpr = fe[e] / row_sum
+                fds = (fpr * (fdp_all[e][:, h:h + 1] - delta)).astype(bf16).astype(f32)
+                fds_cols[e] = jnp.where(col == h, fds, fds_cols[e])
+                fpr_cols[e] = jnp.where(col == h, fpr.astype(bf16).astype(f32), fpr_cols[e])
+        attn_ref[rows, :] = attn_acc.astype(attn_ref.dtype)
+        for e in range(DEG):
+            fds_wide = jnp.dot(fds_cols[e].astype(bf16), spread, preferred_element_type=f32)
+            fpr_wide = jnp.dot(fpr_cols[e].astype(bf16), spread, preferred_element_type=f32)
+            fg_ref[e, rows, :cols] = fds_wide * qf * scale
+            fg_ref[e, rows, cols:] = fpr_wide * dof
+
+
+def forward_tiles(pos, cnt, bias, q, do, ext, hit, recv):
+    heads = bias.shape[0]
+    kt = pos.shape[0] // cnt.shape[0]
+    n, cols = q.shape
+    smem = pl.BlockSpec(memory_space=pltpu.SMEM)
+    vmem = pl.BlockSpec(memory_space=pltpu.VMEM)
+    return pl.pallas_call(
+        functools.partial(_fwd_kernel, heads, kt),
+        out_shape=(
+            jax.ShapeDtypeStruct((n, cols), jnp.bfloat16),
+            jax.ShapeDtypeStruct((DEG, n, 2 * cols), jnp.float32),
+            jax.ShapeDtypeStruct((DEG, n, 2 * cols), jnp.bfloat16),
+        ),
+        in_specs=[smem, smem, smem, vmem, vmem, vmem, vmem, vmem],
+        out_specs=(vmem, vmem, vmem),
+        cost_estimate=pl.CostEstimate(
+            flops=int(2 * n * kt * TILE * cols * 3 * heads + 2 * hit.shape[0] * hit.shape[1] * recv.shape[1]),
+            bytes_accessed=int(8 * 1024 * 1024),
+            transcendentals=int(n * heads * (kt * TILE + DEG)),
+        ),
+    )(pos, cnt, bias, q, do, ext, hit, recv)
+
+
 def shards(
     query_rows,
     key_rows,
@@ -275,23 +386,21 @@
     far_hit = (
         edge_slots[:, None] == jnp.arange(n_recv, dtype=jnp.int32)[None, :]
     ).astype(jnp.bfloat16)
-    far_all = (
-        jnp.dot(far_hit, received.reshape(n_recv, -1), preferred_element_type=jnp.float32)
-        .astype(jnp.bfloat16)
-        .reshape(DEG, node_count, -1)
-    )
     base_tile = dom_index * per_part - HALO
-    kernel_args = (
-        (tile_list - base_tile).reshape(-1),
+    tile_pos = (tile_list - base_tile).reshape(-1)
+    attn_all, far_grad, far_all = forward_tiles(
+        tile_pos,
         tile_count,
         far_bias,
         query_rows,
         attn_grad,
         ext_tiles,
-        far_all,
-    )
-    attn_all, far_grad = attention_tiles(False, *kernel_args)
-    qgrad_all, ext_grad = attention_tiles(True, *kernel_args)
+        far_hit,
+        received.reshape(n_recv, -1),
+    )
+    qgrad_all, ext_grad = attention_tiles(
+        True, tile_pos, tile_count, far_bias, query_rows, attn_grad, ext_tiles, far_all
+    )
     ext_grad = ext_grad.reshape(-1, 2 * col_width)
     attn_mine = attn_all.reshape(node_count, col_width)
     low_part = ext_grad[:rim_rows]

time: 138 us -> 142 us (1.029)
  other arithmetic: 6.36 us -> 9.34 us
  waiting for transfers between devices: 44.5 us -> 41.6 us
  starting transfers between devices: 42.8 us -> 45.2 us
    all_to_all x1, waiting for transfers between devices: 20.6 us -> 0.01 us  [shards(): lax.all_to_all(both, 'dom', split_axis=0, concat_axis=0, tiled=True)]
    ppermute x2, waiting for transfers between devices: 3.82 us -> 24.1 us  [from_behind(): lax.ppermute(value, axis, [(source, source + steps) for source in range(l...]
    ppermute x1, waiting for transfers between devices: 14.6 us -> 0.01 us  [extended_2(): after = lax.ppermute(leading, axis, down)]
    ppermute x1, waiting for transfers between devices: 5.53 us -> 17.5 us  [extended_2(): before = lax.ppermute(last, axis, up)]
    pallas_call x0 -> x1, Pallas kernels: none -> 9.67 us  [forward_tiles(): pl.pallas_call(functools.partial(_fwd_kernel, heads, kt), out_shape=(jax....]
    pallas_call x2 -> x1, Pallas kernels: 23.5 us -> 14.7 us  [attention_tiles(): pl.pallas_call(functools.partial(_attn_kernel, heads, kt, near_out), out_...]
    dot_general x1 -> x0, matrix products: 1.91 us -> none  [shards(): jnp.dot(far_hit, received.reshape(n_recv, -1), preferred_element_type=jnp...]
    dot_general x1, matrix products: 0.99 us -> 2.58 us  [shards(): jnp.dot(slot_hit, pair_hi.astype(jnp.bfloat16), preferred_element_type=jn...]
  transfers between devices with their start and end apart: 7 -> 7, of which waited for: 4 -> 2; matrix products, arithmetic and copies ran while one was open for 7% -> 7% of each run, Pallas kernels for 11% -> 10%
where the time goes in v6:
time: 142 us; the launch traced here: 141 us
  starting transfers between devices  45.2 us (32%)
  waiting for transfers between devices  41.6 us (29%)
  Pallas kernels  24.4 us (17%)
  other arithmetic  9.34 us (7%)
  matrix products  9.27 us (7%)
  local copies, waits for them, and re-layouts  8.68 us (6%)
  blocking collectives  1.98 us (1%)
    ppermute x2, waiting for transfers between devices, from_behind(): lax.ppermute(value, axis, [(source, source + steps) for source in range(l...  24.1 us
    ppermute x1, waiting for transfers between devices, extended_2(): before = lax.ppermute(last, axis, up)  17.5 us
    all_to_all x1, starting transfers between devices, shards(): lax.all_to_all(outgoing, 'dom', split_axis=0, concat_axis=0, tiled=True)  15.9 us
    pallas_call x1, Pallas kernels, attention_tiles(): pl.pallas_call(functools.partial(_attn_kernel, heads, kt, near_out), out_...  14.7 us
    ppermute x2, starting transfers between devices, from_behind(): lax.ppermute(value, axis, [(source, source + steps) for source in range(l...  10.1 us
    pallas_call x1, Pallas kernels, forward_tiles(): pl.pallas_call(functools.partial(_fwd_kernel, heads, kt), out_shape=(jax....  9.67 us
    all_to_all x1, starting transfers between devices, shards(): lax.all_to_all(both, 'dom', split_axis=0, concat_axis=0, tiled=True)  9.19 us
    ppermute x1, starting transfers between devices, extended_2(): after = lax.ppermute(leading, axis, down)  6.68 us
  transfers between devices with their start and end apart: 7, of which 2 were waited for; matrix products, arithmetic and copies ran while one was open for 7% of the time, Pallas kernels for 10%

profile of v6, /device:TPU:6, one launch (start us, length us, event | category | flops | bytes accessed | tf_op | source)
XLA Modules:
  0.0 141.3 jit_solution(5965404220804349650)
XLA Ops:
  0.7 1.0 constant_dynamic-update-slice_fusion.1
  3.4 1.5 %fusion.6 = bf16[128,8,512]{2,1,0:T(8,128)(2,1)} fusion(bf16[256,512]{1,0:T(8,128)(2,1)S(1)} %constant_dynamic-update-slice_fusion, s32[1024]{0:T(1024)S(1)} %eq.60), kind=kOutput, calls=%fused_computation.13 | convolution fusion | flops 269221888 | bytes 1314816 | tf_op jit(solution)/shard_map/dot_general | solution.py:379
  4.9 15.9 %all-to-all-start = ((bf16[128,8,512]{2,1,0:T(8,128)(2,1)}), bf16[128,8,512]{2,1,0:T(8,128)(2,1)S(1)}, u32[]{:S(2)}, u32[]{:S(2)}) async-start(bf16[128,8,512]{2,1,0:T(8,128)(2,1)} %fusion.6), calls=%async_computation | async-start | bytes 2097152 | tf_op jit(solution)/shard_map/all_to_all | solution.py:383
  20.8 3.4 %collective-permute-start = (bf16[256,512]{1,0:T(8,128)(2,1)S(1)}, bf16[256,512]{1,0:T(8,128)(2,1)S(1)}, u32[]{:S(2)}, u32[]{:S(2)}) collective-permute-start(bf16[256,512]{1,0:T(8,128)(2,1)S(1)} %constant_dynamic-update-slice_fusion), channel_id=1, source_target_pairs={{0,2},{2,4},{4,6},{6,8},{8,10},{10,12},{12,14},{14,16},{16,18},{18... | collective-permute-start | bytes 786440 | tf_op jit(solution)/shard_map/ppermute | solution.py:23
  24.2 6.7 %collective-permute-start.1 = (bf16[256,512]{1,0:T(8,128)(2,1)S(1)}, bf16[256,512]{1,0:T(8,128)(2,1)S(1)}, u32[]{:S(2)}, u32[]{:S(2)}) collective-permute-start(bf16[256,512]{1,0:T(8,128)(2,1)S(1)} %constant_dynamic-update-slice_fusion), channel_id=1, source_target_pairs={{2,0},{4,2},{6,4},{8,6},{10,8},{12,10},{14,12},{16,14},{18,16},{20... | collective-permute-start | bytes 786440 | tf_op jit(solution)/shard_map/ppermute | solution.py:24
  31.6 2.0 %all_gather.3 = bf16[256,512]{1,0:T(8,128)(2,1)S(1)} all-gather(bf16[256,256]{1,0:T(8,128)(2,1)S(1)} %copy-done.3), channel_id=1, replica_groups=mesh['dom'=128,'head'=2] {'head'}, dimensions={1}, use_global_device_ids=true | all-gather | bytes 393216 | tf_op jit(solution)/shard_map/all_gather | solution.py:367
  34.5 1.5 %fusion.2.hit_ref = bf16[768,1024]{1,0:T(8,128)(2,1)} fusion(s32[768]{0:T(1024)S(1)} %eq.56), kind=kLoop, calls=%fused_computation.4 | loop fusion | flops 1572864 | bytes 1575936 | tf_op jit(solution)/shard_map/convert_element_type | solution.py:388
  36.0 17.5 %collective-permute-done = bf16[256,512]{1,0:T(8,128)(2,1)S(1)} collective-permute-done((bf16[256,512]{1,0:T(8,128)(2,1)S(1)}, bf16[256,512]{1,0:T(8,128)(2,1)S(1)}, u32[]{:S(2)}, u32[]{:S(2)}) %collective-permute-start) | collective-permute-done | bytes 262176 | tf_op jit(solution)/shard_map/ppermute | solution.py:23
  53.5 0.9 pad_maximum_fusion.1
  54.4 1.0 copy-done.1
  55.4 9.7 %shard_map.147 = (bf16[256,256]{1,0:T(8,128)(2,1)}, f32[3,256,512]{2,1,0:T(8,128)}, bf16[3,256,512]{2,1,0:T(8,128)(2,1)}) custom-call(s32[8]{0:T(128)} %reshape.99.pos_ref, s32[2]{0:T(128)} %cnt_ref.3, f32[4]{0:T(128)} %bias_ref.3, bf16[256,256]{1,0:T(8,128)(2,1)} %q_ref.3, bf16[256,256]{1,0:T(8,128)(2,1)} %convolution_convert_fusion.2.do_ref, ...), custom_call_target="tpu_custom_call" | custom-call | flops 1610612736 | bytes 8388608 | tf_op jit(solution)/shard_map/pallas_call | solution.py:334
  65.1 1.6 %reduce-precision_convert_fusion = (bf16[768,512]{1,0:T(8,128)(2,1)S(1)}, bf16[768,512]{1,0:T(8,128)(2,1)S(1)}) fusion(f32[3,256,512]{2,1,0:T(8,128)} %get-tuple-element.54), kind=kLoop, calls=%fused_computation.6 | loop fusion | flops 1572864 | bytes 3145728 | tf_op jit(solution)/shard_map/convert_element_type | solution.py:420
  66.8 2.3 %fusion = f32[1024,512]{1,0:T(8,128)} fusion(bf16[768,512]{1,0:T(8,128)(2,1)S(1)} %get-tuple-element.56, s32[768]{0:T(1024)S(1)} %eq.56), kind=kOutput, calls=%fused_computation.1 | convolution fusion | flops 806092800 | bytes 2886656 | tf_op jit(solution)/shard_map/dot_general | solution.py:421
  69.7 2.6 %fusion.7 = bf16[128,8,512]{2,1,0:T(8,128)(2,1)S(1)} fusion(f32[1024,512]{1,0:T(8,128)} %fusion, bf16[768,512]{1,0:T(8,128)(2,1)S(1)} %get-tuple-element.55, s32[768]{0:T(1024)S(1)} %eq.56), kind=kOutput, calls=%fused_computation.14 | convolution fusion | flops 807141376 | bytes 3935232 | tf_op jit(solution)/shard_map/dot_general | solution.py:419
  72.2 1.8 %pad_maximum_fusion = bf16[128,10,512]{2,1,0:T(8,128)(2,1)} fusion(bf16[128,2,512]{2,1,0:T(2,128)(2,1)S(1)} %reshape.105, bf16[128,8,512]{2,1,0:T(8,128)(2,1)S(1)} %fusion.7), kind=kLoop, calls=%fused_computation.7 | loop fusion | flops 2621440 | bytes 2621440 | tf_op jit(solution)/shard_map/concatenate | solution.py:425
  74.1 9.2 %all-to-all-start.1 = ((bf16[128,10,512]{2,1,0:T(8,128)(2,1)}), bf16[128,10,512]{2,1,0:T(8,128)(2,1)S(1)}, u32[]{:S(2)}, u32[]{:S(2)}) async-start(bf16[128,10,512]{2,1,0:T(8,128)(2,1)} %pad_maximum_fusion), calls=%async_computation.1 | async-start | bytes 4194304 | tf_op jit(solution)/shard_map/all_to_all | solution.py:428
  83.3 14.7 %shard_map.148 = (bf16[256,256]{1,0:T(8,128)(2,1)}, f32[6,128,512]{2,1,0:T(8,128)}) custom-call(s32[8]{0:T(128)} %reshape.99.pos_ref, s32[2]{0:T(128)} %cnt_ref.3, f32[4]{0:T(128)} %bias_ref.3, bf16[256,256]{1,0:T(8,128)(2,1)} %q_ref.3, bf16[256,256]{1,0:T(8,128)(2,1)} %convolution_convert_fusion.2.do_ref, bf16[6,128,512]{2,1,0:T(8,128)(2,1)} %bitcast.38, ...), custom_call_target="tpu_custom_call" | custom-call | flops 1610612736 | bytes 4194304 | tf_op jit(solution)/shard_map/pallas_call | solution.py:226
  98.0 1.5 %convert.17 = bf16[6,128,512]{2,1,0:T(8,128)(2,1)S(1)} convert(f32[6,128,512]{2,1,0:T(8,128)} %get-tuple-element.53) | non-fusion elementwise | flops 393216 | bytes 2359296 | tf_op jit(solution)/shard_map/convert.8
  101.3 3.4 %collective-permute-start.3 = (bf16[256,512]{1,0:T(8,128)(2,1)}, bf16[256,512]{1,0:T(8,128)(2,1)}, u32[]{:S(2)}, u32[]{:S(2)}) collective-permute-start(bf16[256,512]{1,0:T(8,128)(2,1)} %bitcast.5), channel_id=1, source_target_pairs={{0,2},{2,4},{4,6},{6,8},{8,10},{10,12},{12,14},{14,16},{16,18},{18... | collective-permute-start | bytes 786440 | tf_op jit(solution)/shard_map/ppermute | solution.py:32
  104.7 6.7 %collective-permute-start.4 = (bf16[256,512]{1,0:T(8,128)(2,1)}, bf16[256,512]{1,0:T(8,128)(2,1)}, u32[]{:S(2)}, u32[]{:S(2)}) collective-permute-start(bf16[256,512]{1,0:T(8,128)(2,1)} %bitcast.6), channel_id=1, source_target_pairs={{2,0},{4,2},{6,4},{8,6},{10,8},{12,10},{14,12},{16,14},{18,16},{20... | collective-permute-start | bytes 786440 | tf_op jit(solution)/shard_map/ppermute | solution.py:32
  111.4 1.1 slice.58
  112.5 1.7 %add_convert_fusion.1 = bf16[256,256]{1,0:T(8,128)(2,1)} fusion(f32[256,256]{1,0:T(8,128)} %collective-permute-done.2, f32[256,512]{1,0:T(8,128)S(1)} %fusion.17, s32[]{:T(128)S(6)} %select_n.6), kind=kLoop, calls=%fused_computation.30 | loop fusion | flops 131072 | bytes 655364 | tf_op jit(solution)/shard_map/convert_element_type | solution.py:442
  114.1 24.1 %collective-permute-done.3 = bf16[256,512]{1,0:T(8,128)(2,1)} collective-permute-done((bf16[256,512]{1,0:T(8,128)(2,1)}, bf16[256,512]{1,0:T(8,128)(2,1)}, u32[]{:S(2)}, u32[]{:S(2)}) %collective-permute-start.3) | collective-permute-done | bytes 262176 | tf_op jit(solution)/shard_map/ppermute | solution.py:32
  138.2 1.5 %fusion.12 = bf16[256,512]{1,0:T(8,128)(2,1)S(1)} fusion(f32[2,128,512]{2,1,0:T(8,128)S(1)} %slice.58, bf16[256,512]{1,0:T(8,128)(2,1)} %collective-permute-done.4, bf16[256,512]{1,0:T(8,128)(2,1)} %collective-permute-done.3, bf16[128,10,512]{2,1,0:T(8,128)(2,1)S(1)} %all-to-all-done.1, s32[1024]{0:T(1024)S(1)} %eq.60), kind=kOutput, calls=%fused_computation.26 | convolution fusion | flops 269484032 | bytes 2363392 | tf_op jit(solution)/shard_map/dot_general | solution.py:434
  (33 shorter events, 7.3 us)
Async XLA Ops:
  0.6 32.9 %copy-start = (bf16[256,512]{1,0:T(8,128)(2,1)S(1)}, bf16[256,512]{1,0:T(8,128)(2,1)}, u32[]{:S(2)}) copy-start(bf16[256,512]{1,0:T(8,128)(2,1)} %param.21) | copy-start | bytes 786436
  0.6 30.3 %copy-start.4 = (s32[256,3]{0,1:T(4,128)S(1)}, s32[256,3]{0,1:T(4,128)}, u32[]{:S(2)}) copy-start(s32[256,3]{0,1:T(4,128)} %param.27) | copy-start | bytes 9220
  0.7 30.3 %copy-start.5 = (s32[2,4]{1,0:T(2,128)S(1)}, s32[2,4]{1,0:T(2,128)}, u32[]{:S(2)}) copy-start(s32[2,4]{1,0:T(2,128)} %param.24) | copy-start | bytes 100
  0.7 30.9 %copy-start.3 = (bf16[256,256]{1,0:T(8,128)(2,1)S(1)}, bf16[256,256]{1,0:T(8,128)(2,1)}, u32[]{:S(2)}) copy-start(bf16[256,256]{1,0:T(8,128)(2,1)} %param.22) | copy-start | bytes 393220
  4.9 49.5 %all-to-all-start = ((bf16[128,8,512]{2,1,0:T(8,128)(2,1)}), bf16[128,8,512]{2,1,0:T(8,128)(2,1)S(1)}, u32[]{:S(2)}, u32[]{:S(2)}) async-start(bf16[128,8,512]{2,1,0:T(8,128)(2,1)} %fusion.6), calls=%async_computation | async-start | bytes 2097152 | tf_op jit(solution)/shard_map/all_to_all | solution.py:383
  20.8 32.6 %collective-permute-start = (bf16[256,512]{1,0:T(8,128)(2,1)S(1)}, bf16[256,512]{1,0:T(8,128)(2,1)S(1)}, u32[]{:S(2)}, u32[]{:S(2)}) collective-permute-start(bf16[256,512]{1,0:T(8,128)(2,1)S(1)} %constant_dynamic-update-slice_fusion), channel_id=1, source_target_pairs={{0,2},{2,4},{4,6},{6,8},{8,10},{10,12},{12,14},{14,16},{16,18},{18... | collective-permute-start | bytes 786440 | tf_op jit(solution)/shard_map/ppermute | solution.py:23
  24.2 29.2 %collective-permute-start.1 = (bf16[256,512]{1,0:T(8,128)(2,1)S(1)}, bf16[256,512]{1,0:T(8,128)(2,1)S(1)}, u32[]{:S(2)}, u32[]{:S(2)}) collective-permute-start(bf16[256,512]{1,0:T(8,128)(2,1)S(1)} %constant_dynamic-update-slice_fusion), channel_id=1, source_target_pairs={{2,0},{4,2},{6,4},{8,6},{10,8},{12,10},{14,12},{16,14},{18,16},{20... | collective-permute-start | bytes 786440 | tf_op jit(solution)/shard_map/ppermute | solution.py:24
  54.4 1.0 copy-start.1
  66.7 2.3 %copy-start.2 = (bf16[256,256]{1,0:T(8,128)(2,1)S(1)}, bf16[256,256]{1,0:T(8,128)(2,1)}, u32[]{:S(2)}) copy-start(bf16[256,256]{1,0:T(8,128)(2,1)} %get-tuple-element.50) | copy-start | bytes 393220
  74.1 64.2 %all-to-all-start.1 = ((bf16[128,10,512]{2,1,0:T(8,128)(2,1)}), bf16[128,10,512]{2,1,0:T(8,128)(2,1)S(1)}, u32[]{:S(2)}, u32[]{:S(2)}) async-start(bf16[128,10,512]{2,1,0:T(8,128)(2,1)} %pad_maximum_fusion), calls=%async_computation.1 | async-start | bytes 4194304 | tf_op jit(solution)/shard_map/all_to_all | solution.py:428
  100.5 12.0 %collective-permute-start.2 = (f32[256,256]{1,0:T(8,128)}, f32[256,256]{1,0:T(8,128)}, u32[]{:S(2)}, u32[]{:S(2)}) collective-permute-start(f32[256,256]{1,0:T(8,128)} %constant_dynamic-slice_fusion), channel_id=1, source_target_pairs={{0,1},{1,0},{2,3},{3,2},{4,5},{5,4},{6,7},{7,6},{8,9},{9,8},{10,11... | collective-permute-start | bytes 786440 | tf_op jit(solution)/shard_map/ppermute | solution.py:441
  101.3 36.9 %collective-permute-start.3 = (bf16[256,512]{1,0:T(8,128)(2,1)}, bf16[256,512]{1,0:T(8,128)(2,1)}, u32[]{:S(2)}, u32[]{:S(2)}) collective-permute-start(bf16[256,512]{1,0:T(8,128)(2,1)} %bitcast.5), channel_id=1, source_target_pairs={{0,2},{2,4},{4,6},{6,8},{8,10},{10,12},{12,14},{14,16},{16,18},{18... | collective-permute-start | bytes 786440 | tf_op jit(solution)/shard_map/ppermute | solution.py:32
  104.7 33.5 %collective-permute-start.4 = (bf16[256,512]{1,0:T(8,128)(2,1)}, bf16[256,512]{1,0:T(8,128)(2,1)}, u32[]{:S(2)}, u32[]{:S(2)}) collective-permute-start(bf16[256,512]{1,0:T(8,128)(2,1)} %bitcast.6), channel_id=1, source_target_pairs={{2,0},{4,2},{6,4},{8,6},{10,8},{12,10},{14,12},{16,14},{18,16},{20... | collective-permute-start | bytes 786440 | tf_op jit(solution)/shard_map/ppermute | solution.py:32

commit v7 on v5

--- a/solution.py
+++ b/solution.py
@@ -129,7 +129,7 @@
     if near_out:
         qg_ref, eg_ref, acc = refs
     else:
-        attn_ref, fg_ref, acc = refs
+        fge_ref, fgo_ref, attn_ref, fg_ref, acc = refs
     cols = q_ref.shape[1]
     hs = cols // heads
     scale = hs ** (-0.5)
@@ -189,8 +189,9 @@
                     fdp = jnp.sum(jnp.where(mask, dof * fv[e], 0.0), axis=1, keepdims=True)
                     fpr = fe[e] / row_sum
                     fds = (fpr * (fdp - delta)).astype(bf16).astype(f32)
-                    fg_ref[e, rows, :cols] += jnp.where(mask, fds * qf * scale, 0.0)
-                    fg_ref[e, rows, cols:] += jnp.where(mask, fpr.astype(bf16).astype(f32) * dof, 0.0)
+                    pair_rows = pl.ds(e * q_ref.shape[0] + t * TILE, TILE)
+                    fg_ref[pair_rows, :cols] += jnp.where(mask, fds * qf * scale, 0.0)
+                    fg_ref[pair_rows, cols:] += jnp.where(mask, fpr.astype(bf16).astype(f32) * dof, 0.0)
                 return carry
             qg = None
             for j in range(kt):
@@ -214,19 +215,29 @@
         lax.fori_loop(0, heads, head_body, 0)
         out_ref = qg_ref if near_out else attn_ref
         out_ref[rows, :] = acc[rows, :].astype(out_ref.dtype)
-
-
-def attention_tiles(near_out, pos, cnt, bias, q, do, ext, far):
+    if not near_out:
+        w_rows = pl.ds(DEG * q_ref.shape[0], fge_ref.shape[1])
+        attn_all = attn_ref[...]
+        fg_ref[w_rows, :cols] = lax.dot_general(fge_ref[...], attn_all, tn, preferred_element_type=f32)
+        fg_ref[w_rows, cols:] = lax.dot_general(fgo_ref[...], attn_all, tn, preferred_element_type=f32)
+
+
+def attention_tiles(near_out, pos, cnt, bias, q, do, ext, far, *model_cols):
     heads = bias.shape[0]
     kt = pos.shape[0] // cnt.shape[0]
     n, cols = q.shape
     smem = pl.BlockSpec(memory_space=pltpu.SMEM)
     vmem = pl.BlockSpec(memory_space=pltpu.VMEM)
-    grads = jax.ShapeDtypeStruct(ext.shape if near_out else far.shape, jnp.float32)
+    if near_out:
+        grads = jax.ShapeDtypeStruct(ext.shape, jnp.float32)
+    else:
+        grads = jax.ShapeDtypeStruct(
+            (DEG * n + model_cols[0].shape[1], far.shape[2]), jnp.float32
+        )
     return pl.pallas_call(
         functools.partial(_attn_kernel, heads, kt, near_out),
         out_shape=(jax.ShapeDtypeStruct((n, cols), jnp.bfloat16), grads),
-        in_specs=[smem, smem, smem, vmem, vmem, vmem, vmem],
+        in_specs=[smem, smem, smem] + [vmem] * (4 + len(model_cols)),
         out_specs=(vmem, vmem),
         scratch_shapes=[pltpu.VMEM((n, cols), jnp.float32)],
         cost_estimate=pl.CostEstimate(
@@ -234,7 +245,7 @@
             bytes_accessed=int(4 * 1024 * 1024),
             transcendentals=int(n * heads * (kt * TILE + DEG)),
         ),
-    )(pos, cnt, bias, q, do, ext, far)
+    )(pos, cnt, bias, q, do, ext, far, *model_cols)
 
 
 def shards(
@@ -290,7 +301,9 @@
         ext_tiles,
         far_all,
     )
-    attn_all, far_grad = attention_tiles(False, *kernel_args)
+    attn_all, far_grad = attention_tiles(
+        False, *kernel_args, full_grad[:, 0::2], full_grad[:, 1::2]
+    )
     qgrad_all, ext_grad = attention_tiles(True, *kernel_args)
     ext_grad = ext_grad.reshape(-1, 2 * col_width)
     attn_mine = attn_all.reshape(node_count, col_width)
@@ -301,21 +314,25 @@
     from_prev = from_behind(high_part.astype(jnp.bfloat16), "dom", 1).astype(high_part.dtype)
     own_grad = own_grad.at[:rim_rows].add(from_prev).at[node_count - rim_rows :].add(from_next)
     n_dom, cap = received.shape[0], received.shape[1]
-    pair_grad = far_grad.reshape(-1, 2 * col_width)
-    pair_hi = lax.reduce_precision(pair_grad, exponent_bits=8, mantissa_bits=7)
-    pair_lo = (pair_grad - pair_hi).astype(jnp.bfloat16)
-    slot_hit = (
-        edge_slots.reshape(1, -1) == jnp.arange(n_dom * cap, dtype=jnp.int32)[:, None]
-    ).astype(jnp.bfloat16)
-    slot_grad = jnp.dot(
-        slot_hit, pair_hi.astype(jnp.bfloat16), preferred_element_type=jnp.float32
-    ) + jnp.dot(slot_hit, pair_lo, preferred_element_type=jnp.float32)
-    weight_part = lax.dot_general(
-        full_grad, attn_mine, (((0,), (0,)), ((), ())), preferred_element_type=jnp.float32
-    ).reshape(n_dom, -1, 2 * col_width)
-    both = jnp.concatenate(
-        [slot_grad.reshape(n_dom, cap, -1), weight_part], axis=1
-    ).astype(jnp.bfloat16)
+    n_pairs = DEG * node_count
+    w_per = (far_grad.shape[0] - n_pairs) // n_dom
+    pair_hi = lax.reduce_precision(far_grad, exponent_bits=8, mantissa_bits=7)
+    pair_lo = (far_grad - pair_hi).astype(jnp.bfloat16)
+    rho = jnp.arange(n_dom * (cap + w_per), dtype=jnp.int32)
+    dest, sub = rho // (cap + w_per), rho % (cap + w_per)
+    slot_target = jnp.where(sub < cap, dest * cap + sub, -1)
+    row_target = jnp.where(sub >= cap, n_pairs + dest * w_per + sub - cap, -1)
+    col = jnp.arange(far_grad.shape[0], dtype=jnp.int32)
+    col_slot = jnp.concatenate(
+        [edge_slots, jnp.full((far_grad.shape[0] - n_pairs,), -2, jnp.int32)]
+    )
+    payload_hit = (
+        (col_slot[None, :] == slot_target[:, None]) | (col[None, :] == row_target[:, None])
+    ).astype(jnp.bfloat16)
+    both = (
+        jnp.dot(payload_hit, pair_hi.astype(jnp.bfloat16), preferred_element_type=jnp.float32)
+        + jnp.dot(payload_hit, pair_lo, preferred_element_type=jnp.float32)
+    ).astype(jnp.bfloat16).reshape(n_dom, cap + w_per, -1)
     both_back = lax.all_to_all(both, "dom", split_axis=0, concat_axis=0, tiled=True)
     returned = both_back[:, :cap].reshape(-1, 2 * col_width)
     weight_sum = jnp.sum(both_back[:, cap:].astype(jnp.float32), axis=0)

time: 138 us -> 139 us (level)
  local copies, waits for them, and re-layouts: 7.69 us -> 22.2 us
  waiting for transfers between devices: 44.5 us -> 31.1 us
  matrix products: 9.29 us -> 11.4 us
  other arithmetic: 6.36 us -> 4.38 us
    ppermute x1, waiting for transfers between devices: 14.6 us -> 1.21 us  [extended_2(): after = lax.ppermute(leading, axis, down)]
    slice x0 -> x2, local copies, waits for them, and re-layouts: none -> 13.2 us  [the longest x1 6.6 us: shards(): full_grad[:, 1::2]]
    dot_general x3 -> x2, matrix products: 3.24 us -> 5.38 us  [the longest x1 3.31 us: shards(): jnp.dot(payload_hit, pair_lo, preferred_element_type=jnp.float32)]
    concatenate x1 -> x0, other arithmetic: 1.8 us -> none  [shards(): jnp.concatenate([slot_grad.reshape(n_dom, cap, -1), weight_part], axis=1)]
    reshape x1, local copies, waits for them, and re-layouts: 0.17 us -> 1.57 us  [shards(): both = (jnp.dot(payload_hit, pair_hi.astype(jnp.bfloat16), preferred_elem...]
  transfers between devices with their start and end apart: 7 -> 7, of which waited for: 4 -> 4; matrix products, arithmetic and copies ran while one was open for 7% -> 16% of each run, Pallas kernels for 11% -> 11%
where the time goes in v7:
time: 139 us
  starting transfers between devices  42.8 us (31%)
  waiting for transfers between devices  31.1 us (22%)
  Pallas kernels  24 us (17%)
  local copies, waits for them, and re-layouts  22.2 us (16%)
  matrix products  11.4 us (8%)
  other arithmetic  4.38 us (3%)
  blocking collectives  2.17 us (2%)
    pallas_call x2, Pallas kernels, attention_tiles(): pl.pallas_call(functools.partial(_attn_kernel, heads, kt, near_out), out_...  24 us
    all_to_all x1, waiting for transfers between devices, shards(): lax.all_to_all(both, 'dom', split_axis=0, concat_axis=0, tiled=True)  20.5 us
    all_to_all x1, starting transfers between devices, shards(): lax.all_to_all(outgoing, 'dom', split_axis=0, concat_axis=0, tiled=True)  15.9 us
    all_to_all x1, starting transfers between devices, shards(): lax.all_to_all(both, 'dom', split_axis=0, concat_axis=0, tiled=True)  9.14 us
    ppermute x2, starting transfers between devices, from_behind(): lax.ppermute(value, axis, [(source, source + steps) for source in range(l...  8.88 us
    ppermute x1, starting transfers between devices, extended_2(): after = lax.ppermute(leading, axis, down)  6.98 us
    slice x1, local copies, waits for them, and re-layouts, shards(): full_grad[:, 1::2]  6.6 us
    slice x1, local copies, waits for them, and re-layouts, shards(): full_grad[:, 0::2]  6.6 us
  transfers between devices with their start and end apart: 7, of which 4 were waited for; matrix products, arithmetic and copies ran while one was open for 16% of the time, Pallas kernels for 11%

profile of v7, /device:TPU:6, one launch (start us, length us, event | category | flops | bytes accessed | tf_op | source)
XLA Modules:
  0.0 138.9 jit_solution(644243109008049878)
XLA Ops:
  3.4 1.5 %fusion.21 = bf16[128,8,512]{2,1,0:T(8,128)(2,1)} fusion(bf16[256,512]{1,0:T(8,128)(2,1)S(1)} %constant_dynamic-update-slice_fusion, s32[1024]{0:T(1024)S(1)} %eq.75), kind=kOutput, calls=%fused_computation.20 | convolution fusion | flops 269221888 | bytes 1314816 | tf_op jit(solution)/shard_map/dot_general | solution.py:279
  4.9 15.9 %all-to-all-start = ((bf16[128,8,512]{2,1,0:T(8,128)(2,1)}), bf16[128,8,512]{2,1,0:T(8,128)(2,1)S(1)}, u32[]{:S(2)}, u32[]{:S(2)}) async-start(bf16[128,8,512]{2,1,0:T(8,128)(2,1)} %fusion.21), calls=%async_computation | async-start | bytes 2097152 | tf_op jit(solution)/shard_map/all_to_all | solution.py:283
  20.8 7.0 %collective-permute-start.1 = (bf16[256,512]{1,0:T(8,128)(2,1)S(1)}, bf16[256,512]{1,0:T(8,128)(2,1)S(1)}, u32[]{:S(2)}, u32[]{:S(2)}) collective-permute-start(bf16[256,512]{1,0:T(8,128)(2,1)S(1)} %constant_dynamic-update-slice_fusion), channel_id=1, source_target_pairs={{2,0},{4,2},{6,4},{8,6},{10,8},{12,10},{14,12},{16,14},{18,16},{20... | collective-permute-start | bytes 786440 | tf_op jit(solution)/shard_map/ppermute | solution.py:24
  27.8 1.9 %collective-permute-start = (bf16[256,512]{1,0:T(8,128)(2,1)S(1)}, bf16[256,512]{1,0:T(8,128)(2,1)S(1)}, u32[]{:S(2)}, u32[]{:S(2)}) collective-permute-start(bf16[256,512]{1,0:T(8,128)(2,1)S(1)} %constant_dynamic-update-slice_fusion), channel_id=1, source_target_pairs={{0,2},{2,4},{4,6},{6,8},{8,10},{10,12},{12,14},{14,16},{16,18},{18... | collective-permute-start | bytes 786440 | tf_op jit(solution)/shard_map/ppermute | solution.py:23
  29.8 2.2 %all_gather.3 = bf16[256,512]{1,0:T(8,128)(2,1)S(1)} all-gather(bf16[256,256]{1,0:T(8,128)(2,1)S(1)} %copy-done.1), channel_id=1, replica_groups=mesh['dom'=128,'head'=2] {'head'}, dimensions={1}, use_global_device_ids=true | all-gather | bytes 393216 | tf_op jit(solution)/shard_map/all_gather | solution.py:267
  32.0 6.6 %slice.65.refs_1_ = bf16[256,256]{1,0:T(8,128)(2,1)} slice(bf16[256,512]{1,0:T(8,128)(2,1)S(1)} %all_gather.3), slice={[0:256:1], [1:512:2]} | slice | bytes 262144 | tf_op jit(solution)/shard_map/slice | solution.py:305
  38.6 6.6 %slice.64.refs_0_ = bf16[256,256]{1,0:T(8,128)(2,1)} slice(bf16[256,512]{1,0:T(8,128)(2,1)S(1)} %all_gather.3), slice={[0:256:1], [0:512:2]} | slice | bytes 262144 | tf_op jit(solution)/shard_map/slice | solution.py:305
  46.7 1.2 collective-permute-done.1
  47.9 5.5 %collective-permute-done = bf16[256,512]{1,0:T(8,128)(2,1)S(1)} collective-permute-done((bf16[256,512]{1,0:T(8,128)(2,1)S(1)}, bf16[256,512]{1,0:T(8,128)(2,1)S(1)}, u32[]{:S(2)}, u32[]{:S(2)}) %collective-permute-start) | collective-permute-done | bytes 262176 | tf_op jit(solution)/shard_map/ppermute | solution.py:23
  54.4 1.9 %fusion.20 = bf16[768,512]{1,0:T(8,128)(2,1)} fusion(s32[768]{0:T(1024)S(1)} %eq.36, bf16[128,8,512]{2,1,0:T(8,128)(2,1)S(1)} %all-to-all-done), kind=kOutput, calls=%fused_computation.19 | convolution fusion | flops 806486016 | bytes 1838080 | tf_op jit(solution)/shard_map/dot_general | solution.py:290
  56.3 9.3 %shard_map.147 = (bf16[256,256]{1,0:T(8,128)(2,1)}, f32[1024,512]{1,0:T(8,128)}) custom-call(s32[8]{0:T(128)} %reshape.124.pos_ref, s32[2]{0:T(128)} %cnt_ref.3, f32[4]{0:T(128)} %bias_ref.3, bf16[256,256]{1,0:T(8,128)(2,1)} %q_ref.3, bf16[256,256]{1,0:T(8,128)(2,1)} %convolution_convert_fusion.1.do_ref, bf16[6,128,512]{2,1,0:T(8,128)(2,1)} %bitcast.28, ...), custom_call_target="tpu_custom_call" | custom-call | flops 805306368 | bytes 4194304 | tf_op jit(solution)/shard_map/pallas_call | solution.py:237
  65.6 3.3 %fusion.1 = f32[1280,512]{1,0:T(8,128)S(1)} fusion(s32[1280]{0:T(1024)S(1)} %get-tuple-element.58, s32[1024]{0:T(1024)S(1)} %concatenate.17, s32[1280]{0:T(1024)S(1)} %get-tuple-element.57, f32[1024,512]{1,0:T(8,128)} %get-tuple-element.52), kind=kOutput, calls=%fused_computation.2 | convolution fusion | flops 1347682304 | bytes 4732928 | tf_op jit(solution)/shard_map/dot_general | solution.py:334
  68.9 2.1 %fusion.9 = bf16[1280,512]{1,0:T(8,128)(2,1)S(1)} fusion(f32[1280,512]{1,0:T(8,128)S(1)} %fusion.1, s32[1280]{0:T(1024)S(1)} %get-tuple-element.58, s32[1024]{0:T(1024)S(1)} %concatenate.17, s32[1280]{0:T(1024)S(1)} %get-tuple-element.57, f32[1024,512]{1,0:T(8,128)S(1)} %copy-done.5), kind=kOutput, calls=%fused_computation.9 | convolution fusion | flops 1348468736 | bytes 6043648 | tf_op jit(solution)/shard_map/dot_general | solution.py:333
  71.0 1.6 %reshape.129 = bf16[128,10,512]{2,1,0:T(8,128)(2,1)} reshape(bf16[1280,512]{1,0:T(8,128)(2,1)S(1)} %fusion.9) | data formatting | bytes 2621440 | tf_op jit(solution)/shard_map/reshape | solution.py:335
  72.6 9.1 %all-to-all-start.1 = ((bf16[128,10,512]{2,1,0:T(8,128)(2,1)}), bf16[128,10,512]{2,1,0:T(8,128)(2,1)S(1)}, u32[]{:S(2)}, u32[]{:S(2)}) async-start(bf16[128,10,512]{2,1,0:T(8,128)(2,1)} %reshape.129), calls=%async_computation.1 | async-start | bytes 4194304 | tf_op jit(solution)/shard_map/all_to_all | solution.py:336
  82.7 14.7 %shard_map.148 = (bf16[256,256]{1,0:T(8,128)(2,1)}, f32[6,128,512]{2,1,0:T(8,128)}) custom-call(s32[8]{0:T(128)} %reshape.124.pos_ref, s32[2]{0:T(128)} %cnt_ref.3, f32[4]{0:T(128)} %bias_ref.3, bf16[256,256]{1,0:T(8,128)(2,1)} %q_ref.3, bf16[256,256]{1,0:T(8,128)(2,1)} %convolution_convert_fusion.1.do_ref, bf16[6,128,512]{2,1,0:T(8,128)(2,1)} %bitcast.29, ...), custom_call_target="tpu_custom_call" | custom-call | flops 1610612736 | bytes 4194304 | tf_op jit(solution)/shard_map/pallas_call | solution.py:237
  97.4 1.1 slice.66
  98.5 1.5 %convert.8 = bf16[6,128,512]{2,1,0:T(8,128)(2,1)S(1)} convert(f32[6,128,512]{2,1,0:T(8,128)} %get-tuple-element.51) | non-fusion elementwise | flops 393216 | bytes 2359296 | tf_op jit(solution)/shard_map/convert.3
  100.8 7.0 %collective-permute-start.4 = (bf16[256,512]{1,0:T(8,128)(2,1)}, bf16[256,512]{1,0:T(8,128)(2,1)}, u32[]{:S(2)}, u32[]{:S(2)}) collective-permute-start(bf16[256,512]{1,0:T(8,128)(2,1)} %bitcast.7), channel_id=1, source_target_pairs={{2,0},{4,2},{6,4},{8,6},{10,8},{12,10},{14,12},{16,14},{18,16},{20... | collective-permute-start | bytes 786440 | tf_op jit(solution)/shard_map/ppermute | solution.py:32
  107.8 1.9 %collective-permute-start.3 = (bf16[256,512]{1,0:T(8,128)(2,1)}, bf16[256,512]{1,0:T(8,128)(2,1)}, u32[]{:S(2)}, u32[]{:S(2)}) collective-permute-start(bf16[256,512]{1,0:T(8,128)(2,1)} %bitcast.6), channel_id=1, source_target_pairs={{0,2},{2,4},{4,6},{6,8},{8,10},{10,12},{12,14},{14,16},{16,18},{18... | collective-permute-start | bytes 786440 | tf_op jit(solution)/shard_map/ppermute | solution.py:32
  109.7 1.6 %add_convert_fusion = bf16[256,256]{1,0:T(8,128)(2,1)} fusion(f32[256,256]{1,0:T(8,128)} %collective-permute-done.2, f32[256,512]{1,0:T(8,128)S(1)} %fusion.46, s32[]{:T(128)S(6)} %select_n.51), kind=kLoop, calls=%fused_computation.35 | loop fusion | flops 131072 | bytes 655364 | tf_op jit(solution)/shard_map/convert_element_type | solution.py:350
  111.4 20.5 %all-to-all-done.1 = bf16[128,10,512]{2,1,0:T(8,128)(2,1)S(1)} async-done(((bf16[128,10,512]{2,1,0:T(8,128)(2,1)}), bf16[128,10,512]{2,1,0:T(8,128)(2,1)S(1)}, u32[]{:S(2)}, u32[]{:S(2)}) %all-to-all-start.1) | async-done | bytes 1310752 | tf_op jit(solution)/shard_map/all_to_all | solution.py:336
  132.8 3.8 %collective-permute-done.3 = bf16[256,512]{1,0:T(8,128)(2,1)} collective-permute-done((bf16[256,512]{1,0:T(8,128)(2,1)}, bf16[256,512]{1,0:T(8,128)(2,1)}, u32[]{:S(2)}, u32[]{:S(2)}) %collective-permute-start.3) | collective-permute-done | bytes 262176 | tf_op jit(solution)/shard_map/ppermute | solution.py:32
  136.7 1.5 %fusion.27 = bf16[256,512]{1,0:T(8,128)(2,1)S(1)} fusion(f32[2,128,512]{2,1,0:T(8,128)S(1)} %slice.66, bf16[256,512]{1,0:T(8,128)(2,1)} %collective-permute-done.4, bf16[256,512]{1,0:T(8,128)(2,1)} %collective-permute-done.3, bf16[128,10,512]{2,1,0:T(8,128)(2,1)S(1)} %all-to-all-done.1, s32[1024]{0:T(1024)S(1)} %eq.75), kind=kOutput, calls=%fused_computation.31 | convolution fusion | flops 269484032 | bytes 2363392 | tf_op jit(solution)/shard_map/dot_general | solution.py:342
  (33 shorter events, 8.7 us)
Async XLA Ops:
  0.6 45.2 %copy-start = (bf16[256,512]{1,0:T(8,128)(2,1)S(1)}, bf16[256,512]{1,0:T(8,128)(2,1)}, u32[]{:S(2)}) copy-start(bf16[256,512]{1,0:T(8,128)(2,1)} %param.21) | copy-start | bytes 786436
  0.6 29.1 %copy-start.4 = (s32[2,4]{1,0:T(2,128)S(1)}, s32[2,4]{1,0:T(2,128)}, u32[]{:S(2)}) copy-start(s32[2,4]{1,0:T(2,128)} %param.24) | copy-start | bytes 100
  0.7 29.1 %copy-start.1 = (bf16[256,256]{1,0:T(8,128)(2,1)S(1)}, bf16[256,256]{1,0:T(8,128)(2,1)}, u32[]{:S(2)}) copy-start(bf16[256,256]{1,0:T(8,128)(2,1)} %param.22) | copy-start | bytes 393220
  3.4 42.4 %copy-start.3 = (s32[256,3]{0,1:T(4,128)S(1)}, s32[256,3]{0,1:T(4,128)}, u32[]{:S(2)}) copy-start(s32[256,3]{0,1:T(4,128)} %param.27) | copy-start | bytes 9220
  4.9 49.5 %all-to-all-start = ((bf16[128,8,512]{2,1,0:T(8,128)(2,1)}), bf16[128,8,512]{2,1,0:T(8,128)(2,1)S(1)}, u32[]{:S(2)}, u32[]{:S(2)}) async-start(bf16[128,8,512]{2,1,0:T(8,128)(2,1)} %fusion.21), calls=%async_computation | async-start | bytes 2097152 | tf_op jit(solution)/shard_map/all_to_all | solution.py:283
  20.8 27.1 %collective-permute-start.1 = (bf16[256,512]{1,0:T(8,128)(2,1)S(1)}, bf16[256,512]{1,0:T(8,128)(2,1)S(1)}, u32[]{:S(2)}, u32[]{:S(2)}) collective-permute-start(bf16[256,512]{1,0:T(8,128)(2,1)S(1)} %constant_dynamic-update-slice_fusion), channel_id=1, source_target_pairs={{2,0},{4,2},{6,4},{8,6},{10,8},{12,10},{14,12},{16,14},{18,16},{20... | collective-permute-start | bytes 786440 | tf_op jit(solution)/shard_map/ppermute | solution.py:24
  27.8 25.6 %collective-permute-start = (bf16[256,512]{1,0:T(8,128)(2,1)S(1)}, bf16[256,512]{1,0:T(8,128)(2,1)S(1)}, u32[]{:S(2)}, u32[]{:S(2)}) collective-permute-start(bf16[256,512]{1,0:T(8,128)(2,1)S(1)} %constant_dynamic-update-slice_fusion), channel_id=1, source_target_pairs={{0,2},{2,4},{4,6},{6,8},{8,10},{10,12},{12,14},{14,16},{16,18},{18... | collective-permute-start | bytes 786440 | tf_op jit(solution)/shard_map/ppermute | solution.py:23
  65.6 3.3 %copy-start.5 = (f32[1024,512]{1,0:T(8,128)S(1)}, f32[1024,512]{1,0:T(8,128)}, u32[]{:S(2)}) copy-start(f32[1024,512]{1,0:T(8,128)} %get-tuple-element.52) | copy-start | bytes 6291460
  72.6 9.2 %copy-start.2 = (bf16[256,256]{1,0:T(8,128)(2,1)S(1)}, bf16[256,256]{1,0:T(8,128)(2,1)}, u32[]{:S(2)}) copy-start(bf16[256,256]{1,0:T(8,128)(2,1)} %get-tuple-element.49) | copy-start | bytes 393220
  72.6 59.4 %all-to-all-start.1 = ((bf16[128,10,512]{2,1,0:T(8,128)(2,1)}), bf16[128,10,512]{2,1,0:T(8,128)(2,1)S(1)}, u32[]{:S(2)}, u32[]{:S(2)}) async-start(bf16[128,10,512]{2,1,0:T(8,128)(2,1)} %reshape.129), calls=%async_computation.1 | async-start | bytes 4194304 | tf_op jit(solution)/shard_map/all_to_all | solution.py:336
  82.7 27.0 %collective-permute-start.2 = (f32[256,256]{1,0:T(8,128)}, f32[256,256]{1,0:T(8,128)}, u32[]{:S(2)}, u32[]{:S(2)}) collective-permute-start(f32[256,256]{1,0:T(8,128)} %constant_dynamic-slice_fusion), channel_id=1, source_target_pairs={{0,1},{1,0},{2,3},{3,2},{4,5},{5,4},{6,7},{7,6},{8,9},{9,8},{10,11... | collective-permute-start | bytes 786440 | tf_op jit(solution)/shard_map/ppermute | solution.py:349
  100.8 32.0 %collective-permute-start.4 = (bf16[256,512]{1,0:T(8,128)(2,1)}, bf16[256,512]{1,0:T(8,128)(2,1)}, u32[]{:S(2)}, u32[]{:S(2)}) collective-permute-start(bf16[256,512]{1,0:T(8,128)(2,1)} %bitcast.7), channel_id=1, source_target_pairs={{2,0},{4,2},{6,4},{8,6},{10,8},{12,10},{14,12},{16,14},{18,16},{20... | collective-permute-start | bytes 786440 | tf_op jit(solution)/shard_map/ppermute | solution.py:32
  107.8 28.9 %collective-permute-start.3 = (bf16[256,512]{1,0:T(8,128)(2,1)}, bf16[256,512]{1,0:T(8,128)(2,1)}, u32[]{:S(2)}, u32[]{:S(2)}) collective-permute-start(bf16[256,512]{1,0:T(8,128)(2,1)} %bitcast.6), channel_id=1, source_target_pairs={{0,2},{2,4},{4,6},{6,8},{8,10},{10,12},{12,14},{14,16},{16,18},{18... | collective-permute-start | bytes 786440 | tf_op jit(solution)/shard_map/ppermute | solution.py:32

commit v8 on v5

--- a/solution.py
+++ b/solution.py
@@ -129,7 +129,7 @@
     if near_out:
         qg_ref, eg_ref, acc = refs
     else:
-        attn_ref, fg_ref, acc = refs
+        mx_ref, st_ref, attn_ref, fg_ref, acc = refs
     cols = q_ref.shape[1]
     hs = cols // heads
     scale = hs ** (-0.5)
@@ -156,29 +156,41 @@
             dof = do.astype(f32)
             qh = jnp.where(mask, q, jnp.zeros_like(q))
             doh = jnp.where(mask, do, jnp.zeros_like(do))
-            keys = [ext_ref[pos[j], :, :cols] for j in range(kt)]
-            vals = [ext_ref[pos[j], :, cols:] for j in range(kt)]
-            live = [j < count for j in range(kt)]
-            s = [lax.dot_general(qh, keys[j], nt, preferred_element_type=f32) * scale for j in range(kt)]
             fk = [far_ref[e, rows, :cols].astype(f32) for e in range(DEG)]
             fv = [far_ref[e, rows, cols:].astype(f32) for e in range(DEG)]
             bias = bias_ref[h]
             fs = [jnp.sum(jnp.where(mask, qf * fk[e], 0.0), axis=1, keepdims=True) * scale + bias
                   for e in range(DEG)]
-            m = fs[0]
-            for e in range(1, DEG):
-                m = jnp.maximum(m, fs[e])
-            for j in range(kt):
-                m = jnp.maximum(m, jnp.where(live[j], jnp.max(s[j], axis=1, keepdims=True), -jnp.inf))
-            ne = [jnp.where(live[j], jnp.exp(s[j] - m), 0.0) for j in range(kt)]
-            fe = [jnp.exp(fs[e] - m) for e in range(DEG)]
-            row_sum = fe[0] + fe[1] + fe[2]
-            row_sum = jnp.sum(ne[0], axis=1, keepdims=True) + row_sum
-            for j in range(1, kt):
-                row_sum = row_sum + jnp.sum(ne[j], axis=1, keepdims=True)
-            mixed = jnp.dot(ne[0].astype(bf16), vals[0], preferred_element_type=f32)
-            for j in range(1, kt):
-                mixed = mixed + jnp.dot(ne[j].astype(bf16), vals[j], preferred_element_type=f32)
+            if near_out:
+                keys = [ext_ref[pos[j], :, :cols] for j in range(kt)]
+                vals = [ext_ref[pos[j], :, cols:] for j in range(kt)]
+                live = [j < count for j in range(kt)]
+                s = [lax.dot_general(qh, keys[j], nt, preferred_element_type=f32) * scale for j in range(kt)]
+                m = fs[0]
+                for e in range(1, DEG):
+                    m = jnp.maximum(m, fs[e])
+                for j in range(kt):
+                    m = jnp.maximum(m, jnp.where(live[j], jnp.max(s[j], axis=1, keepdims=True), -jnp.inf))
+                ne = [jnp.where(live[j], jnp.exp(s[j] - m), 0.0) for j in range(kt)]
+                fe = [jnp.exp(fs[e] - m) for e in range(DEG)]
+                row_sum = fe[0] + fe[1] + fe[2]
+                row_sum = jnp.sum(ne[0], axis=1, keepdims=True) + row_sum
+                for j in range(1, kt):
+                    row_sum = row_sum + jnp.sum(ne[j], axis=1, keepdims=True)
+                mixed = jnp.dot(ne[0].astype(bf16), vals[0], preferred_element_type=f32)
+                for j in range(1, kt):
+                    mixed = mixed + jnp.dot(ne[j].astype(bf16), vals[j], preferred_element_type=f32)
+            else:
+                colh = lax.broadcasted_iota(jnp.int32, (TILE, TILE), 1) == h
+                near_max = jnp.sum(jnp.where(colh, st_ref[0, rows, :], 0.0), axis=1, keepdims=True)
+                near_total = jnp.sum(jnp.where(colh, st_ref[1, rows, :], 0.0), axis=1, keepdims=True)
+                m = jnp.maximum(near_max, fs[0])
+                for e in range(1, DEG):
+                    m = jnp.maximum(m, fs[e])
+                rescale = jnp.exp(near_max - m)
+                fe = [jnp.exp(fs[e] - m) for e in range(DEG)]
+                row_sum = near_total * rescale + (fe[0] + fe[1] + fe[2])
+                mixed = mx_ref[rows, :] * rescale
             for e in range(DEG):
                 mixed = mixed + fe[e].astype(bf16).astype(f32) * fv[e]
             attn = (mixed / row_sum).astype(bf16).astype(f32)
@@ -216,7 +228,70 @@
         out_ref[rows, :] = acc[rows, :].astype(out_ref.dtype)
 
 
-def attention_tiles(near_out, pos, cnt, bias, q, do, ext, far):
+def _near_kernel(heads, kt, pos_ref, cnt_ref, q_ref, ext_ref, mx_ref, st_ref):
+    cols = q_ref.shape[1]
+    hs = cols // heads
+    scale = hs ** (-0.5)
+    n_tiles = q_ref.shape[0] // TILE
+    f32, bf16 = jnp.float32, jnp.bfloat16
+    mx_ref[...] = jnp.zeros(mx_ref.shape, f32)
+    st_ref[...] = jnp.zeros(st_ref.shape, f32)
+    lane = lax.broadcasted_iota(jnp.int32, (TILE, cols), 1)
+    col = lax.broadcasted_iota(jnp.int32, (TILE, TILE), 1)
+    nt = (((1,), (1,)), ((), ()))
+    for t in range(n_tiles):
+        rows = pl.ds(t * TILE, TILE)
+        count = cnt_ref[t]
+        pos = [pos_ref[t * kt + j] for j in range(kt)]
+
+        def head_body(h, carry):
+            mask = (lane >= h * hs) & (lane < (h + 1) * hs)
+            q = q_ref[rows, :]
+            qh = jnp.where(mask, q, jnp.zeros_like(q))
+            keys = [ext_ref[pos[j], :, :cols] for j in range(kt)]
+            vals = [ext_ref[pos[j], :, cols:] for j in range(kt)]
+            live = [j < count for j in range(kt)]
+            s = [lax.dot_general(qh, keys[j], nt, preferred_element_type=f32) * scale for j in range(kt)]
+            m = jnp.max(s[0], axis=1, keepdims=True)
+            for j in range(1, kt):
+                m = jnp.maximum(m, jnp.where(live[j], jnp.max(s[j], axis=1, keepdims=True), -jnp.inf))
+            ne = [jnp.where(live[j], jnp.exp(s[j] - m), 0.0) for j in range(kt)]
+            total = jnp.sum(ne[0], axis=1, keepdims=True)
+            for j in range(1, kt):
+                total = total + jnp.sum(ne[j], axis=1, keepdims=True)
+            mixed = jnp.dot(ne[0].astype(bf16), vals[0], preferred_element_type=f32)
+            for j in range(1, kt):
+                mixed = mixed + jnp.dot(ne[j].astype(bf16), vals[j], preferred_element_type=f32)
+            mx_ref[rows, :] += jnp.where(mask, mixed, 0.0)
+            st_ref[0, rows, :] = jnp.where(col == h, m, st_ref[0, rows, :])
+            st_ref[1, rows, :] = jnp.where(col == h, total, st_ref[1, rows, :])
+            return carry
+
+        lax.fori_loop(0, heads, head_body, 0)
+
+
+def near_tiles(pos, cnt, q, ext, heads):
+    kt = pos.shape[0] // cnt.shape[0]
+    n, cols = q.shape
+    smem = pl.BlockSpec(memory_space=pltpu.SMEM)
+    vmem = pl.BlockSpec(memory_space=pltpu.VMEM)
+    return pl.pallas_call(
+        functools.partial(_near_kernel, heads, kt),
+        out_shape=(
+            jax.ShapeDtypeStruct((n, cols), jnp.float32),
+            jax.ShapeDtypeStruct((2, n, TILE), jnp.float32),
+        ),
+        in_specs=[smem, smem, vmem, vmem],
+        out_specs=(vmem, vmem),
+        cost_estimate=pl.CostEstimate(
+            flops=int(2 * n * kt * TILE * cols * 2 * heads),
+            bytes_accessed=int(2 * 1024 * 1024),
+            transcendentals=int(n * heads * kt * TILE),
+        ),
+    )(pos, cnt, q, ext)
+
+
+def attention_tiles(near_out, pos, cnt, bias, q, do, ext, far, *near_stats):
     heads = bias.shape[0]
     kt = pos.shape[0] // cnt.shape[0]
     n, cols = q.shape
@@ -226,7 +301,7 @@
     return pl.pallas_call(
         functools.partial(_attn_kernel, heads, kt, near_out),
         out_shape=(jax.ShapeDtypeStruct((n, cols), jnp.bfloat16), grads),
-        in_specs=[smem, smem, smem, vmem, vmem, vmem, vmem],
+        in_specs=[smem, smem, smem] + [vmem] * (4 + len(near_stats)),
         out_specs=(vmem, vmem),
         scratch_shapes=[pltpu.VMEM((n, cols), jnp.float32)],
         cost_estimate=pl.CostEstimate(
@@ -234,7 +309,7 @@
             bytes_accessed=int(4 * 1024 * 1024),
             transcendentals=int(n * heads * (kt * TILE + DEG)),
         ),
-    )(pos, cnt, bias, q, do, ext, far)
+    )(pos, cnt, bias, q, do, ext, far, *near_stats)
 
 
 def shards(
@@ -290,7 +365,10 @@
         ext_tiles,
         far_all,
     )
-    attn_all, far_grad = attention_tiles(False, *kernel_args)
+    near_mixed, near_stats = near_tiles(
+        kernel_args[0], tile_count, query_rows, ext_tiles, far_bias.shape[0]
+    )
+    attn_all, far_grad = attention_tiles(False, *kernel_args, near_mixed, near_stats)
     qgrad_all, ext_grad = attention_tiles(True, *kernel_args)
     ext_grad = ext_grad.reshape(-1, 2 * col_width)
     attn_mine = attn_all.reshape(node_count, col_width)

time: 138 us -> 142 us (1.029)
  Pallas kernels: 23.5 us -> 27.8 us
    pallas_call x0 -> x1, Pallas kernels: none -> 6.7 us  [near_tiles(): pl.pallas_call(functools.partial(_near_kernel, heads, kt), out_shape=(jax...]
    pallas_call x2, Pallas kernels: 23.5 us -> 21.1 us  [attention_tiles(): pl.pallas_call(functools.partial(_attn_kernel, heads, kt, near_out), out_...]
  transfers between devices with their start and end apart: 7 -> 7, of which waited for: 4 -> 4; matrix products, arithmetic and copies ran while one was open for 7% -> 7% of each run, Pallas kernels for 11% -> 15%
where the time goes in v8:
time: 142 us; the launch traced here: 141 us
  waiting for transfers between devices  44.5 us (31%)
  starting transfers between devices  42.8 us (30%)
  Pallas kernels  27.8 us (20%)
  matrix products  9.27 us (7%)
  local copies, waits for them, and re-layouts  7.7 us (5%)
  other arithmetic  6.37 us (4%)
  blocking collectives  1.99 us (1%)
    pallas_call x2, Pallas kernels, attention_tiles(): pl.pallas_call(functools.partial(_attn_kernel, heads, kt, near_out), out_...  21.1 us
    all_to_all x1, waiting for transfers between devices, shards(): lax.all_to_all(both, 'dom', split_axis=0, concat_axis=0, tiled=True)  20.6 us
    all_to_all x1, starting transfers between devices, shards(): lax.all_to_all(outgoing, 'dom', split_axis=0, concat_axis=0, tiled=True)  15.9 us
    ppermute x1, waiting for transfers between devices, extended_2(): after = lax.ppermute(leading, axis, down)  14.6 us
    all_to_all x1, starting transfers between devices, shards(): lax.all_to_all(both, 'dom', split_axis=0, concat_axis=0, tiled=True)  9.14 us
    ppermute x2, starting transfers between devices, from_behind(): lax.ppermute(value, axis, [(source, source + steps) for source in range(l...  8.88 us
    ppermute x1, starting transfers between devices, extended_2(): after = lax.ppermute(leading, axis, down)  6.98 us
    pallas_call x1, Pallas kernels, near_tiles(): pl.pallas_call(functools.partial(_near_kernel, heads, kt), out_shape=(jax...  6.7 us
  transfers between devices with their start and end apart: 7, of which 4 were waited for; matrix products, arithmetic and copies ran while one was open for 7% of the time, Pallas kernels for 15%

profile of v8, /device:TPU:6, one launch (start us, length us, event | category | flops | bytes accessed | tf_op | source)
XLA Modules:
  0.0 141.4 jit_solution(7661237916999877438)
XLA Ops:
  3.4 1.5 %fusion.8 = bf16[128,8,512]{2,1,0:T(8,128)(2,1)} fusion(bf16[256,512]{1,0:T(8,128)(2,1)S(1)} %constant_dynamic-update-slice_fusion, s32[1024]{0:T(1024)S(1)} %eq.60), kind=kOutput, calls=%fused_computation.15 | convolution fusion | flops 269221888 | bytes 1314816 | tf_op jit(solution)/shard_map/dot_general | solution.py:343
  4.9 15.9 %all-to-all-start = ((bf16[128,8,512]{2,1,0:T(8,128)(2,1)}), bf16[128,8,512]{2,1,0:T(8,128)(2,1)S(1)}, u32[]{:S(2)}, u32[]{:S(2)}) async-start(bf16[128,8,512]{2,1,0:T(8,128)(2,1)} %fusion.8), calls=%async_computation | async-start | bytes 2097152 | tf_op jit(solution)/shard_map/all_to_all | solution.py:347
  20.8 7.0 %collective-permute-start.1 = (bf16[256,512]{1,0:T(8,128)(2,1)S(1)}, bf16[256,512]{1,0:T(8,128)(2,1)S(1)}, u32[]{:S(2)}, u32[]{:S(2)}) collective-permute-start(bf16[256,512]{1,0:T(8,128)(2,1)S(1)} %constant_dynamic-update-slice_fusion), channel_id=1, source_target_pairs={{2,0},{4,2},{6,4},{8,6},{10,8},{12,10},{14,12},{16,14},{18,16},{20... | collective-permute-start | bytes 786440 | tf_op jit(solution)/shard_map/ppermute | solution.py:24
  27.8 1.9 %collective-permute-start = (bf16[256,512]{1,0:T(8,128)(2,1)S(1)}, bf16[256,512]{1,0:T(8,128)(2,1)S(1)}, u32[]{:S(2)}, u32[]{:S(2)}) collective-permute-start(bf16[256,512]{1,0:T(8,128)(2,1)S(1)} %constant_dynamic-update-slice_fusion), channel_id=1, source_target_pairs={{0,2},{2,4},{4,6},{6,8},{8,10},{10,12},{12,14},{14,16},{16,18},{18... | collective-permute-start | bytes 786440 | tf_op jit(solution)/shard_map/ppermute | solution.py:23
  29.8 2.0 %all_gather.3 = bf16[256,512]{1,0:T(8,128)(2,1)S(1)} all-gather(bf16[256,256]{1,0:T(8,128)(2,1)S(1)} %copy-done.3), channel_id=1, replica_groups=mesh['dom'=128,'head'=2] {'head'}, dimensions={1}, use_global_device_ids=true | all-gather | bytes 393216 | tf_op jit(solution)/shard_map/all_gather | solution.py:331
  33.3 14.6 %collective-permute-done.1 = bf16[256,512]{1,0:T(8,128)(2,1)S(1)} collective-permute-done((bf16[256,512]{1,0:T(8,128)(2,1)S(1)}, bf16[256,512]{1,0:T(8,128)(2,1)S(1)}, u32[]{:S(2)}, u32[]{:S(2)}) %collective-permute-start.1) | collective-permute-done | bytes 262176 | tf_op jit(solution)/shard_map/ppermute | solution.py:24
  47.9 5.5 %collective-permute-done = bf16[256,512]{1,0:T(8,128)(2,1)S(1)} collective-permute-done((bf16[256,512]{1,0:T(8,128)(2,1)S(1)}, bf16[256,512]{1,0:T(8,128)(2,1)S(1)}, u32[]{:S(2)}, u32[]{:S(2)}) %collective-permute-start) | collective-permute-done | bytes 262176 | tf_op jit(solution)/shard_map/ppermute | solution.py:23
  54.4 6.7 %shard_map.147 = (f32[256,256]{1,0:T(8,128)}, f32[2,256,128]{2,1,0:T(8,128)}) custom-call(s32[8]{0:T(128)} %reshape.102.pos_ref, s32[2]{0:T(128)} %cnt_ref.5, bf16[256,256]{1,0:T(8,128)(2,1)} %q_ref.5, bf16[6,128,512]{2,1,0:T(8,128)(2,1)} %bitcast.39), custom_call_target="tpu_custom_call" | custom-call | flops 536870912 | bytes 2097152 | tf_op jit(solution)/shard_map/pallas_call | solution.py:278
  61.1 1.9 %fusion.7 = bf16[768,512]{1,0:T(8,128)(2,1)} fusion(s32[768]{0:T(1024)S(1)} %eq.56, bf16[128,8,512]{2,1,0:T(8,128)(2,1)S(1)} %all-to-all-done), kind=kOutput, calls=%fused_computation.14 | convolution fusion | flops 806486016 | bytes 1838080 | tf_op jit(solution)/shard_map/dot_general | solution.py:354
  63.0 6.4 %shard_map.148 = (bf16[256,256]{1,0:T(8,128)(2,1)}, f32[3,256,512]{2,1,0:T(8,128)}) custom-call(s32[8]{0:T(128)} %reshape.102.pos_ref, s32[2]{0:T(128)} %cnt_ref.5, f32[4]{0:T(128)} %bias_ref.3, bf16[256,256]{1,0:T(8,128)(2,1)} %q_ref.5, bf16[256,256]{1,0:T(8,128)(2,1)} %convolution_convert_fusion.2.do_ref, bf16[6,128,512]{2,1,0:T(8,128)(2,1)} %bitcast.40, ...), custom_call_target="tpu_custom_call" | custom-call | flops 805306368 | bytes 4194304 | tf_op jit(solution)/shard_map/pallas_call | solution.py:301
  69.5 1.3 fusion.10
  71.3 1.0 fusion
  72.3 1.0 fusion.9
  73.3 1.8 %pad_maximum_fusion = bf16[128,10,512]{2,1,0:T(8,128)(2,1)} fusion(bf16[128,2,512]{2,1,0:T(2,128)(2,1)S(1)} %reshape.109, bf16[128,8,512]{2,1,0:T(8,128)(2,1)S(1)} %fusion.9), kind=kLoop, calls=%fused_computation.7 | loop fusion | flops 2621440 | bytes 2621440 | tf_op jit(solution)/shard_map/concatenate | solution.py:394
  75.1 9.1 %all-to-all-start.1 = ((bf16[128,10,512]{2,1,0:T(8,128)(2,1)}), bf16[128,10,512]{2,1,0:T(8,128)(2,1)S(1)}, u32[]{:S(2)}, u32[]{:S(2)}) async-start(bf16[128,10,512]{2,1,0:T(8,128)(2,1)} %pad_maximum_fusion), calls=%async_computation.1 | async-start | bytes 4194304 | tf_op jit(solution)/shard_map/all_to_all | solution.py:397
  85.2 14.7 %shard_map.149 = (bf16[256,256]{1,0:T(8,128)(2,1)}, f32[6,128,512]{2,1,0:T(8,128)}) custom-call(s32[8]{0:T(128)} %reshape.102.pos_ref, s32[2]{0:T(128)} %cnt_ref.5, f32[4]{0:T(128)} %bias_ref.3, bf16[256,256]{1,0:T(8,128)(2,1)} %q_ref.5, bf16[256,256]{1,0:T(8,128)(2,1)} %convolution_convert_fusion.2.do_ref, bf16[6,128,512]{2,1,0:T(8,128)(2,1)} %bitcast.41, ...), custom_call_target="tpu_custom_call" | custom-call | flops 1610612736 | bytes 4194304 | tf_op jit(solution)/shard_map/pallas_call | solution.py:301
  99.9 1.1 slice.58
  101.0 1.5 %convert.17 = bf16[6,128,512]{2,1,0:T(8,128)(2,1)S(1)} convert(f32[6,128,512]{2,1,0:T(8,128)} %get-tuple-element.55) | non-fusion elementwise | flops 393216 | bytes 2359296 | tf_op jit(solution)/shard_map/convert.8
  103.3 7.0 %collective-permute-start.4 = (bf16[256,512]{1,0:T(8,128)(2,1)}, bf16[256,512]{1,0:T(8,128)(2,1)}, u32[]{:S(2)}, u32[]{:S(2)}) collective-permute-start(bf16[256,512]{1,0:T(8,128)(2,1)} %bitcast.7), channel_id=1, source_target_pairs={{2,0},{4,2},{6,4},{8,6},{10,8},{12,10},{14,12},{16,14},{18,16},{20... | collective-permute-start | bytes 786440 | tf_op jit(solution)/shard_map/ppermute | solution.py:32
  110.3 1.9 %collective-permute-start.3 = (bf16[256,512]{1,0:T(8,128)(2,1)}, bf16[256,512]{1,0:T(8,128)(2,1)}, u32[]{:S(2)}, u32[]{:S(2)}) collective-permute-start(bf16[256,512]{1,0:T(8,128)(2,1)} %bitcast.6), channel_id=1, source_target_pairs={{0,2},{2,4},{4,6},{6,8},{8,10},{10,12},{12,14},{14,16},{16,18},{18... | collective-permute-start | bytes 786440 | tf_op jit(solution)/shard_map/ppermute | solution.py:32
  112.2 1.6 %add_convert_fusion.1 = bf16[256,256]{1,0:T(8,128)(2,1)} fusion(f32[256,256]{1,0:T(8,128)} %collective-permute-done.2, f32[256,512]{1,0:T(8,128)S(1)} %fusion.20, s32[]{:T(128)S(6)} %select_n.6), kind=kLoop, calls=%fused_computation.33 | loop fusion | flops 131072 | bytes 655364 | tf_op jit(solution)/shard_map/convert_element_type | solution.py:411
  113.9 20.6 %all-to-all-done.1 = bf16[128,10,512]{2,1,0:T(8,128)(2,1)S(1)} async-done(((bf16[128,10,512]{2,1,0:T(8,128)(2,1)}), bf16[128,10,512]{2,1,0:T(8,128)(2,1)S(1)}, u32[]{:S(2)}, u32[]{:S(2)}) %all-to-all-start.1) | async-done | bytes 1310752 | tf_op jit(solution)/shard_map/all_to_all | solution.py:397
  135.3 3.8 %collective-permute-done.3 = bf16[256,512]{1,0:T(8,128)(2,1)} collective-permute-done((bf16[256,512]{1,0:T(8,128)(2,1)}, bf16[256,512]{1,0:T(8,128)(2,1)}, u32[]{:S(2)}, u32[]{:S(2)}) %collective-permute-start.3) | collective-permute-done | bytes 262176 | tf_op jit(solution)/shard_map/ppermute | solution.py:32
  139.2 1.5 %fusion.15 = bf16[256,512]{1,0:T(8,128)(2,1)S(1)} fusion(f32[2,128,512]{2,1,0:T(8,128)S(1)} %slice.58, bf16[256,512]{1,0:T(8,128)(2,1)} %collective-permute-done.4, bf16[256,512]{1,0:T(8,128)(2,1)} %collective-permute-done.3, bf16[128,10,512]{2,1,0:T(8,128)(2,1)S(1)} %all-to-all-done.1, s32[1024]{0:T(1024)S(1)} %eq.60), kind=kOutput, calls=%fused_computation.29 | convolution fusion | flops 269484032 | bytes 2363392 | tf_op jit(solution)/shard_map/dot_general | solution.py:403
  (34 shorter events, 9.2 us)
Async XLA Ops:
  0.6 31.8 %copy-start = (bf16[256,512]{1,0:T(8,128)(2,1)S(1)}, bf16[256,512]{1,0:T(8,128)(2,1)}, u32[]{:S(2)}) copy-start(bf16[256,512]{1,0:T(8,128)(2,1)} %param.21) | copy-start | bytes 786436
  0.6 29.1 %copy-start.5 = (s32[2,4]{1,0:T(2,128)S(1)}, s32[2,4]{1,0:T(2,128)}, u32[]{:S(2)}) copy-start(s32[2,4]{1,0:T(2,128)} %param.24) | copy-start | bytes 100
  0.7 29.1 %copy-start.3 = (bf16[256,256]{1,0:T(8,128)(2,1)S(1)}, bf16[256,256]{1,0:T(8,128)(2,1)}, u32[]{:S(2)}) copy-start(bf16[256,256]{1,0:T(8,128)(2,1)} %param.22) | copy-start | bytes 393220
  2.5 29.9 %copy-start.4 = (s32[256,3]{0,1:T(4,128)S(1)}, s32[256,3]{0,1:T(4,128)}, u32[]{:S(2)}) copy-start(s32[256,3]{0,1:T(4,128)} %param.27) | copy-start | bytes 9220
  4.9 56.2 %all-to-all-start = ((bf16[128,8,512]{2,1,0:T(8,128)(2,1)}), bf16[128,8,512]{2,1,0:T(8,128)(2,1)S(1)}, u32[]{:S(2)}, u32[]{:S(2)}) async-start(bf16[128,8,512]{2,1,0:T(8,128)(2,1)} %fusion.8), calls=%async_computation | async-start | bytes 2097152 | tf_op jit(solution)/shard_map/all_to_all | solution.py:347
  20.8 27.1 %collective-permute-start.1 = (bf16[256,512]{1,0:T(8,128)(2,1)S(1)}, bf16[256,512]{1,0:T(8,128)(2,1)S(1)}, u32[]{:S(2)}, u32[]{:S(2)}) collective-permute-start(bf16[256,512]{1,0:T(8,128)(2,1)S(1)} %constant_dynamic-update-slice_fusion), channel_id=1, source_target_pairs={{2,0},{4,2},{6,4},{8,6},{10,8},{12,10},{14,12},{16,14},{18,16},{20... | collective-permute-start | bytes 786440 | tf_op jit(solution)/shard_map/ppermute | solution.py:24
  27.8 25.6 %collective-permute-start = (bf16[256,512]{1,0:T(8,128)(2,1)S(1)}, bf16[256,512]{1,0:T(8,128)(2,1)S(1)}, u32[]{:S(2)}, u32[]{:S(2)}) collective-permute-start(bf16[256,512]{1,0:T(8,128)(2,1)S(1)} %constant_dynamic-update-slice_fusion), channel_id=1, source_target_pairs={{0,2},{2,4},{4,6},{6,8},{8,10},{10,12},{12,14},{14,16},{16,18},{18... | collective-permute-start | bytes 786440 | tf_op jit(solution)/shard_map/ppermute | solution.py:23
  69.5 1.6 %copy-start.1 = (f32[3,256,512]{2,1,0:T(8,128)S(1)}, f32[3,256,512]{2,1,0:T(8,128)}, u32[]{:S(2)}) copy-start(f32[3,256,512]{2,1,0:T(8,128)} %get-tuple-element.56) | copy-start | bytes 4718596
  75.1 9.2 %copy-start.2 = (bf16[256,256]{1,0:T(8,128)(2,1)S(1)}, bf16[256,256]{1,0:T(8,128)(2,1)}, u32[]{:S(2)}) copy-start(bf16[256,256]{1,0:T(8,128)(2,1)} %get-tuple-element.53) | copy-start | bytes 393220
  75.1 59.4 %all-to-all-start.1 = ((bf16[128,10,512]{2,1,0:T(8,128)(2,1)}), bf16[128,10,512]{2,1,0:T(8,128)(2,1)S(1)}, u32[]{:S(2)}, u32[]{:S(2)}) async-start(bf16[128,10,512]{2,1,0:T(8,128)(2,1)} %pad_maximum_fusion), calls=%async_computation.1 | async-start | bytes 4194304 | tf_op jit(solution)/shard_map/all_to_all | solution.py:397
  85.2 27.0 %collective-permute-start.2 = (f32[256,256]{1,0:T(8,128)}, f32[256,256]{1,0:T(8,128)}, u32[]{:S(2)}, u32[]{:S(2)}) collective-permute-start(f32[256,256]{1,0:T(8,128)} %constant_dynamic-slice_fusion), channel_id=1, source_target_pairs={{0,1},{1,0},{2,3},{3,2},{4,5},{5,4},{6,7},{7,6},{8,9},{9,8},{10,11... | collective-permute-start | bytes 786440 | tf_op jit(solution)/shard_map/ppermute | solution.py:410
  103.3 32.0 %collective-permute-start.4 = (bf16[256,512]{1,0:T(8,128)(2,1)}, bf16[256,512]{1,0:T(8,128)(2,1)}, u32[]{:S(2)}, u32[]{:S(2)}) collective-permute-start(bf16[256,512]{1,0:T(8,128)(2,1)} %bitcast.7), channel_id=1, source_target_pairs={{2,0},{4,2},{6,4},{8,6},{10,8},{12,10},{14,12},{16,14},{18,16},{20... | collective-permute-start | bytes 786440 | tf_op jit(solution)/shard_map/ppermute | solution.py:32
  110.3 28.9 %collective-permute-start.3 = (bf16[256,512]{1,0:T(8,128)(2,1)}, bf16[256,512]{1,0:T(8,128)(2,1)}, u32[]{:S(2)}, u32[]{:S(2)}) collective-permute-start(bf16[256,512]{1,0:T(8,128)(2,1)} %bitcast.6), channel_id=1, source_target_pairs={{0,2},{2,4},{4,6},{6,8},{8,10},{10,12},{12,14},{14,16},{16,18},{18... | collective-permute-start | bytes 786440 | tf_op jit(solution)/shard_map/ppermute | solution.py:32

commit v9 on v8

--- a/solution.py
+++ b/solution.py
@@ -1,5 +1,4 @@
 import functools
-import math
 
 import jax
 import jax.numpy as jnp
@@ -7,6 +6,7 @@
 from jax.experimental import pallas as pl
 from jax.experimental.pallas import tpu as pltpu
 from jax.sharding import PartitionSpec as P
+
 
 TILE = 128
 HALO = 2
@@ -30,99 +30,6 @@
     count = lax.axis_size(axis)
     leading, last = (max(0, -steps), min(count, count - steps))
     return lax.ppermute(value, axis, [(source, source + steps) for source in range(leading, last)])
-
-
-def rounded(values):
-    return lax.optimization_barrier(values.astype(jnp.bfloat16)).astype(jnp.float32)
-
-
-def tile_work(query_tile, grad_tile, tile_ids, live_count, far_tile, ext_tiles, bias, base_tile):
-    col_width = query_tile.shape[1]
-    heads_here = bias.shape[0]
-    head_size = col_width // heads_here
-    score_scale = head_size ** (-0.5)
-    key_block = ext_tiles[tile_ids - base_tile].reshape(-1, 2 * col_width)
-    near_keys = key_block[:, :col_width].reshape(-1, heads_here, head_size)
-    near_values = key_block[:, col_width:].reshape(-1, heads_here, head_size)
-    far_keys = far_tile[:, :, :col_width].reshape(TILE, -1, heads_here, head_size)
-    far_values = far_tile[:, :, col_width:].reshape(TILE, -1, heads_here, head_size)
-    queries = query_tile.reshape(TILE, heads_here, head_size)
-    upstream = grad_tile.reshape(TILE, heads_here, head_size)
-    live_keys = jnp.repeat(jnp.arange(tile_ids.shape[0]) < live_count, TILE)
-    near_score = (
-        jnp.einsum("qhd,khd->hqk", queries, near_keys, preferred_element_type=jnp.float32)
-        * score_scale
-    )
-    far_score = (
-        jnp.einsum("qhd,qehd->hqe", queries, far_keys, preferred_element_type=jnp.float32)
-        * score_scale
-        + bias[:, None, None]
-    )
-    row_max = jnp.maximum(
-        jnp.max(jnp.where(live_keys, near_score, -jnp.inf), axis=2), jnp.max(far_score, axis=2)
-    )
-    near_exp = jnp.where(live_keys, jnp.exp(near_score - row_max[:, :, None]), 0.0)
-    far_exp = jnp.exp(far_score - row_max[:, :, None])
-    row_sum = jnp.sum(near_exp, axis=2) + jnp.sum(far_exp, axis=2)
-    mixed = jnp.einsum(
-        "hqk,khd->qhd",
-        near_exp.astype(jnp.bfloat16),
-        near_values,
-        preferred_element_type=jnp.float32,
-    )
-    mixed = mixed + jnp.einsum(
-        "hqe,qehd->qhd",
-        far_exp.astype(jnp.bfloat16),
-        far_values,
-        preferred_element_type=jnp.float32,
-    )
-    attention = (mixed / row_sum.T[:, :, None]).astype(jnp.bfloat16)
-    delta_term = jnp.sum(
-        upstream.astype(jnp.float32) * rounded(mixed / row_sum.T[:, :, None]), axis=2
-    ).T
-    near_dprob = jnp.einsum(
-        "qhd,khd->hqk", upstream, near_values, preferred_element_type=jnp.float32
-    )
-    far_dprob = jnp.einsum(
-        "qhd,qehd->hqe", upstream, far_values, preferred_element_type=jnp.float32
-    )
-    near_prob = near_exp / row_sum[:, :, None]
-    far_prob = far_exp / row_sum[:, :, None]
-    near_dscore = (near_prob * (near_dprob - delta_term[:, :, None])).astype(jnp.bfloat16)
-    far_dscore = (far_prob * (far_dprob - delta_term[:, :, None])).astype(jnp.bfloat16)
-    query_grad = jnp.einsum(
-        "hqk,khd->qhd", near_dscore, near_keys, preferred_element_type=jnp.float32
-    )
-    query_grad = (
-        query_grad
-        + jnp.einsum("hqe,qehd->qhd", far_dscore, far_keys, preferred_element_type=jnp.float32)
-    ) * score_scale
-    near_kgrad = (
-        jnp.einsum("hqk,qhd->khd", near_dscore, queries, preferred_element_type=jnp.float32)
-        * score_scale
-    )
-    near_vgrad = jnp.einsum(
-        "hqk,qhd->khd", near_prob.astype(jnp.bfloat16), upstream, preferred_element_type=jnp.float32
-    )
-    far_kgrad = (
-        jnp.einsum("hqe,qhd->qehd", far_dscore, queries, preferred_element_type=jnp.float32)
-        * score_scale
-    )
-    far_vgrad = jnp.einsum(
-        "hqe,qhd->qehd", far_prob.astype(jnp.bfloat16), upstream, preferred_element_type=jnp.float32
-    )
-    near_grad = jnp.concatenate(
-        [near_kgrad.reshape(-1, col_width), near_vgrad.reshape(-1, col_width)], axis=1
-    )
-    far_grad = jnp.concatenate(
-        [far_kgrad.reshape(TILE, -1, col_width), far_vgrad.reshape(TILE, -1, col_width)], axis=2
-    )
-    return (
-        attention.reshape(TILE, col_width),
-        query_grad.astype(jnp.bfloat16).reshape(TILE, col_width),
-        near_grad,
-        far_grad,
-    )
 
 
 def _attn_kernel(heads, kt, near_out, pos_ref, cnt_ref, bias_ref, q_ref, do_ref, ext_ref, far_ref, *refs):
@@ -439,4 +346,5 @@
         P("dom", "head"),
         P("dom", "head"),
     )
+
     return jax.shard_map(shards, mesh=mesh, in_specs=in_specs, out_specs=out_specs, check_vma=False)

time: 142 us -> 142 us (level)
  no operation moved by 1% of the time
where the time goes in v9:
time: 142 us; the launch traced here: 141 us
  waiting for transfers between devices  44.5 us (31%)
  starting transfers between devices  42.8 us (30%)
  Pallas kernels  27.8 us (20%)
  matrix products  9.27 us (7%)
  local copies, waits for them, and re-layouts  7.7 us (5%)
  other arithmetic  6.37 us (4%)
  blocking collectives  1.99 us (1%)
    pallas_call x2, Pallas kernels, attention_tiles(): pl.pallas_call(functools.partial(_attn_kernel, heads, kt, near_out), out_...  21.1 us
    all_to_all x1, waiting for transfers between devices, shards(): lax.all_to_all(both, 'dom', split_axis=0, concat_axis=0, tiled=True)  20.6 us
    all_to_all x1, starting transfers between devices, shards(): lax.all_to_all(outgoing, 'dom', split_axis=0, concat_axis=0, tiled=True)  15.9 us
    ppermute x1, waiting for transfers between devices, extended_2(): after = lax.ppermute(leading, axis, down)  14.6 us
    all_to_all x1, starting transfers between devices, shards(): lax.all_to_all(both, 'dom', split_axis=0, concat_axis=0, tiled=True)  9.14 us
    ppermute x2, starting transfers between devices, from_behind(): lax.ppermute(value, axis, [(source, source + steps) for source in range(l...  8.88 us
    ppermute x1, starting transfers between devices, extended_2(): after = lax.ppermute(leading, axis, down)  6.98 us
    pallas_call x1, Pallas kernels, near_tiles(): pl.pallas_call(functools.partial(_near_kernel, heads, kt), out_shape=(jax...  6.7 us
  transfers between devices with their start and end apart: 7, of which 4 were waited for; matrix products, arithmetic and copies ran while one was open for 7% of the time, Pallas kernels for 15%

profile of v9, /device:TPU:6, one launch (start us, length us, event | category | flops | bytes accessed | tf_op | source)
XLA Modules:
  0.0 141.4 jit_solution(7661237916999877438)
XLA Ops:
  3.4 1.5 %fusion.8 = bf16[128,8,512]{2,1,0:T(8,128)(2,1)} fusion(bf16[256,512]{1,0:T(8,128)(2,1)S(1)} %constant_dynamic-update-slice_fusion, s32[1024]{0:T(1024)S(1)} %eq.60), kind=kOutput, calls=%fused_computation.15 | convolution fusion | flops 269221888 | bytes 1314816 | tf_op jit(solution)/shard_map/dot_general | solution.py:250
  4.9 15.9 %all-to-all-start = ((bf16[128,8,512]{2,1,0:T(8,128)(2,1)}), bf16[128,8,512]{2,1,0:T(8,128)(2,1)S(1)}, u32[]{:S(2)}, u32[]{:S(2)}) async-start(bf16[128,8,512]{2,1,0:T(8,128)(2,1)} %fusion.8), calls=%async_computation | async-start | bytes 2097152 | tf_op jit(solution)/shard_map/all_to_all | solution.py:254
  20.8 7.0 %collective-permute-start.1 = (bf16[256,512]{1,0:T(8,128)(2,1)S(1)}, bf16[256,512]{1,0:T(8,128)(2,1)S(1)}, u32[]{:S(2)}, u32[]{:S(2)}) collective-permute-start(bf16[256,512]{1,0:T(8,128)(2,1)S(1)} %constant_dynamic-update-slice_fusion), channel_id=1, source_target_pairs={{2,0},{4,2},{6,4},{8,6},{10,8},{12,10},{14,12},{16,14},{18,16},{20... | collective-permute-start | bytes 786440 | tf_op jit(solution)/shard_map/ppermute | solution.py:24
  27.8 1.9 %collective-permute-start = (bf16[256,512]{1,0:T(8,128)(2,1)S(1)}, bf16[256,512]{1,0:T(8,128)(2,1)S(1)}, u32[]{:S(2)}, u32[]{:S(2)}) collective-permute-start(bf16[256,512]{1,0:T(8,128)(2,1)S(1)} %constant_dynamic-update-slice_fusion), channel_id=1, source_target_pairs={{0,2},{2,4},{4,6},{6,8},{8,10},{10,12},{12,14},{14,16},{16,18},{18... | collective-permute-start | bytes 786440 | tf_op jit(solution)/shard_map/ppermute | solution.py:23
  29.8 2.0 %all_gather.3 = bf16[256,512]{1,0:T(8,128)(2,1)S(1)} all-gather(bf16[256,256]{1,0:T(8,128)(2,1)S(1)} %copy-done.3), channel_id=1, replica_groups=mesh['dom'=128,'head'=2] {'head'}, dimensions={1}, use_global_device_ids=true | all-gather | bytes 393216 | tf_op jit(solution)/shard_map/all_gather | solution.py:238
  33.3 14.6 %collective-permute-done.1 = bf16[256,512]{1,0:T(8,128)(2,1)S(1)} collective-permute-done((bf16[256,512]{1,0:T(8,128)(2,1)S(1)}, bf16[256,512]{1,0:T(8,128)(2,1)S(1)}, u32[]{:S(2)}, u32[]{:S(2)}) %collective-permute-start.1) | collective-permute-done | bytes 262176 | tf_op jit(solution)/shard_map/ppermute | solution.py:24
  47.9 5.5 %collective-permute-done = bf16[256,512]{1,0:T(8,128)(2,1)S(1)} collective-permute-done((bf16[256,512]{1,0:T(8,128)(2,1)S(1)}, bf16[256,512]{1,0:T(8,128)(2,1)S(1)}, u32[]{:S(2)}, u32[]{:S(2)}) %collective-permute-start) | collective-permute-done | bytes 262176 | tf_op jit(solution)/shard_map/ppermute | solution.py:23
  54.4 6.7 %shard_map.147 = (f32[256,256]{1,0:T(8,128)}, f32[2,256,128]{2,1,0:T(8,128)}) custom-call(s32[8]{0:T(128)} %reshape.102.pos_ref, s32[2]{0:T(128)} %cnt_ref.5, bf16[256,256]{1,0:T(8,128)(2,1)} %q_ref.5, bf16[6,128,512]{2,1,0:T(8,128)(2,1)} %bitcast.39), custom_call_target="tpu_custom_call" | custom-call | flops 536870912 | bytes 2097152 | tf_op jit(solution)/shard_map/pallas_call | solution.py:185
  61.1 1.9 %fusion.7 = bf16[768,512]{1,0:T(8,128)(2,1)} fusion(s32[768]{0:T(1024)S(1)} %eq.56, bf16[128,8,512]{2,1,0:T(8,128)(2,1)S(1)} %all-to-all-done), kind=kOutput, calls=%fused_computation.14 | convolution fusion | flops 806486016 | bytes 1838080 | tf_op jit(solution)/shard_map/dot_general | solution.py:261
  63.0 6.4 %shard_map.148 = (bf16[256,256]{1,0:T(8,128)(2,1)}, f32[3,256,512]{2,1,0:T(8,128)}) custom-call(s32[8]{0:T(128)} %reshape.102.pos_ref, s32[2]{0:T(128)} %cnt_ref.5, f32[4]{0:T(128)} %bias_ref.3, bf16[256,256]{1,0:T(8,128)(2,1)} %q_ref.5, bf16[256,256]{1,0:T(8,128)(2,1)} %convolution_convert_fusion.2.do_ref, bf16[6,128,512]{2,1,0:T(8,128)(2,1)} %bitcast.40, ...), custom_call_target="tpu_custom_call" | custom-call | flops 805306368 | bytes 4194304 | tf_op jit(solution)/shard_map/pallas_call | solution.py:208
  69.5 1.3 fusion.10
  71.3 1.0 fusion
  72.3 1.0 fusion.9
  73.3 1.8 %pad_maximum_fusion = bf16[128,10,512]{2,1,0:T(8,128)(2,1)} fusion(bf16[128,2,512]{2,1,0:T(2,128)(2,1)S(1)} %reshape.109, bf16[128,8,512]{2,1,0:T(8,128)(2,1)S(1)} %fusion.9), kind=kLoop, calls=%fused_computation.7 | loop fusion | flops 2621440 | bytes 2621440 | tf_op jit(solution)/shard_map/concatenate | solution.py:301
  75.1 9.1 %all-to-all-start.1 = ((bf16[128,10,512]{2,1,0:T(8,128)(2,1)}), bf16[128,10,512]{2,1,0:T(8,128)(2,1)S(1)}, u32[]{:S(2)}, u32[]{:S(2)}) async-start(bf16[128,10,512]{2,1,0:T(8,128)(2,1)} %pad_maximum_fusion), calls=%async_computation.1 | async-start | bytes 4194304 | tf_op jit(solution)/shard_map/all_to_all | solution.py:304
  85.2 14.7 %shard_map.149 = (bf16[256,256]{1,0:T(8,128)(2,1)}, f32[6,128,512]{2,1,0:T(8,128)}) custom-call(s32[8]{0:T(128)} %reshape.102.pos_ref, s32[2]{0:T(128)} %cnt_ref.5, f32[4]{0:T(128)} %bias_ref.3, bf16[256,256]{1,0:T(8,128)(2,1)} %q_ref.5, bf16[256,256]{1,0:T(8,128)(2,1)} %convolution_convert_fusion.2.do_ref, bf16[6,128,512]{2,1,0:T(8,128)(2,1)} %bitcast.41, ...), custom_call_target="tpu_custom_call" | custom-call | flops 1610612736 | bytes 4194304 | tf_op jit(solution)/shard_map/pallas_call | solution.py:208
  99.9 1.1 slice.58
  101.0 1.5 %convert.17 = bf16[6,128,512]{2,1,0:T(8,128)(2,1)S(1)} convert(f32[6,128,512]{2,1,0:T(8,128)} %get-tuple-element.55) | non-fusion elementwise | flops 393216 | bytes 2359296 | tf_op jit(solution)/shard_map/convert.8
  103.3 7.0 %collective-permute-start.4 = (bf16[256,512]{1,0:T(8,128)(2,1)}, bf16[256,512]{1,0:T(8,128)(2,1)}, u32[]{:S(2)}, u32[]{:S(2)}) collective-permute-start(bf16[256,512]{1,0:T(8,128)(2,1)} %bitcast.7), channel_id=1, source_target_pairs={{2,0},{4,2},{6,4},{8,6},{10,8},{12,10},{14,12},{16,14},{18,16},{20... | collective-permute-start | bytes 786440 | tf_op jit(solution)/shard_map/ppermute | solution.py:32
  110.3 1.9 %collective-permute-start.3 = (bf16[256,512]{1,0:T(8,128)(2,1)}, bf16[256,512]{1,0:T(8,128)(2,1)}, u32[]{:S(2)}, u32[]{:S(2)}) collective-permute-start(bf16[256,512]{1,0:T(8,128)(2,1)} %bitcast.6), channel_id=1, source_target_pairs={{0,2},{2,4},{4,6},{6,8},{8,10},{10,12},{12,14},{14,16},{16,18},{18... | collective-permute-start | bytes 786440 | tf_op jit(solution)/shard_map/ppermute | solution.py:32
  112.2 1.6 %add_convert_fusion.1 = bf16[256,256]{1,0:T(8,128)(2,1)} fusion(f32[256,256]{1,0:T(8,128)} %collective-permute-done.2, f32[256,512]{1,0:T(8,128)S(1)} %fusion.20, s32[]{:T(128)S(6)} %select_n.6), kind=kLoop, calls=%fused_computation.33 | loop fusion | flops 131072 | bytes 655364 | tf_op jit(solution)/shard_map/convert_element_type | solution.py:318
  113.9 20.6 %all-to-all-done.1 = bf16[128,10,512]{2,1,0:T(8,128)(2,1)S(1)} async-done(((bf16[128,10,512]{2,1,0:T(8,128)(2,1)}), bf16[128,10,512]{2,1,0:T(8,128)(2,1)S(1)}, u32[]{:S(2)}, u32[]{:S(2)}) %all-to-all-start.1) | async-done | bytes 1310752 | tf_op jit(solution)/shard_map/all_to_all | solution.py:304
  135.3 3.8 %collective-permute-done.3 = bf16[256,512]{1,0:T(8,128)(2,1)} collective-permute-done((bf16[256,512]{1,0:T(8,128)(2,1)}, bf16[256,512]{1,0:T(8,128)(2,1)}, u32[]{:S(2)}, u32[]{:S(2)}) %collective-permute-start.3) | collective-permute-done | bytes 262176 | tf_op jit(solution)/shard_map/ppermute | solution.py:32
  139.2 1.5 %fusion.15 = bf16[256,512]{1,0:T(8,128)(2,1)S(1)} fusion(f32[2,128,512]{2,1,0:T(8,128)S(1)} %slice.58, bf16[256,512]{1,0:T(8,128)(2,1)} %collective-permute-done.4, bf16[256,512]{1,0:T(8,128)(2,1)} %collective-permute-done.3, bf16[128,10,512]{2,1,0:T(8,128)(2,1)S(1)} %all-to-all-done.1, s32[1024]{0:T(1024)S(1)} %eq.60), kind=kOutput, calls=%fused_computation.29 | convolution fusion | flops 269484032 | bytes 2363392 | tf_op jit(solution)/shard_map/dot_general | solution.py:310
  (34 shorter events, 9.2 us)
Async XLA Ops:
  0.6 31.8 %copy-start = (bf16[256,512]{1,0:T(8,128)(2,1)S(1)}, bf16[256,512]{1,0:T(8,128)(2,1)}, u32[]{:S(2)}) copy-start(bf16[256,512]{1,0:T(8,128)(2,1)} %param.21) | copy-start | bytes 786436
  0.6 29.1 %copy-start.5 = (s32[2,4]{1,0:T(2,128)S(1)}, s32[2,4]{1,0:T(2,128)}, u32[]{:S(2)}) copy-start(s32[2,4]{1,0:T(2,128)} %param.24) | copy-start | bytes 100
  0.7 29.1 %copy-start.3 = (bf16[256,256]{1,0:T(8,128)(2,1)S(1)}, bf16[256,256]{1,0:T(8,128)(2,1)}, u32[]{:S(2)}) copy-start(bf16[256,256]{1,0:T(8,128)(2,1)} %param.22) | copy-start | bytes 393220
  2.5 29.9 %copy-start.4 = (s32[256,3]{0,1:T(4,128)S(1)}, s32[256,3]{0,1:T(4,128)}, u32[]{:S(2)}) copy-start(s32[256,3]{0,1:T(4,128)} %param.27) | copy-start | bytes 9220
  4.9 56.2 %all-to-all-start = ((bf16[128,8,512]{2,1,0:T(8,128)(2,1)}), bf16[128,8,512]{2,1,0:T(8,128)(2,1)S(1)}, u32[]{:S(2)}, u32[]{:S(2)}) async-start(bf16[128,8,512]{2,1,0:T(8,128)(2,1)} %fusion.8), calls=%async_computation | async-start | bytes 2097152 | tf_op jit(solution)/shard_map/all_to_all | solution.py:254
  20.8 27.1 %collective-permute-start.1 = (bf16[256,512]{1,0:T(8,128)(2,1)S(1)}, bf16[256,512]{1,0:T(8,128)(2,1)S(1)}, u32[]{:S(2)}, u32[]{:S(2)}) collective-permute-start(bf16[256,512]{1,0:T(8,128)(2,1)S(1)} %constant_dynamic-update-slice_fusion), channel_id=1, source_target_pairs={{2,0},{4,2},{6,4},{8,6},{10,8},{12,10},{14,12},{16,14},{18,16},{20... | collective-permute-start | bytes 786440 | tf_op jit(solution)/shard_map/ppermute | solution.py:24
  27.8 25.6 %collective-permute-start = (bf16[256,512]{1,0:T(8,128)(2,1)S(1)}, bf16[256,512]{1,0:T(8,128)(2,1)S(1)}, u32[]{:S(2)}, u32[]{:S(2)}) collective-permute-start(bf16[256,512]{1,0:T(8,128)(2,1)S(1)} %constant_dynamic-update-slice_fusion), channel_id=1, source_target_pairs={{0,2},{2,4},{4,6},{6,8},{8,10},{10,12},{12,14},{14,16},{16,18},{18... | collective-permute-start | bytes 786440 | tf_op jit(solution)/shard_map/ppermute | solution.py:23
  69.5 1.6 %copy-start.1 = (f32[3,256,512]{2,1,0:T(8,128)S(1)}, f32[3,256,512]{2,1,0:T(8,128)}, u32[]{:S(2)}) copy-start(f32[3,256,512]{2,1,0:T(8,128)} %get-tuple-element.56) | copy-start | bytes 4718596
  75.1 9.2 %copy-start.2 = (bf16[256,256]{1,0:T(8,128)(2,1)S(1)}, bf16[256,256]{1,0:T(8,128)(2,1)}, u32[]{:S(2)}) copy-start(bf16[256,256]{1,0:T(8,128)(2,1)} %get-tuple-element.53) | copy-start | bytes 393220
  75.1 59.4 %all-to-all-start.1 = ((bf16[128,10,512]{2,1,0:T(8,128)(2,1)}), bf16[128,10,512]{2,1,0:T(8,128)(2,1)S(1)}, u32[]{:S(2)}, u32[]{:S(2)}) async-start(bf16[128,10,512]{2,1,0:T(8,128)(2,1)} %pad_maximum_fusion), calls=%async_computation.1 | async-start | bytes 4194304 | tf_op jit(solution)/shard_map/all_to_all | solution.py:304
  85.2 27.0 %collective-permute-start.2 = (f32[256,256]{1,0:T(8,128)}, f32[256,256]{1,0:T(8,128)}, u32[]{:S(2)}, u32[]{:S(2)}) collective-permute-start(f32[256,256]{1,0:T(8,128)} %constant_dynamic-slice_fusion), channel_id=1, source_target_pairs={{0,1},{1,0},{2,3},{3,2},{4,5},{5,4},{6,7},{7,6},{8,9},{9,8},{10,11... | collective-permute-start | bytes 786440 | tf_op jit(solution)/shard_map/ppermute | solution.py:317
  103.3 32.0 %collective-permute-start.4 = (bf16[256,512]{1,0:T(8,128)(2,1)}, bf16[256,512]{1,0:T(8,128)(2,1)}, u32[]{:S(2)}, u32[]{:S(2)}) collective-permute-start(bf16[256,512]{1,0:T(8,128)(2,1)} %bitcast.7), channel_id=1, source_target_pairs={{2,0},{4,2},{6,4},{8,6},{10,8},{12,10},{14,12},{16,14},{18,16},{20... | collective-permute-start | bytes 786440 | tf_op jit(solution)/shard_map/ppermute | solution.py:32
  110.3 28.9 %collective-permute-start.3 = (bf16[256,512]{1,0:T(8,128)(2,1)}, bf16[256,512]{1,0:T(8,128)(2,1)}, u32[]{:S(2)}, u32[]{:S(2)}) collective-permute-start(bf16[256,512]{1,0:T(8,128)(2,1)} %bitcast.6), channel_id=1, source_target_pairs={{0,2},{2,4},{4,6},{6,8},{8,10},{10,12},{12,14},{14,16},{16,18},{18... | collective-permute-start | bytes 786440 | tf_op jit(solution)/shard_map/ppermute | solution.py:32

commit v10 on v9

--- a/solution.py
+++ b/solution.py
@@ -287,14 +287,12 @@
     own_grad = own_grad.at[:rim_rows].add(from_prev).at[node_count - rim_rows :].add(from_next)
     n_dom, cap = received.shape[0], received.shape[1]
     pair_grad = far_grad.reshape(-1, 2 * col_width)
-    pair_hi = lax.reduce_precision(pair_grad, exponent_bits=8, mantissa_bits=7)
-    pair_lo = (pair_grad - pair_hi).astype(jnp.bfloat16)
     slot_hit = (
         edge_slots.reshape(1, -1) == jnp.arange(n_dom * cap, dtype=jnp.int32)[:, None]
     ).astype(jnp.bfloat16)
     slot_grad = jnp.dot(
-        slot_hit, pair_hi.astype(jnp.bfloat16), preferred_element_type=jnp.float32
-    ) + jnp.dot(slot_hit, pair_lo, preferred_element_type=jnp.float32)
+        slot_hit, pair_grad.astype(jnp.bfloat16), preferred_element_type=jnp.float32
+    )
     weight_part = lax.dot_general(
         full_grad, attn_mine, (((0,), (0,)), ((), ())), preferred_element_type=jnp.float32
     ).reshape(n_dom, -1, 2 * col_width)

time: 142 us -> 142 us (level)
  local copies, waits for them, and re-layouts: 7.7 us -> 9.87 us
  matrix products: 9.27 us -> 7.3 us
    concatenate x0 -> x1, local copies, waits for them, and re-layouts: none -> 2.16 us  [shards(): jnp.concatenate([slot_grad.reshape(n_dom, cap, -1), weight_part], axis=1)]
    concatenate x1, other arithmetic: 1.79 us -> 0.12 us  [shards(): jnp.concatenate([slot_grad.reshape(n_dom, cap, -1), weight_part], axis=1)]
where the time goes in v10:
time: 142 us; the launch traced here: 141 us
  waiting for transfers between devices  44.5 us (31%)
  starting transfers between devices  42.8 us (30%)
  Pallas kernels  27.8 us (20%)
  local copies, waits for them, and re-layouts  9.87 us (7%)
  matrix products  7.3 us (5%)
  other arithmetic  6.03 us (4%)
  blocking collectives  1.99 us (1%)
    pallas_call x2, Pallas kernels, attention_tiles(): pl.pallas_call(functools.partial(_attn_kernel, heads, kt, near_out), out_...  21.1 us
    all_to_all x1, waiting for transfers between devices, shards(): lax.all_to_all(both, 'dom', split_axis=0, concat_axis=0, tiled=True)  20.6 us
    all_to_all x1, starting transfers between devices, shards(): lax.all_to_all(outgoing, 'dom', split_axis=0, concat_axis=0, tiled=True)  16 us
    ppermute x1, waiting for transfers between devices, extended_2(): after = lax.ppermute(leading, axis, down)  14.6 us
    all_to_all x1, starting transfers between devices, shards(): lax.all_to_all(both, 'dom', split_axis=0, concat_axis=0, tiled=True)  9.01 us
    ppermute x2, starting transfers between devices, from_behind(): lax.ppermute(value, axis, [(source, source + steps) for source in range(l...  8.89 us
    ppermute x1, starting transfers between devices, extended_2(): after = lax.ppermute(leading, axis, down)  6.98 us
    pallas_call x1, Pallas kernels, near_tiles(): pl.pallas_call(functools.partial(_near_kernel, heads, kt), out_shape=(jax...  6.71 us
  transfers between devices with their start and end apart: 7, of which 4 were waited for; matrix products, arithmetic and copies ran while one was open for 7% of the time, Pallas kernels for 15%

profile of v10, /device:TPU:6, one launch (start us, length us, event | category | flops | bytes accessed | tf_op | source)
XLA Modules:
  0.0 141.3 jit_solution(1690104042121357755)
XLA Ops:
  3.4 1.5 %fusion.10 = bf16[128,8,512]{2,1,0:T(8,128)(2,1)} fusion(bf16[256,512]{1,0:T(8,128)(2,1)S(1)} %constant_dynamic-update-slice_fusion, s32[1024]{0:T(1024)S(1)} %eq.71), kind=kOutput, calls=%fused_computation.10 | convolution fusion | flops 269221888 | bytes 1314816 | tf_op jit(solution)/shard_map/dot_general | solution.py:250
  4.9 16.0 %all-to-all-start = ((bf16[128,8,512]{2,1,0:T(8,128)(2,1)}), bf16[128,8,512]{2,1,0:T(8,128)(2,1)S(1)}, u32[]{:S(2)}, u32[]{:S(2)}) async-start(bf16[128,8,512]{2,1,0:T(8,128)(2,1)} %fusion.10), calls=%async_computation | async-start | bytes 2097152 | tf_op jit(solution)/shard_map/all_to_all | solution.py:254
  20.9 7.0 %collective-permute-start.1 = (bf16[256,512]{1,0:T(8,128)(2,1)S(1)}, bf16[256,512]{1,0:T(8,128)(2,1)S(1)}, u32[]{:S(2)}, u32[]{:S(2)}) collective-permute-start(bf16[256,512]{1,0:T(8,128)(2,1)S(1)} %constant_dynamic-update-slice_fusion), channel_id=1, source_target_pairs={{2,0},{4,2},{6,4},{8,6},{10,8},{12,10},{14,12},{16,14},{18,16},{20... | collective-permute-start | bytes 786440 | tf_op jit(solution)/shard_map/ppermute | solution.py:24
  27.9 1.9 %collective-permute-start = (bf16[256,512]{1,0:T(8,128)(2,1)S(1)}, bf16[256,512]{1,0:T(8,128)(2,1)S(1)}, u32[]{:S(2)}, u32[]{:S(2)}) collective-permute-start(bf16[256,512]{1,0:T(8,128)(2,1)S(1)} %constant_dynamic-update-slice_fusion), channel_id=1, source_target_pairs={{0,2},{2,4},{4,6},{6,8},{8,10},{10,12},{12,14},{14,16},{16,18},{18... | collective-permute-start | bytes 786440 | tf_op jit(solution)/shard_map/ppermute | solution.py:23
  29.9 2.0 %all_gather.3 = bf16[256,512]{1,0:T(8,128)(2,1)S(1)} all-gather(bf16[256,256]{1,0:T(8,128)(2,1)S(1)} %copy-done.2), channel_id=1, replica_groups=mesh['dom'=128,'head'=2] {'head'}, dimensions={1}, use_global_device_ids=true | all-gather | bytes 393216 | tf_op jit(solution)/shard_map/all_gather | solution.py:238
  33.4 14.6 %collective-permute-done.1 = bf16[256,512]{1,0:T(8,128)(2,1)S(1)} collective-permute-done((bf16[256,512]{1,0:T(8,128)(2,1)S(1)}, bf16[256,512]{1,0:T(8,128)(2,1)S(1)}, u32[]{:S(2)}, u32[]{:S(2)}) %collective-permute-start.1) | collective-permute-done | bytes 262176 | tf_op jit(solution)/shard_map/ppermute | solution.py:24
  48.0 5.5 %collective-permute-done = bf16[256,512]{1,0:T(8,128)(2,1)S(1)} collective-permute-done((bf16[256,512]{1,0:T(8,128)(2,1)S(1)}, bf16[256,512]{1,0:T(8,128)(2,1)S(1)}, u32[]{:S(2)}, u32[]{:S(2)}) %collective-permute-start) | collective-permute-done | bytes 262176 | tf_op jit(solution)/shard_map/ppermute | solution.py:23
  53.6 0.9 pad_maximum_fusion.1
  54.5 6.7 %shard_map.147 = (f32[256,256]{1,0:T(8,128)}, f32[2,256,128]{2,1,0:T(8,128)}) custom-call(s32[8]{0:T(128)} %reshape.116.pos_ref, s32[2]{0:T(128)} %cnt_ref.5, bf16[256,256]{1,0:T(8,128)(2,1)} %q_ref.5, bf16[6,128,512]{2,1,0:T(8,128)(2,1)} %bitcast.36), custom_call_target="tpu_custom_call" | custom-call | flops 536870912 | bytes 2097152 | tf_op jit(solution)/shard_map/pallas_call | solution.py:185
  61.2 1.9 %fusion.9 = bf16[768,512]{1,0:T(8,128)(2,1)} fusion(s32[768]{0:T(1024)S(1)} %eq.67, bf16[128,8,512]{2,1,0:T(8,128)(2,1)S(1)} %all-to-all-done), kind=kOutput, calls=%fused_computation.9 | convolution fusion | flops 806486016 | bytes 1838080 | tf_op jit(solution)/shard_map/dot_general | solution.py:261
  63.1 6.5 %shard_map.148 = (bf16[256,256]{1,0:T(8,128)(2,1)}, f32[3,256,512]{2,1,0:T(8,128)}) custom-call(s32[8]{0:T(128)} %reshape.116.pos_ref, s32[2]{0:T(128)} %cnt_ref.5, f32[4]{0:T(128)} %bias_ref.3, bf16[256,256]{1,0:T(8,128)(2,1)} %q_ref.5, bf16[256,256]{1,0:T(8,128)(2,1)} %convolution_convert_fusion.2.do_ref, bf16[6,128,512]{2,1,0:T(8,128)(2,1)} %bitcast.37, ...), custom_call_target="tpu_custom_call" | custom-call | flops 805306368 | bytes 4194304 | tf_op jit(solution)/shard_map/pallas_call | solution.py:208
  69.6 1.5 %convert_element_type.50 = bf16[3,256,512]{2,1,0:T(8,128)(2,1)S(1)} convert(f32[3,256,512]{2,1,0:T(8,128)} %get-tuple-element.56) | non-fusion elementwise | flops 393216 | bytes 2359296 | tf_op jit(solution)/shard_map/convert_element_type | solution.py:294
  71.8 1.0 fusion.6
  72.9 2.2 %copy.22 = bf16[128,10,512]{2,1,0:T(8,128)(2,1)} copy(bf16[128,10,512]{2,0,1:T(8,128)(2,1)S(1)} %pad_maximum_fusion) | data formatting | bytes 2621440 | tf_op jit(solution)/shard_map/concatenate | solution.py:299
  75.1 9.0 %all-to-all-start.1 = ((bf16[128,10,512]{2,1,0:T(8,128)(2,1)}), bf16[128,10,512]{2,1,0:T(8,128)(2,1)S(1)}, u32[]{:S(2)}, u32[]{:S(2)}) async-start(bf16[128,10,512]{2,1,0:T(8,128)(2,1)} %copy.22), calls=%async_computation.1 | async-start | bytes 4194304 | tf_op jit(solution)/shard_map/all_to_all | solution.py:302
  85.1 14.7 %shard_map.149 = (bf16[256,256]{1,0:T(8,128)(2,1)}, f32[6,128,512]{2,1,0:T(8,128)}) custom-call(s32[8]{0:T(128)} %reshape.116.pos_ref, s32[2]{0:T(128)} %cnt_ref.5, f32[4]{0:T(128)} %bias_ref.3, bf16[256,256]{1,0:T(8,128)(2,1)} %q_ref.5, bf16[256,256]{1,0:T(8,128)(2,1)} %convolution_convert_fusion.2.do_ref, bf16[6,128,512]{2,1,0:T(8,128)(2,1)} %bitcast.38, ...), custom_call_target="tpu_custom_call" | custom-call | flops 1610612736 | bytes 4194304 | tf_op jit(solution)/shard_map/pallas_call | solution.py:208
  99.7 1.1 slice.58
  100.8 1.5 %convert.16 = bf16[6,128,512]{2,1,0:T(8,128)(2,1)S(1)} convert(f32[6,128,512]{2,1,0:T(8,128)} %get-tuple-element.55) | non-fusion elementwise | flops 393216 | bytes 2359296 | tf_op jit(solution)/shard_map/convert.7
  103.2 7.0 %collective-permute-start.4 = (bf16[256,512]{1,0:T(8,128)(2,1)}, bf16[256,512]{1,0:T(8,128)(2,1)}, u32[]{:S(2)}, u32[]{:S(2)}) collective-permute-start(bf16[256,512]{1,0:T(8,128)(2,1)} %bitcast.7), channel_id=1, source_target_pairs={{2,0},{4,2},{6,4},{8,6},{10,8},{12,10},{14,12},{16,14},{18,16},{20... | collective-permute-start | bytes 786440 | tf_op jit(solution)/shard_map/ppermute | solution.py:32
  110.2 1.9 %collective-permute-start.3 = (bf16[256,512]{1,0:T(8,128)(2,1)}, bf16[256,512]{1,0:T(8,128)(2,1)}, u32[]{:S(2)}, u32[]{:S(2)}) collective-permute-start(bf16[256,512]{1,0:T(8,128)(2,1)} %bitcast.6), channel_id=1, source_target_pairs={{0,2},{2,4},{4,6},{6,8},{8,10},{10,12},{12,14},{14,16},{16,18},{18... | collective-permute-start | bytes 786440 | tf_op jit(solution)/shard_map/ppermute | solution.py:32
  112.1 1.6 %add_convert_fusion = bf16[256,256]{1,0:T(8,128)(2,1)} fusion(f32[256,256]{1,0:T(8,128)} %collective-permute-done.2, f32[256,512]{1,0:T(8,128)S(1)} %fusion.21, s32[]{:T(128)S(6)} %select_n.6), kind=kLoop, calls=%fused_computation.28 | loop fusion | flops 131072 | bytes 655364 | tf_op jit(solution)/shard_map/convert_element_type | solution.py:316
  113.7 20.6 %all-to-all-done.1 = bf16[128,10,512]{2,1,0:T(8,128)(2,1)S(1)} async-done(((bf16[128,10,512]{2,1,0:T(8,128)(2,1)}), bf16[128,10,512]{2,1,0:T(8,128)(2,1)S(1)}, u32[]{:S(2)}, u32[]{:S(2)}) %all-to-all-start.1) | async-done | bytes 1310752 | tf_op jit(solution)/shard_map/all_to_all | solution.py:302
  135.2 3.8 %collective-permute-done.3 = bf16[256,512]{1,0:T(8,128)(2,1)} collective-permute-done((bf16[256,512]{1,0:T(8,128)(2,1)}, bf16[256,512]{1,0:T(8,128)(2,1)}, u32[]{:S(2)}, u32[]{:S(2)}) %collective-permute-start.3) | collective-permute-done | bytes 262176 | tf_op jit(solution)/shard_map/ppermute | solution.py:32
  139.0 1.5 %fusion.16 = bf16[256,512]{1,0:T(8,128)(2,1)S(1)} fusion(f32[2,128,512]{2,1,0:T(8,128)S(1)} %slice.58, bf16[256,512]{1,0:T(8,128)(2,1)} %collective-permute-done.4, bf16[256,512]{1,0:T(8,128)(2,1)} %collective-permute-done.3, bf16[128,10,512]{2,1,0:T(8,128)(2,1)S(1)} %all-to-all-done.1, s32[1024]{0:T(1024)S(1)} %eq.71), kind=kOutput, calls=%fused_computation.24 | convolution fusion | flops 269484032 | bytes 2363392 | tf_op jit(solution)/shard_map/dot_general | solution.py:308
  (34 shorter events, 8.4 us)
Async XLA Ops:
  0.6 31.9 %copy-start = (bf16[256,512]{1,0:T(8,128)(2,1)S(1)}, bf16[256,512]{1,0:T(8,128)(2,1)}, u32[]{:S(2)}) copy-start(bf16[256,512]{1,0:T(8,128)(2,1)} %param.21) | copy-start | bytes 786436
  3.4 26.5 %copy-start.4 = (s32[2,4]{1,0:T(2,128)S(1)}, s32[2,4]{1,0:T(2,128)}, u32[]{:S(2)}) copy-start(s32[2,4]{1,0:T(2,128)} %param.24) | copy-start | bytes 100
  3.4 26.5 %copy-start.2 = (bf16[256,256]{1,0:T(8,128)(2,1)S(1)}, bf16[256,256]{1,0:T(8,128)(2,1)}, u32[]{:S(2)}) copy-start(bf16[256,256]{1,0:T(8,128)(2,1)} %param.22) | copy-start | bytes 393220
  4.9 27.6 %copy-start.3 = (s32[256,3]{0,1:T(4,128)S(1)}, s32[256,3]{0,1:T(4,128)}, u32[]{:S(2)}) copy-start(s32[256,3]{0,1:T(4,128)} %param.27) | copy-start | bytes 9220
  4.9 56.3 %all-to-all-start = ((bf16[128,8,512]{2,1,0:T(8,128)(2,1)}), bf16[128,8,512]{2,1,0:T(8,128)(2,1)S(1)}, u32[]{:S(2)}, u32[]{:S(2)}) async-start(bf16[128,8,512]{2,1,0:T(8,128)(2,1)} %fusion.10), calls=%async_computation | async-start | bytes 2097152 | tf_op jit(solution)/shard_map/all_to_all | solution.py:254
  20.9 27.1 %collective-permute-start.1 = (bf16[256,512]{1,0:T(8,128)(2,1)S(1)}, bf16[256,512]{1,0:T(8,128)(2,1)S(1)}, u32[]{:S(2)}, u32[]{:S(2)}) collective-permute-start(bf16[256,512]{1,0:T(8,128)(2,1)S(1)} %constant_dynamic-update-slice_fusion), channel_id=1, source_target_pairs={{2,0},{4,2},{6,4},{8,6},{10,8},{12,10},{14,12},{16,14},{18,16},{20... | collective-permute-start | bytes 786440 | tf_op jit(solution)/shard_map/ppermute | solution.py:24
  27.9 25.6 %collective-permute-start = (bf16[256,512]{1,0:T(8,128)(2,1)S(1)}, bf16[256,512]{1,0:T(8,128)(2,1)S(1)}, u32[]{:S(2)}, u32[]{:S(2)}) collective-permute-start(bf16[256,512]{1,0:T(8,128)(2,1)S(1)} %constant_dynamic-update-slice_fusion), channel_id=1, source_target_pairs={{0,2},{2,4},{4,6},{6,8},{8,10},{10,12},{12,14},{14,16},{16,18},{18... | collective-permute-start | bytes 786440 | tf_op jit(solution)/shard_map/ppermute | solution.py:23
  69.6 1.6 %copy-start.1 = (bf16[256,256]{1,0:T(8,128)(2,1)S(1)}, bf16[256,256]{1,0:T(8,128)(2,1)}, u32[]{:S(2)}) copy-start(bf16[256,256]{1,0:T(8,128)(2,1)} %get-tuple-element.53) | copy-start | bytes 393220
  75.1 59.3 %all-to-all-start.1 = ((bf16[128,10,512]{2,1,0:T(8,128)(2,1)}), bf16[128,10,512]{2,1,0:T(8,128)(2,1)S(1)}, u32[]{:S(2)}, u32[]{:S(2)}) async-start(bf16[128,10,512]{2,1,0:T(8,128)(2,1)} %copy.22), calls=%async_computation.1 | async-start | bytes 4194304 | tf_op jit(solution)/shard_map/all_to_all | solution.py:302
  85.1 27.0 %collective-permute-start.2 = (f32[256,256]{1,0:T(8,128)}, f32[256,256]{1,0:T(8,128)}, u32[]{:S(2)}, u32[]{:S(2)}) collective-permute-start(f32[256,256]{1,0:T(8,128)} %constant_dynamic-slice_fusion), channel_id=1, source_target_pairs={{0,1},{1,0},{2,3},{3,2},{4,5},{5,4},{6,7},{7,6},{8,9},{9,8},{10,11... | collective-permute-start | bytes 786440 | tf_op jit(solution)/shard_map/ppermute | solution.py:315
  103.2 32.0 %collective-permute-start.4 = (bf16[256,512]{1,0:T(8,128)(2,1)}, bf16[256,512]{1,0:T(8,128)(2,1)}, u32[]{:S(2)}, u32[]{:S(2)}) collective-permute-start(bf16[256,512]{1,0:T(8,128)(2,1)} %bitcast.7), channel_id=1, source_target_pairs={{2,0},{4,2},{6,4},{8,6},{10,8},{12,10},{14,12},{16,14},{18,16},{20... | collective-permute-start | bytes 786440 | tf_op jit(solution)/shard_map/ppermute | solution.py:32
  110.2 28.9 %collective-permute-start.3 = (bf16[256,512]{1,0:T(8,128)(2,1)}, bf16[256,512]{1,0:T(8,128)(2,1)}, u32[]{:S(2)}, u32[]{:S(2)}) collective-permute-start(bf16[256,512]{1,0:T(8,128)(2,1)} %bitcast.6), channel_id=1, source_target_pairs={{0,2},{2,4},{4,6},{6,8},{8,10},{10,12},{12,14},{14,16},{16,18},{18... | collective-permute-start | bytes 786440 | tf_op jit(solution)/shard_map/ppermute | solution.py:32

commit v11 on v9

--- a/solution.py
+++ b/solution.py
@@ -302,12 +302,14 @@
         [slot_grad.reshape(n_dom, cap, -1), weight_part], axis=1
     ).astype(jnp.bfloat16)
     both_back = lax.all_to_all(both, "dom", split_axis=0, concat_axis=0, tiled=True)
-    returned = both_back[:, :cap].reshape(-1, 2 * col_width)
     weight_sum = jnp.sum(both_back[:, cap:].astype(jnp.float32), axis=0)
     row_hit = (
-        send_rows[0].reshape(1, -1) == jnp.arange(node_count, dtype=jnp.int32)[:, None]
-    ).astype(jnp.bfloat16)
-    own_grad = own_grad + jnp.dot(row_hit, returned, preferred_element_type=jnp.float32)
+        jnp.pad(send_rows[0], ((0, 0), (0, both_back.shape[1] - cap)), constant_values=-1)[None]
+        == jnp.arange(node_count, dtype=jnp.int32)[:, None, None]
+    ).astype(jnp.bfloat16)
+    own_grad = own_grad + lax.dot_general(
+        row_hit, both_back, (((1, 2), (0, 1)), ((), ())), preferred_element_type=jnp.float32
+    )
     key_grad = own_grad[:, :col_width].astype(jnp.bfloat16)
     value_grad = own_grad[:, col_width:].astype(jnp.bfloat16)
     partial_out = jnp.dot(attn_mine, out_weight, preferred_element_type=jnp.float32)

time: 142 us -> 144 us (1.014)
    ppermute x2, waiting for transfers between devices: 3.82 us -> 25.3 us  [from_behind(): lax.ppermute(value, axis, [(source, source + steps) for source in range(l...]
    all_to_all x1, waiting for transfers between devices: 20.6 us -> 0.01 us  [shards(): lax.all_to_all(both, 'dom', split_axis=0, concat_axis=0, tiled=True)]
  transfers between devices with their start and end apart: 7 -> 7, of which waited for: 4 -> 4; matrix products, arithmetic and copies ran while one was open for 7% -> 6% of each run, Pallas kernels for 15% -> 15%
where the time goes in v11:
time: 144 us
  waiting for transfers between devices  45.4 us (32%)
  starting transfers between devices  42.8 us (30%)
  Pallas kernels  27.8 us (19%)
  matrix products  10.5 us (7%)
  local copies, waits for them, and re-layouts  7.68 us (5%)
  other arithmetic  6.38 us (4%)
  blocking collectives  1.99 us (1%)
    ppermute x2, waiting for transfers between devices, from_behind(): lax.ppermute(value, axis, [(source, source + steps) for source in range(l...  25.3 us
    pallas_call x2, Pallas kernels, attention_tiles(): pl.pallas_call(functools.partial(_attn_kernel, heads, kt, near_out), out_...  21.1 us
    all_to_all x1, starting transfers between devices, shards(): lax.all_to_all(outgoing, 'dom', split_axis=0, concat_axis=0, tiled=True)  15.9 us
    ppermute x1, waiting for transfers between devices, extended_2(): after = lax.ppermute(leading, axis, down)  14.6 us
    all_to_all x1, starting transfers between devices, shards(): lax.all_to_all(both, 'dom', split_axis=0, concat_axis=0, tiled=True)  9.14 us
    ppermute x2, starting transfers between devices, from_behind(): lax.ppermute(value, axis, [(source, source + steps) for source in range(l...  8.89 us
    ppermute x1, starting transfers between devices, extended_2(): after = lax.ppermute(leading, axis, down)  6.98 us
    pallas_call x1, Pallas kernels, near_tiles(): pl.pallas_call(functools.partial(_near_kernel, heads, kt), out_shape=(jax...  6.71 us
  transfers between devices with their start and end apart: 7, of which 4 were waited for; matrix products, arithmetic and copies ran while one was open for 6% of the time, Pallas kernels for 15%

profile of v11, /device:TPU:6, one launch (start us, length us, event | category | flops | bytes accessed | tf_op | source)
XLA Modules:
  0.0 143.5 jit_solution(5178737773384195728)
XLA Ops:
  3.4 1.5 %fusion.8 = bf16[128,8,512]{2,1,0:T(8,128)(2,1)} fusion(bf16[256,512]{1,0:T(8,128)(2,1)S(1)} %constant_dynamic-update-slice_fusion, s32[1024]{0:T(1024)S(1)} %eq.60), kind=kOutput, calls=%fused_computation.15 | convolution fusion | flops 269221888 | bytes 1314816 | tf_op jit(solution)/shard_map/dot_general | solution.py:250
  4.9 15.9 %all-to-all-start = ((bf16[128,8,512]{2,1,0:T(8,128)(2,1)}), bf16[128,8,512]{2,1,0:T(8,128)(2,1)S(1)}, u32[]{:S(2)}, u32[]{:S(2)}) async-start(bf16[128,8,512]{2,1,0:T(8,128)(2,1)} %fusion.8), calls=%async_computation | async-start | bytes 2097152 | tf_op jit(solution)/shard_map/all_to_all | solution.py:254
  20.8 7.0 %collective-permute-start.1 = (bf16[256,512]{1,0:T(8,128)(2,1)S(1)}, bf16[256,512]{1,0:T(8,128)(2,1)S(1)}, u32[]{:S(2)}, u32[]{:S(2)}) collective-permute-start(bf16[256,512]{1,0:T(8,128)(2,1)S(1)} %constant_dynamic-update-slice_fusion), channel_id=1, source_target_pairs={{2,0},{4,2},{6,4},{8,6},{10,8},{12,10},{14,12},{16,14},{18,16},{20... | collective-permute-start | bytes 786440 | tf_op jit(solution)/shard_map/ppermute | solution.py:24
  27.8 1.9 %collective-permute-start = (bf16[256,512]{1,0:T(8,128)(2,1)S(1)}, bf16[256,512]{1,0:T(8,128)(2,1)S(1)}, u32[]{:S(2)}, u32[]{:S(2)}) collective-permute-start(bf16[256,512]{1,0:T(8,128)(2,1)S(1)} %constant_dynamic-update-slice_fusion), channel_id=1, source_target_pairs={{0,2},{2,4},{4,6},{6,8},{8,10},{10,12},{12,14},{14,16},{16,18},{18... | collective-permute-start | bytes 786440 | tf_op jit(solution)/shard_map/ppermute | solution.py:23
  29.8 2.0 %all_gather.3 = bf16[256,512]{1,0:T(8,128)(2,1)S(1)} all-gather(bf16[256,256]{1,0:T(8,128)(2,1)S(1)} %copy-done.3), channel_id=1, replica_groups=mesh['dom'=128,'head'=2] {'head'}, dimensions={1}, use_global_device_ids=true | all-gather | bytes 393216 | tf_op jit(solution)/shard_map/all_gather | solution.py:238
  33.3 14.6 %collective-permute-done.1 = bf16[256,512]{1,0:T(8,128)(2,1)S(1)} collective-permute-done((bf16[256,512]{1,0:T(8,128)(2,1)S(1)}, bf16[256,512]{1,0:T(8,128)(2,1)S(1)}, u32[]{:S(2)}, u32[]{:S(2)}) %collective-permute-start.1) | collective-permute-done | bytes 262176 | tf_op jit(solution)/shard_map/ppermute | solution.py:24
  47.9 5.5 %collective-permute-done = bf16[256,512]{1,0:T(8,128)(2,1)S(1)} collective-permute-done((bf16[256,512]{1,0:T(8,128)(2,1)S(1)}, bf16[256,512]{1,0:T(8,128)(2,1)S(1)}, u32[]{:S(2)}, u32[]{:S(2)}) %collective-permute-start) | collective-permute-done | bytes 262176 | tf_op jit(solution)/shard_map/ppermute | solution.py:23
  54.4 6.7 %shard_map.147 = (f32[256,256]{1,0:T(8,128)}, f32[2,256,128]{2,1,0:T(8,128)}) custom-call(s32[8]{0:T(128)} %reshape.99.pos_ref, s32[2]{0:T(128)} %cnt_ref.5, bf16[256,256]{1,0:T(8,128)(2,1)} %q_ref.5, bf16[6,128,512]{2,1,0:T(8,128)(2,1)} %bitcast.37), custom_call_target="tpu_custom_call" | custom-call | flops 536870912 | bytes 2097152 | tf_op jit(solution)/shard_map/pallas_call | solution.py:185
  61.1 1.9 %fusion.7 = bf16[768,512]{1,0:T(8,128)(2,1)} fusion(s32[768]{0:T(1024)S(1)} %eq.56, bf16[128,8,512]{2,1,0:T(8,128)(2,1)S(1)} %all-to-all-done), kind=kOutput, calls=%fused_computation.14 | convolution fusion | flops 806486016 | bytes 1838080 | tf_op jit(solution)/shard_map/dot_general | solution.py:261
  63.0 6.5 %shard_map.148 = (bf16[256,256]{1,0:T(8,128)(2,1)}, f32[3,256,512]{2,1,0:T(8,128)}) custom-call(s32[8]{0:T(128)} %reshape.99.pos_ref, s32[2]{0:T(128)} %cnt_ref.5, f32[4]{0:T(128)} %bias_ref.3, bf16[256,256]{1,0:T(8,128)(2,1)} %q_ref.5, bf16[256,256]{1,0:T(8,128)(2,1)} %convolution_convert_fusion.2.do_ref, bf16[6,128,512]{2,1,0:T(8,128)(2,1)} %bitcast.38, ...), custom_call_target="tpu_custom_call" | custom-call | flops 805306368 | bytes 4194304 | tf_op jit(solution)/shard_map/pallas_call | solution.py:208
  69.5 1.3 fusion.15
  71.3 1.0 fusion
  72.3 1.0 fusion.9
  73.3 1.8 %pad_maximum_fusion = bf16[128,10,512]{2,1,0:T(8,128)(2,1)} fusion(bf16[128,2,512]{2,1,0:T(2,128)(2,1)S(1)} %reshape.106, bf16[128,8,512]{2,1,0:T(8,128)(2,1)S(1)} %fusion.9), kind=kLoop, calls=%fused_computation.7 | loop fusion | flops 2621440 | bytes 2621440 | tf_op jit(solution)/shard_map/concatenate | solution.py:301
  75.1 9.1 %all-to-all-start.1 = ((bf16[128,10,512]{2,1,0:T(8,128)(2,1)}), bf16[128,10,512]{2,1,0:T(8,128)(2,1)S(1)}, u32[]{:S(2)}, u32[]{:S(2)}) async-start(bf16[128,10,512]{2,1,0:T(8,128)(2,1)} %pad_maximum_fusion), calls=%async_computation.1 | async-start | bytes 4194304 | tf_op jit(solution)/shard_map/all_to_all | solution.py:304
  85.2 14.7 %shard_map.149 = (bf16[256,256]{1,0:T(8,128)(2,1)}, f32[6,128,512]{2,1,0:T(8,128)}) custom-call(s32[8]{0:T(128)} %reshape.99.pos_ref, s32[2]{0:T(128)} %cnt_ref.5, f32[4]{0:T(128)} %bias_ref.3, bf16[256,256]{1,0:T(8,128)(2,1)} %q_ref.5, bf16[256,256]{1,0:T(8,128)(2,1)} %convolution_convert_fusion.2.do_ref, bf16[6,128,512]{2,1,0:T(8,128)(2,1)} %bitcast.39, ...), custom_call_target="tpu_custom_call" | custom-call | flops 1610612736 | bytes 4194304 | tf_op jit(solution)/shard_map/pallas_call | solution.py:208
  99.9 1.5 %convert.17 = bf16[6,128,512]{2,1,0:T(8,128)(2,1)S(1)} convert(f32[6,128,512]{2,1,0:T(8,128)} %get-tuple-element.55) | non-fusion elementwise | flops 393216 | bytes 2359296 | tf_op jit(solution)/shard_map/convert.8
  102.3 7.0 %collective-permute-start.4 = (bf16[256,512]{1,0:T(8,128)(2,1)}, bf16[256,512]{1,0:T(8,128)(2,1)}, u32[]{:S(2)}, u32[]{:S(2)}) collective-permute-start(bf16[256,512]{1,0:T(8,128)(2,1)} %bitcast.7), channel_id=1, source_target_pairs={{2,0},{4,2},{6,4},{8,6},{10,8},{12,10},{14,12},{16,14},{18,16},{20... | collective-permute-start | bytes 786440 | tf_op jit(solution)/shard_map/ppermute | solution.py:32
  109.2 1.9 %collective-permute-start.3 = (bf16[256,512]{1,0:T(8,128)(2,1)}, bf16[256,512]{1,0:T(8,128)(2,1)}, u32[]{:S(2)}, u32[]{:S(2)}) collective-permute-start(bf16[256,512]{1,0:T(8,128)(2,1)} %bitcast.6), channel_id=1, source_target_pairs={{0,2},{2,4},{4,6},{6,8},{8,10},{10,12},{12,14},{14,16},{16,18},{18... | collective-permute-start | bytes 786440 | tf_op jit(solution)/shard_map/ppermute | solution.py:32
  111.2 1.1 slice.55
  112.3 1.6 %add_convert_fusion.1 = bf16[256,256]{1,0:T(8,128)(2,1)} fusion(f32[256,256]{1,0:T(8,128)} %collective-permute-done.2, f32[256,512]{1,0:T(8,128)S(1)} %fusion.24, s32[]{:T(128)S(6)} %select_n.6), kind=kLoop, calls=%fused_computation.34 | loop fusion | flops 131072 | bytes 655364 | tf_op jit(solution)/shard_map/convert_element_type | solution.py:320
  113.9 19.7 %collective-permute-done.4 = bf16[256,512]{1,0:T(8,128)(2,1)} collective-permute-done((bf16[256,512]{1,0:T(8,128)(2,1)}, bf16[256,512]{1,0:T(8,128)(2,1)}, u32[]{:S(2)}, u32[]{:S(2)}) %collective-permute-start.4) | collective-permute-done | bytes 262176 | tf_op jit(solution)/shard_map/ppermute | solution.py:32
  133.7 5.5 %collective-permute-done.3 = bf16[256,512]{1,0:T(8,128)(2,1)} collective-permute-done((bf16[256,512]{1,0:T(8,128)(2,1)}, bf16[256,512]{1,0:T(8,128)(2,1)}, u32[]{:S(2)}, u32[]{:S(2)}) %collective-permute-start.3) | collective-permute-done | bytes 262176 | tf_op jit(solution)/shard_map/ppermute | solution.py:32
  139.2 2.7 %fusion.20 = bf16[256,512]{1,0:T(8,128)(2,1)S(1)} fusion(f32[2,128,512]{2,1,0:T(8,128)S(1)} %slice.55, bf16[256,512]{1,0:T(8,128)(2,1)} %collective-permute-done.4, bf16[256,512]{1,0:T(8,128)(2,1)} %collective-permute-done.3, bf16[128,10,512]{2,1,0:T(8,128)(2,1)S(1)} %all-to-all-done.1, s32[128,10]{0,1:T(8,128)S(1)} %pad.10), kind=kOutput, calls=%fused_computation.31 | convolution fusion | flops 336658432 | bytes 2626560 | tf_op jit(solution)/shard_map/dot_general | solution.py:310
  (37 shorter events, 9.2 us)
Async XLA Ops:
  0.6 31.7 %copy-start = (bf16[256,512]{1,0:T(8,128)(2,1)S(1)}, bf16[256,512]{1,0:T(8,128)(2,1)}, u32[]{:S(2)}) copy-start(bf16[256,512]{1,0:T(8,128)(2,1)} %param.21) | copy-start | bytes 786436
  0.6 29.1 %copy-start.6 = (s32[2,4]{1,0:T(2,128)S(1)}, s32[2,4]{1,0:T(2,128)}, u32[]{:S(2)}) copy-start(s32[2,4]{1,0:T(2,128)} %param.24) | copy-start | bytes 100
  0.7 29.1 %copy-start.3 = (bf16[256,256]{1,0:T(8,128)(2,1)S(1)}, bf16[256,256]{1,0:T(8,128)(2,1)}, u32[]{:S(2)}) copy-start(bf16[256,256]{1,0:T(8,128)(2,1)} %param.22) | copy-start | bytes 393220
  1.6 30.7 %copy-start.5 = (s32[256,3]{0,1:T(4,128)S(1)}, s32[256,3]{0,1:T(4,128)}, u32[]{:S(2)}) copy-start(s32[256,3]{0,1:T(4,128)} %param.27) | copy-start | bytes 9220
  4.9 56.2 %all-to-all-start = ((bf16[128,8,512]{2,1,0:T(8,128)(2,1)}), bf16[128,8,512]{2,1,0:T(8,128)(2,1)S(1)}, u32[]{:S(2)}, u32[]{:S(2)}) async-start(bf16[128,8,512]{2,1,0:T(8,128)(2,1)} %fusion.8), calls=%async_computation | async-start | bytes 2097152 | tf_op jit(solution)/shard_map/all_to_all | solution.py:254
  20.8 27.1 %collective-permute-start.1 = (bf16[256,512]{1,0:T(8,128)(2,1)S(1)}, bf16[256,512]{1,0:T(8,128)(2,1)S(1)}, u32[]{:S(2)}, u32[]{:S(2)}) collective-permute-start(bf16[256,512]{1,0:T(8,128)(2,1)S(1)} %constant_dynamic-update-slice_fusion), channel_id=1, source_target_pairs={{2,0},{4,2},{6,4},{8,6},{10,8},{12,10},{14,12},{16,14},{18,16},{20... | collective-permute-start | bytes 786440 | tf_op jit(solution)/shard_map/ppermute | solution.py:24
  27.8 25.6 %collective-permute-start = (bf16[256,512]{1,0:T(8,128)(2,1)S(1)}, bf16[256,512]{1,0:T(8,128)(2,1)S(1)}, u32[]{:S(2)}, u32[]{:S(2)}) collective-permute-start(bf16[256,512]{1,0:T(8,128)(2,1)S(1)} %constant_dynamic-update-slice_fusion), channel_id=1, source_target_pairs={{0,2},{2,4},{4,6},{6,8},{8,10},{10,12},{12,14},{14,16},{16,18},{18... | collective-permute-start | bytes 786440 | tf_op jit(solution)/shard_map/ppermute | solution.py:23
  69.5 1.6 %copy-start.1 = (f32[3,256,512]{2,1,0:T(8,128)S(1)}, f32[3,256,512]{2,1,0:T(8,128)}, u32[]{:S(2)}) copy-start(f32[3,256,512]{2,1,0:T(8,128)} %get-tuple-element.56) | copy-start | bytes 4718596
  75.1 9.2 %copy-start.2 = (bf16[256,256]{1,0:T(8,128)(2,1)S(1)}, bf16[256,256]{1,0:T(8,128)(2,1)}, u32[]{:S(2)}) copy-start(bf16[256,256]{1,0:T(8,128)(2,1)} %get-tuple-element.53) | copy-start | bytes 393220
  75.1 64.1 %all-to-all-start.1 = ((bf16[128,10,512]{2,1,0:T(8,128)(2,1)}), bf16[128,10,512]{2,1,0:T(8,128)(2,1)S(1)}, u32[]{:S(2)}, u32[]{:S(2)}) async-start(bf16[128,10,512]{2,1,0:T(8,128)(2,1)} %pad_maximum_fusion), calls=%async_computation.1 | async-start | bytes 4194304 | tf_op jit(solution)/shard_map/all_to_all | solution.py:304
  85.2 27.0 %collective-permute-start.2 = (f32[256,256]{1,0:T(8,128)}, f32[256,256]{1,0:T(8,128)}, u32[]{:S(2)}, u32[]{:S(2)}) collective-permute-start(f32[256,256]{1,0:T(8,128)} %constant_dynamic-slice_fusion), channel_id=1, source_target_pairs={{0,1},{1,0},{2,3},{3,2},{4,5},{5,4},{6,7},{7,6},{8,9},{9,8},{10,11... | collective-permute-start | bytes 786440 | tf_op jit(solution)/shard_map/ppermute | solution.py:319
  99.9 11.3 %copy-start.4 = (s32[1,128,8]{1,2,0:T(8,128)S(1)}, s32[1,128,8]{1,2,0:T(8,128)}, u32[]{:S(2)}) copy-start(s32[1,128,8]{1,2,0:T(8,128)} %param.26) | copy-start | bytes 12292
  102.3 31.4 %collective-permute-start.4 = (bf16[256,512]{1,0:T(8,128)(2,1)}, bf16[256,512]{1,0:T(8,128)(2,1)}, u32[]{:S(2)}, u32[]{:S(2)}) collective-permute-start(bf16[256,512]{1,0:T(8,128)(2,1)} %bitcast.7), channel_id=1, source_target_pairs={{2,0},{4,2},{6,4},{8,6},{10,8},{12,10},{14,12},{16,14},{18,16},{20... | collective-permute-start | bytes 786440 | tf_op jit(solution)/shard_map/ppermute | solution.py:32
  109.2 29.9 %collective-permute-start.3 = (bf16[256,512]{1,0:T(8,128)(2,1)}, bf16[256,512]{1,0:T(8,128)(2,1)}, u32[]{:S(2)}, u32[]{:S(2)}) collective-permute-start(bf16[256,512]{1,0:T(8,128)(2,1)} %bitcast.6), channel_id=1, source_target_pairs={{0,2},{2,4},{4,6},{6,8},{8,10},{10,12},{12,14},{14,16},{16,18},{18... | collective-permute-start | bytes 786440 | tf_op jit(solution)/shard_map/ppermute | solution.py:32

commit v12 on v9

--- a/solution.py
+++ b/solution.py
@@ -55,18 +55,21 @@
         count = cnt_ref[t]
         pos = [pos_ref[t * kt + j] for j in range(kt)]
 
+        q = q_ref[rows, :]
+        do = do_ref[rows, :]
+        qf = q.astype(f32)
+        dof = do.astype(f32)
+        fk = [far_ref[e, rows, :cols].astype(f32) for e in range(DEG)]
+        fv = [far_ref[e, rows, cols:].astype(f32) for e in range(DEG)]
+        pk = [qf * fk[e] for e in range(DEG)]
+        pv = [dof * fv[e] for e in range(DEG)]
+
         def head_body(h, carry):
             mask = (lane >= h * hs) & (lane < (h + 1) * hs)
-            q = q_ref[rows, :]
-            do = do_ref[rows, :]
-            qf = q.astype(f32)
-            dof = do.astype(f32)
             qh = jnp.where(mask, q, jnp.zeros_like(q))
             doh = jnp.where(mask, do, jnp.zeros_like(do))
-            fk = [far_ref[e, rows, :cols].astype(f32) for e in range(DEG)]
-            fv = [far_ref[e, rows, cols:].astype(f32) for e in range(DEG)]
             bias = bias_ref[h]
-            fs = [jnp.sum(jnp.where(mask, qf * fk[e], 0.0), axis=1, keepdims=True) * scale + bias
+            fs = [jnp.sum(jnp.where(mask, pk[e], 0.0), axis=1, keepdims=True) * scale + bias
                   for e in range(DEG)]
             if near_out:
                 keys = [ext_ref[pos[j], :, :cols] for j in range(kt)]
@@ -105,7 +108,7 @@
             if not near_out:
                 acc[rows, :] += jnp.where(mask, attn, 0.0)
                 for e in range(DEG):
-                    fdp = jnp.sum(jnp.where(mask, dof * fv[e], 0.0), axis=1, keepdims=True)
+                    fdp = jnp.sum(jnp.where(mask, pv[e], 0.0), axis=1, keepdims=True)
                     fpr = fe[e] / row_sum
                     fds = (fpr * (fdp - delta)).astype(bf16).astype(f32)
                     fg_ref[e, rows, :cols] += jnp.where(mask, fds * qf * scale, 0.0)
@@ -123,7 +126,7 @@
                 eg_ref[pos[j], :, :cols] += kg
                 eg_ref[pos[j], :, cols:] += vg
             for e in range(DEG):
-                fdp = jnp.sum(jnp.where(mask, dof * fv[e], 0.0), axis=1, keepdims=True)
+                fdp = jnp.sum(jnp.where(mask, pv[e], 0.0), axis=1, keepdims=True)
                 fpr = fe[e] / row_sum
                 fds = (fpr * (fdp - delta)).astype(bf16).astype(f32)
                 qg = qg + fds * fk[e]

time: 142 us -> 142 us (level)
  no operation moved by 1% of the time
where the time goes in v12:
time: 142 us; the launch traced here: 141 us
  waiting for transfers between devices  44.3 us (31%)
  starting transfers between devices  42.9 us (30%)
  Pallas kernels  28 us (20%)
  matrix products  9.27 us (7%)
  local copies, waits for them, and re-layouts  7.7 us (5%)
  other arithmetic  6.37 us (4%)
  blocking collectives  1.99 us (1%)
    pallas_call x2, Pallas kernels, attention_tiles(): pl.pallas_call(functools.partial(_attn_kernel, heads, kt, near_out), out_...  21.3 us
    all_to_all x1, waiting for transfers between devices, shards(): lax.all_to_all(both, 'dom', split_axis=0, concat_axis=0, tiled=True)  20.3 us
    all_to_all x1, starting transfers between devices, shards(): lax.all_to_all(outgoing, 'dom', split_axis=0, concat_axis=0, tiled=True)  15.9 us
    ppermute x1, waiting for transfers between devices, extended_2(): after = lax.ppermute(leading, axis, down)  14.6 us
    all_to_all x1, starting transfers between devices, shards(): lax.all_to_all(both, 'dom', split_axis=0, concat_axis=0, tiled=True)  9.13 us
    ppermute x2, starting transfers between devices, from_behind(): lax.ppermute(value, axis, [(source, source + steps) for source in range(l...  8.91 us
    ppermute x1, starting transfers between devices, extended_2(): after = lax.ppermute(leading, axis, down)  6.98 us
    pallas_call x1, Pallas kernels, near_tiles(): pl.pallas_call(functools.partial(_near_kernel, heads, kt), out_shape=(jax...  6.7 us
  transfers between devices with their start and end apart: 7, of which 4 were waited for; matrix products, arithmetic and copies ran while one was open for 7% of the time, Pallas kernels for 15%

profile of v12, /device:TPU:6, one launch (start us, length us, event | category | flops | bytes accessed | tf_op | source)
XLA Modules:
  0.0 141.3 jit_solution(13347165780515357648)
XLA Ops:
  3.4 1.5 %fusion.8 = bf16[128,8,512]{2,1,0:T(8,128)(2,1)} fusion(bf16[256,512]{1,0:T(8,128)(2,1)S(1)} %constant_dynamic-update-slice_fusion, s32[1024]{0:T(1024)S(1)} %eq.60), kind=kOutput, calls=%fused_computation.15 | convolution fusion | flops 269221888 | bytes 1314816 | tf_op jit(solution)/shard_map/dot_general | solution.py:253
  4.9 15.9 %all-to-all-start = ((bf16[128,8,512]{2,1,0:T(8,128)(2,1)}), bf16[128,8,512]{2,1,0:T(8,128)(2,1)S(1)}, u32[]{:S(2)}, u32[]{:S(2)}) async-start(bf16[128,8,512]{2,1,0:T(8,128)(2,1)} %fusion.8), calls=%async_computation | async-start | bytes 2097152 | tf_op jit(solution)/shard_map/all_to_all | solution.py:257
  20.8 7.0 %collective-permute-start.1 = (bf16[256,512]{1,0:T(8,128)(2,1)S(1)}, bf16[256,512]{1,0:T(8,128)(2,1)S(1)}, u32[]{:S(2)}, u32[]{:S(2)}) collective-permute-start(bf16[256,512]{1,0:T(8,128)(2,1)S(1)} %constant_dynamic-update-slice_fusion), channel_id=1, source_target_pairs={{2,0},{4,2},{6,4},{8,6},{10,8},{12,10},{14,12},{16,14},{18,16},{20... | collective-permute-start | bytes 786440 | tf_op jit(solution)/shard_map/ppermute | solution.py:24
  27.8 1.9 %collective-permute-start = (bf16[256,512]{1,0:T(8,128)(2,1)S(1)}, bf16[256,512]{1,0:T(8,128)(2,1)S(1)}, u32[]{:S(2)}, u32[]{:S(2)}) collective-permute-start(bf16[256,512]{1,0:T(8,128)(2,1)S(1)} %constant_dynamic-update-slice_fusion), channel_id=1, source_target_pairs={{0,2},{2,4},{4,6},{6,8},{8,10},{10,12},{12,14},{14,16},{16,18},{18... | collective-permute-start | bytes 786440 | tf_op jit(solution)/shard_map/ppermute | solution.py:23
  29.8 2.0 %all_gather.3 = bf16[256,512]{1,0:T(8,128)(2,1)S(1)} all-gather(bf16[256,256]{1,0:T(8,128)(2,1)S(1)} %copy-done.3), channel_id=1, replica_groups=mesh['dom'=128,'head'=2] {'head'}, dimensions={1}, use_global_device_ids=true | all-gather | bytes 393216 | tf_op jit(solution)/shard_map/all_gather | solution.py:241
  33.3 14.6 %collective-permute-done.1 = bf16[256,512]{1,0:T(8,128)(2,1)S(1)} collective-permute-done((bf16[256,512]{1,0:T(8,128)(2,1)S(1)}, bf16[256,512]{1,0:T(8,128)(2,1)S(1)}, u32[]{:S(2)}, u32[]{:S(2)}) %collective-permute-start.1) | collective-permute-done | bytes 262176 | tf_op jit(solution)/shard_map/ppermute | solution.py:24
  47.9 5.5 %collective-permute-done = bf16[256,512]{1,0:T(8,128)(2,1)S(1)} collective-permute-done((bf16[256,512]{1,0:T(8,128)(2,1)S(1)}, bf16[256,512]{1,0:T(8,128)(2,1)S(1)}, u32[]{:S(2)}, u32[]{:S(2)}) %collective-permute-start) | collective-permute-done | bytes 262176 | tf_op jit(solution)/shard_map/ppermute | solution.py:23
  54.4 6.7 %shard_map.147 = (f32[256,256]{1,0:T(8,128)}, f32[2,256,128]{2,1,0:T(8,128)}) custom-call(s32[8]{0:T(128)} %reshape.102.pos_ref, s32[2]{0:T(128)} %cnt_ref.5, bf16[256,256]{1,0:T(8,128)(2,1)} %q_ref.5, bf16[6,128,512]{2,1,0:T(8,128)(2,1)} %bitcast.39), custom_call_target="tpu_custom_call" | custom-call | flops 536870912 | bytes 2097152 | tf_op jit(solution)/shard_map/pallas_call | solution.py:188
  61.1 1.9 %fusion.7 = bf16[768,512]{1,0:T(8,128)(2,1)} fusion(s32[768]{0:T(1024)S(1)} %eq.56, bf16[128,8,512]{2,1,0:T(8,128)(2,1)S(1)} %all-to-all-done), kind=kOutput, calls=%fused_computation.14 | convolution fusion | flops 806486016 | bytes 1838080 | tf_op jit(solution)/shard_map/dot_general | solution.py:264
  63.0 6.4 %shard_map.148 = (bf16[256,256]{1,0:T(8,128)(2,1)}, f32[3,256,512]{2,1,0:T(8,128)}) custom-call(s32[8]{0:T(128)} %reshape.102.pos_ref, s32[2]{0:T(128)} %cnt_ref.5, f32[4]{0:T(128)} %bias_ref.3, bf16[256,256]{1,0:T(8,128)(2,1)} %q_ref.5, bf16[256,256]{1,0:T(8,128)(2,1)} %convolution_convert_fusion.2.do_ref, bf16[6,128,512]{2,1,0:T(8,128)(2,1)} %bitcast.40, ...), custom_call_target="tpu_custom_call" | custom-call | flops 805306368 | bytes 4194304 | tf_op jit(solution)/shard_map/pallas_call | solution.py:211
  69.4 1.3 fusion.10
  71.2 1.0 fusion
  72.2 1.0 fusion.9
  73.2 1.8 %pad_maximum_fusion = bf16[128,10,512]{2,1,0:T(8,128)(2,1)} fusion(bf16[128,2,512]{2,1,0:T(2,128)(2,1)S(1)} %reshape.109, bf16[128,8,512]{2,1,0:T(8,128)(2,1)S(1)} %fusion.9), kind=kLoop, calls=%fused_computation.7 | loop fusion | flops 2621440 | bytes 2621440 | tf_op jit(solution)/shard_map/concatenate | solution.py:304
  75.0 9.1 %all-to-all-start.1 = ((bf16[128,10,512]{2,1,0:T(8,128)(2,1)}), bf16[128,10,512]{2,1,0:T(8,128)(2,1)S(1)}, u32[]{:S(2)}, u32[]{:S(2)}) async-start(bf16[128,10,512]{2,1,0:T(8,128)(2,1)} %pad_maximum_fusion), calls=%async_computation.1 | async-start | bytes 4194304 | tf_op jit(solution)/shard_map/all_to_all | solution.py:307
  85.2 14.9 %shard_map.149 = (bf16[256,256]{1,0:T(8,128)(2,1)}, f32[6,128,512]{2,1,0:T(8,128)}) custom-call(s32[8]{0:T(128)} %reshape.102.pos_ref, s32[2]{0:T(128)} %cnt_ref.5, f32[4]{0:T(128)} %bias_ref.3, bf16[256,256]{1,0:T(8,128)(2,1)} %q_ref.5, bf16[256,256]{1,0:T(8,128)(2,1)} %convolution_convert_fusion.2.do_ref, bf16[6,128,512]{2,1,0:T(8,128)(2,1)} %bitcast.41, ...), custom_call_target="tpu_custom_call" | custom-call | flops 1610612736 | bytes 4194304 | tf_op jit(solution)/shard_map/pallas_call | solution.py:211
  100.1 1.1 slice.58
  101.1 1.5 %convert.17 = bf16[6,128,512]{2,1,0:T(8,128)(2,1)S(1)} convert(f32[6,128,512]{2,1,0:T(8,128)} %get-tuple-element.55) | non-fusion elementwise | flops 393216 | bytes 2359296 | tf_op jit(solution)/shard_map/convert.8
  103.5 7.0 %collective-permute-start.4 = (bf16[256,512]{1,0:T(8,128)(2,1)}, bf16[256,512]{1,0:T(8,128)(2,1)}, u32[]{:S(2)}, u32[]{:S(2)}) collective-permute-start(bf16[256,512]{1,0:T(8,128)(2,1)} %bitcast.7), channel_id=1, source_target_pairs={{2,0},{4,2},{6,4},{8,6},{10,8},{12,10},{14,12},{16,14},{18,16},{20... | collective-permute-start | bytes 786440 | tf_op jit(solution)/shard_map/ppermute | solution.py:32
  110.5 1.9 %collective-permute-start.3 = (bf16[256,512]{1,0:T(8,128)(2,1)}, bf16[256,512]{1,0:T(8,128)(2,1)}, u32[]{:S(2)}, u32[]{:S(2)}) collective-permute-start(bf16[256,512]{1,0:T(8,128)(2,1)} %bitcast.6), channel_id=1, source_target_pairs={{0,2},{2,4},{4,6},{6,8},{8,10},{10,12},{12,14},{14,16},{16,18},{18... | collective-permute-start | bytes 786440 | tf_op jit(solution)/shard_map/ppermute | solution.py:32
  112.4 1.6 %add_convert_fusion.1 = bf16[256,256]{1,0:T(8,128)(2,1)} fusion(f32[256,256]{1,0:T(8,128)} %collective-permute-done.2, f32[256,512]{1,0:T(8,128)S(1)} %fusion.20, s32[]{:T(128)S(6)} %select_n.6), kind=kLoop, calls=%fused_computation.33 | loop fusion | flops 131072 | bytes 655364 | tf_op jit(solution)/shard_map/convert_element_type | solution.py:321
  114.1 20.3 %all-to-all-done.1 = bf16[128,10,512]{2,1,0:T(8,128)(2,1)S(1)} async-done(((bf16[128,10,512]{2,1,0:T(8,128)(2,1)}), bf16[128,10,512]{2,1,0:T(8,128)(2,1)S(1)}, u32[]{:S(2)}, u32[]{:S(2)}) %all-to-all-start.1) | async-done | bytes 1310752 | tf_op jit(solution)/shard_map/all_to_all | solution.py:307
  135.3 3.8 %collective-permute-done.3 = bf16[256,512]{1,0:T(8,128)(2,1)} collective-permute-done((bf16[256,512]{1,0:T(8,128)(2,1)}, bf16[256,512]{1,0:T(8,128)(2,1)}, u32[]{:S(2)}, u32[]{:S(2)}) %collective-permute-start.3) | collective-permute-done | bytes 262176 | tf_op jit(solution)/shard_map/ppermute | solution.py:32
  139.1 1.5 %fusion.15 = bf16[256,512]{1,0:T(8,128)(2,1)S(1)} fusion(f32[2,128,512]{2,1,0:T(8,128)S(1)} %slice.58, bf16[256,512]{1,0:T(8,128)(2,1)} %collective-permute-done.4, bf16[256,512]{1,0:T(8,128)(2,1)} %collective-permute-done.3, bf16[128,10,512]{2,1,0:T(8,128)(2,1)S(1)} %all-to-all-done.1, s32[1024]{0:T(1024)S(1)} %eq.60), kind=kOutput, calls=%fused_computation.29 | convolution fusion | flops 269484032 | bytes 2363392 | tf_op jit(solution)/shard_map/dot_general | solution.py:313
  (34 shorter events, 9.2 us)
Async XLA Ops:
  0.6 31.8 %copy-start = (bf16[256,512]{1,0:T(8,128)(2,1)S(1)}, bf16[256,512]{1,0:T(8,128)(2,1)}, u32[]{:S(2)}) copy-start(bf16[256,512]{1,0:T(8,128)(2,1)} %param.21) | copy-start | bytes 786436
  0.6 29.1 %copy-start.5 = (s32[2,4]{1,0:T(2,128)S(1)}, s32[2,4]{1,0:T(2,128)}, u32[]{:S(2)}) copy-start(s32[2,4]{1,0:T(2,128)} %param.24) | copy-start | bytes 100
  0.7 29.1 %copy-start.3 = (bf16[256,256]{1,0:T(8,128)(2,1)S(1)}, bf16[256,256]{1,0:T(8,128)(2,1)}, u32[]{:S(2)}) copy-start(bf16[256,256]{1,0:T(8,128)(2,1)} %param.22) | copy-start | bytes 393220
  2.5 29.9 %copy-start.4 = (s32[256,3]{0,1:T(4,128)S(1)}, s32[256,3]{0,1:T(4,128)}, u32[]{:S(2)}) copy-start(s32[256,3]{0,1:T(4,128)} %param.27) | copy-start | bytes 9220
  4.9 56.2 %all-to-all-start = ((bf16[128,8,512]{2,1,0:T(8,128)(2,1)}), bf16[128,8,512]{2,1,0:T(8,128)(2,1)S(1)}, u32[]{:S(2)}, u32[]{:S(2)}) async-start(bf16[128,8,512]{2,1,0:T(8,128)(2,1)} %fusion.8), calls=%async_computation | async-start | bytes 2097152 | tf_op jit(solution)/shard_map/all_to_all | solution.py:257
  20.8 27.1 %collective-permute-start.1 = (bf16[256,512]{1,0:T(8,128)(2,1)S(1)}, bf16[256,512]{1,0:T(8,128)(2,1)S(1)}, u32[]{:S(2)}, u32[]{:S(2)}) collective-permute-start(bf16[256,512]{1,0:T(8,128)(2,1)S(1)} %constant_dynamic-update-slice_fusion), channel_id=1, source_target_pairs={{2,0},{4,2},{6,4},{8,6},{10,8},{12,10},{14,12},{16,14},{18,16},{20... | collective-permute-start | bytes 786440 | tf_op jit(solution)/shard_map/ppermute | solution.py:24
  27.8 25.6 %collective-permute-start = (bf16[256,512]{1,0:T(8,128)(2,1)S(1)}, bf16[256,512]{1,0:T(8,128)(2,1)S(1)}, u32[]{:S(2)}, u32[]{:S(2)}) collective-permute-start(bf16[256,512]{1,0:T(8,128)(2,1)S(1)} %constant_dynamic-update-slice_fusion), channel_id=1, source_target_pairs={{0,2},{2,4},{4,6},{6,8},{8,10},{10,12},{12,14},{14,16},{16,18},{18... | collective-permute-start | bytes 786440 | tf_op jit(solution)/shard_map/ppermute | solution.py:23
  69.4 1.6 %copy-start.1 = (f32[3,256,512]{2,1,0:T(8,128)S(1)}, f32[3,256,512]{2,1,0:T(8,128)}, u32[]{:S(2)}) copy-start(f32[3,256,512]{2,1,0:T(8,128)} %get-tuple-element.56) | copy-start | bytes 4718596
  75.0 9.1 %copy-start.2 = (bf16[256,256]{1,0:T(8,128)(2,1)S(1)}, bf16[256,256]{1,0:T(8,128)(2,1)}, u32[]{:S(2)}) copy-start(bf16[256,256]{1,0:T(8,128)(2,1)} %get-tuple-element.53) | copy-start | bytes 393220
  75.0 59.4 %all-to-all-start.1 = ((bf16[128,10,512]{2,1,0:T(8,128)(2,1)}), bf16[128,10,512]{2,1,0:T(8,128)(2,1)S(1)}, u32[]{:S(2)}, u32[]{:S(2)}) async-start(bf16[128,10,512]{2,1,0:T(8,128)(2,1)} %pad_maximum_fusion), calls=%async_computation.1 | async-start | bytes 4194304 | tf_op jit(solution)/shard_map/all_to_all | solution.py:307
  85.2 27.3 %collective-permute-start.2 = (f32[256,256]{1,0:T(8,128)}, f32[256,256]{1,0:T(8,128)}, u32[]{:S(2)}, u32[]{:S(2)}) collective-permute-start(f32[256,256]{1,0:T(8,128)} %constant_dynamic-slice_fusion), channel_id=1, source_target_pairs={{0,1},{1,0},{2,3},{3,2},{4,5},{5,4},{6,7},{7,6},{8,9},{9,8},{10,11... | collective-permute-start | bytes 786440 | tf_op jit(solution)/shard_map/ppermute | solution.py:320
  103.5 31.8 %collective-permute-start.4 = (bf16[256,512]{1,0:T(8,128)(2,1)}, bf16[256,512]{1,0:T(8,128)(2,1)}, u32[]{:S(2)}, u32[]{:S(2)}) collective-permute-start(bf16[256,512]{1,0:T(8,128)(2,1)} %bitcast.7), channel_id=1, source_target_pairs={{2,0},{4,2},{6,4},{8,6},{10,8},{12,10},{14,12},{16,14},{18,16},{20... | collective-permute-start | bytes 786440 | tf_op jit(solution)/shard_map/ppermute | solution.py:32
  110.5 28.6 %collective-permute-start.3 = (bf16[256,512]{1,0:T(8,128)(2,1)}, bf16[256,512]{1,0:T(8,128)(2,1)}, u32[]{:S(2)}, u32[]{:S(2)}) collective-permute-start(bf16[256,512]{1,0:T(8,128)(2,1)} %bitcast.6), channel_id=1, source_target_pairs={{0,2},{2,4},{4,6},{6,8},{8,10},{10,12},{12,14},{14,16},{16,18},{18... | collective-permute-start | bytes 786440 | tf_op jit(solution)/shard_map/ppermute | solution.py:32
